TPU v7x, 256 devices: a whole 4x4x8 slice. The times are simulated.
256 devices in a mesh: space: 64 (over x, z, core), tm: 4 (over y).
Axes of the slice: x: 4, y: 4, z: 8, core: 2. Of those that a mesh axis runs over, the one named last changes fastest.
Arguments:
- snapshots: float32 [4608, 65536], P('tm', 'space'), as said below
- block_starts: int32 [32], P('tm'), may hold values from 0 to 4352, as said below
- owner: int32 [9], replicated, may hold values from 0 to 3, as said below
Outputs:
- modes: float32 [20, 32, 2, 65536], P('tm', None, None, 'space')
Inputs may be any that keep to these rules, and one draw needn't show every extreme that they name: `block_starts`: block k lies inside the snapshots held by index k // 8 of tm: its start is that range's first snapshot plus an even offset of 0 to 896; within one range the starts rise with k by 112 or more, the range's first block starts at offset 0 and its last at 896. `owner`: one index of tm owns exactly 5 frequencies, every other index owns one or more and fewer than 5. `snapshots`: finite real values.
All inputs are finite; a program needn't handle non-finite values.
Results may differ from a plain program's by a relative error of at most 0.0003.
Values sent between devices are 32-bit elements; how exact they have to be, the bound alone decides.
No kernel may reach another device: no remote copies, remote signals or barrier semaphores. Data moves between devices by JAX's collectives and lax.ppermute only.
A program may use at most 64 MiB of HBM per device.

v0:
```python
import jax
import jax.numpy as jnp
from jax import lax
from jax.sharding import PartitionSpec as P

NFFT = 256
NF = 9
FCAP = 5


def dft_table():
    times = jnp.arange(NFFT, dtype=jnp.int32)
    freqs = jnp.arange(NF, dtype=jnp.int32)
    phase = freqs[:, None] * times[None, :] % NFFT
    angle = 2.0 * jnp.pi / NFFT * phase.astype(jnp.float32)
    window = 0.5 - 0.5 * jnp.cos(2.0 * jnp.pi / NFFT * times.astype(jnp.float32))
    return jnp.stack([window * jnp.cos(angle), -window * jnp.sin(angle)], axis=1)


def slot_selector(owner, slot_count):
    freq_ids = jnp.arange(owner.shape[0], dtype=jnp.int32)
    before = (owner[None, :] == owner[:, None]) & (freq_ids[None, :] < freq_ids[:, None])
    rank_in = jnp.sum(before.astype(jnp.int32), axis=1)
    slot_of = owner * FCAP + rank_in
    targets = jnp.arange(slot_count, dtype=jnp.int32)
    return (slot_of[None, :] == targets[:, None]).astype(jnp.float32)


def partial_gram(matrices):
    return jnp.einsum("kip,kjp->kij", matrices, matrices, precision=lax.Precision.HIGHEST)


def finish_pass(matrices, totals, rows_total):
    gram = totals / rows_total
    identity = jnp.eye(gram.shape[-1], dtype=jnp.float32)
    diagonal_sum = jnp.trace(gram, axis1=1, axis2=2)
    gram = gram + jnp.where(diagonal_sum == 0.0, 1.0, 0.0)[:, None, None] * identity
    factor = jnp.linalg.cholesky(gram)
    inverse = jax.scipy.linalg.solve_triangular(
        factor, jnp.broadcast_to(identity, gram.shape), lower=True
    )
    return jnp.einsum("kij,kjp->kip", inverse, matrices, precision=lax.Precision.HIGHEST)


def local(snapshots, block_starts, owner):
    table = dft_table()
    samples, points = snapshots.shape
    block_count = block_starts.shape[0]
    tm_count = lax.axis_size("tm")
    space_count = lax.axis_size("space")
    rows_total = 2.0 * points * space_count
    column_count = block_count * tm_count
    offset = lax.axis_index("tm") * samples
    segments = jnp.stack(
        [
            lax.dynamic_slice_in_dim(snapshots, block_starts[block] - offset, NFFT, 0)
            for block in range(block_count)
        ]
    )
    spectra = jnp.einsum("fct,btp->fbcp", table, segments, precision=lax.Precision.HIGHEST)
    selector = slot_selector(owner, tm_count * FCAP)
    outgoing = jnp.einsum("lf,fbcp->lbcp", selector, spectra, precision=lax.Precision.HIGHEST)
    outgoing = outgoing.reshape(tm_count, FCAP, block_count, 2, points)
    received = lax.all_to_all(outgoing, "tm", split_axis=0, concat_axis=2, tiled=True)
    count = received.shape[1]
    matrices = received[0].reshape(count, column_count, 2 * points)
    for turn in range(2):
        partial_sums = partial_gram(matrices)
        totals = jnp.stack([lax.psum(partial_sums[item], "space") for item in range(count)])
        matrices = finish_pass(matrices, totals, rows_total)
    return matrices.reshape(count, column_count, 2, points)


def solution(mesh):
    placed = (P("tm", "space"), P("tm"), P())
    return jax.shard_map(
        local, mesh=mesh, in_specs=placed, out_specs=P("tm", None, None, "space"), check_vma=False
    )
```

profile of v0, /device:TPU:8, one launch (start us, length us, event | category | flops | bytes accessed | tf_op | source)
XLA Modules:
  0.0 621.2 jit_solution(3651869889522997822)
XLA Ops:
  0.0 1.6 fusion.31
  6.7 0.9 convert_reduce_fusion
  7.6 0.7 multiply_add_fusion.2
  8.3 2.4 bitcast_dynamic-update-slice_fusion.7
  10.7 2.4 bitcast_dynamic-update-slice_fusion.6
  13.1 2.4 bitcast_dynamic-update-slice_fusion.5
  15.5 2.4 bitcast_dynamic-update-slice_fusion.4
  17.9 2.4 bitcast_dynamic-update-slice_fusion.3
  20.2 2.4 bitcast_dynamic-update-slice_fusion.2
  22.7 2.4 bitcast_dynamic-update-slice_fusion.1
  25.1 2.4 bitcast_dynamic-update-slice_fusion
  27.4 0.1 sine_multiply_fusion
  27.5 7.5 %fusion.2 = f32[9,8,2,1024]{3,0,2,1:T(8,128)S(1)} fusion(f32[8,256,1024]{2,1,0:T(8,128)} %bitcast_dynamic-update-slice_fusion, f32[9,1,256]{2,0,1:T(8,128)S(1)} %get-tuple-element.35, f32[9,1,256]{2,0,1:T(8,128)S(1)} %get-tuple-element.36), kind=kOutput, calls=%fused_computation.2 | convolution fusion | flops 452989440 | bytes 8996864 | tf_op jit(solution)/shard_map/fct,btp->fbcp/dot_general | solution.py:60
  35.0 0.9 fusion.23
  35.9 1.8 copy.31
  37.7 5.7 all-to-all-start
  43.5 15.6 %all-to-all-done = f32[4,5,8,2,1024]{4,2,3,1,0:T(8,128)S(1)} async-done(((f32[4,5,8,2,1024]{4,2,3,1,0:T(8,128)}), f32[4,5,8,2,1024]{4,2,3,1,0:T(8,128)S(1)}, u32[]{:S(2)}, u32[]{:S(2)}) %all-to-all-start) | async-done | bytes 1310752 | tf_op jit(solution)/shard_map/all_to_all | solution.py:64
  59.1 0.1 copy.32
  59.2 1.2 fusion.32
  60.5 252.4 %all-reduce.1 = (f32[1,32,32]{1,2,0:T(8,128)S(1)}, f32[1,32,32]{1,2,0:T(8,128)S(1)}, f32[1,32,32]{1,2,0:T(8,128)S(1)}, f32[1,32,32]{1,2,0:T(8,128)S(1)}, f32[1,32,32]{1,2,0:T(8,128)S(1)}) all-reduce(f32[1,32,32]{1,2,0:T(8,128)S(1)} %get-tuple-element.26, ...), channel_id=1, replica_groups=mesh['space'=64,'tm'=4] {'space'}, use_global_device_ids=true, to_apply=%region_1.2 | all-reduce | flops 5120 | bytes 40960 | tf_op jit(solution)/shard_map/psum | solution.py:69
  313.0 0.1 select_reduce_fusion.3
  313.1 0.1 multiply_add_fusion.1
  313.2 0.1 copy.38
  313.3 0.1 fusion.10
  313.3 14.7 %custom-call.8 = f32[5,32,32]{2,1,0:T(8,128)S(1)} custom-call(f32[5,32,32]{2,1,0:T(8,128)S(1)} %fusion.10), custom_call_target="Cholesky" | custom-call | tf_op jit(solution)/shard_map/jit(cholesky)/cholesky | solution.py:38
  328.0 0.1 compare_reduce_fusion.1
  328.2 0.1 select_bitcast_fusion.1
  328.2 12.3 %custom-call.9 = f32[5,1,32,32]{2,3,1,0:T(8,128)S(1)} custom-call(f32[5,1,32,32]{3,2,1,0:T(8,128)S(1)} %select_bitcast_fusion.1), custom_call_target="InvertDiagBlocksLowerTriangular" | custom-call | tf_op jit(solution)/shard_map/jit(_solve_triangular)/vmap()/triangular_solve | solution.py:39
  340.6 0.3 fusion.8
  340.9 1.2 fusion.33
  342.1 1.2 fusion.34
  343.4 246.4 %all-reduce = (f32[1,32,32]{1,2,0:T(8,128)S(1)}, f32[1,32,32]{1,2,0:T(8,128)S(1)}, f32[1,32,32]{1,2,0:T(8,128)S(1)}, f32[1,32,32]{1,2,0:T(8,128)S(1)}, f32[1,32,32]{1,2,0:T(8,128)S(1)}) all-reduce(f32[1,32,32]{1,2,0:T(8,128)S(1)} %get-tuple-element.21, ...), channel_id=1, replica_groups=mesh['space'=64,'tm'=4] {'space'}, use_global_device_ids=true, to_apply=%region_9.12 | all-reduce | flops 5120 | bytes 40960 | tf_op jit(solution)/shard_map/psum | solution.py:69
  589.8 0.1 select_reduce_fusion.2
  589.9 0.1 multiply_add_fusion
  590.0 0.1 copy.46
  590.1 0.1 fusion.7
  590.2 14.7 %custom-call.10 = f32[5,32,32]{2,1,0:T(8,128)S(1)} custom-call(f32[5,32,32]{2,1,0:T(8,128)S(1)} %fusion.7), custom_call_target="Cholesky" | custom-call | tf_op jit(solution)/shard_map/jit(cholesky)/cholesky | solution.py:38
  604.9 0.1 compare_reduce_fusion
  605.0 0.1 select_bitcast_fusion
  605.1 12.3 %custom-call.11 = f32[5,1,32,32]{2,3,1,0:T(8,128)S(1)} custom-call(f32[5,1,32,32]{3,2,1,0:T(8,128)S(1)} %select_bitcast_fusion), custom_call_target="InvertDiagBlocksLowerTriangular" | custom-call | tf_op jit(solution)/shard_map/jit(_solve_triangular)/vmap()/triangular_solve | solution.py:39
  617.4 0.3 fusion.5
  617.7 1.2 fusion.35
  619.0 2.2 reshape.155
  (22 shorter events, 0.2 us)
Async XLA Ops:
  37.7 21.4 %all-to-all-start = ((f32[4,5,8,2,1024]{4,2,3,1,0:T(8,128)}), f32[4,5,8,2,1024]{4,2,3,1,0:T(8,128)S(1)}, u32[]{:S(2)}, u32[]{:S(2)}) async-start(f32[4,5,8,2,1024]{4,2,3,1,0:T(8,128)} %bitcast.22), calls=%async_computation | async-start | bytes 2621440 | tf_op jit(solution)/shard_map/all_to_all | solution.py:64
where the time goes:
time: 622 us; the launch traced here: 621 us
  blocking collectives  499 us (80%)
  other arithmetic  56.8 us (9%)
  local copies, waits for them, and re-layouts  25.1 us (4%)
  waiting for transfers between devices  15.6 us (3%)
  matrix products  14 us (2%)
    psum x2, blocking collectives, local(): lax.psum(partial_sums[item], 'space')  499 us
    another operation x7, other arithmetic, finish_pass(): factor = jnp.linalg.cholesky(gram)  29.6 us
    another operation x5, other arithmetic, finish_pass(): jax.scipy.linalg.solve_triangular(factor, jnp.broadcast_to(identity, gram...  24.8 us
    unnamed x15, local copies, waits for them, and re-layouts  16.8 us
    all_to_all x1, waiting for transfers between devices, local(): lax.all_to_all(outgoing, 'tm', split_axis=0, concat_axis=2, tiled=True)  15.6 us
  transfers between devices with their start and end apart: 1, of which 1 were waited for; matrix products, arithmetic and copies ran while one was open for 0% of the time, Pallas kernels for 0%

commit v1 on v0

--- a/solution.py
+++ b/solution.py
@@ -42,6 +42,18 @@
     return jnp.einsum("kij,kjp->kip", inverse, matrices, precision=lax.Precision.HIGHEST)
 
 
+def reduce_space(values):
+    count = lax.axis_size("space")
+    if count & (count - 1):
+        return lax.psum(values, "space")
+    distance = 1
+    while distance < count:
+        pairs = [(index, index ^ distance) for index in range(count)]
+        values = values + lax.ppermute(values, "space", pairs)
+        distance *= 2
+    return values
+
+
 def local(snapshots, block_starts, owner):
     table = dft_table()
     samples, points = snapshots.shape
@@ -66,7 +78,7 @@
     matrices = received[0].reshape(count, column_count, 2 * points)
     for turn in range(2):
         partial_sums = partial_gram(matrices)
-        totals = jnp.stack([lax.psum(partial_sums[item], "space") for item in range(count)])
+        totals = reduce_space(partial_sums)
         matrices = finish_pass(matrices, totals, rows_total)
     return matrices.reshape(count, column_count, 2, points)
 

time: 622 us -> 188 us (0.30)
  blocking collectives: 499 us -> 21.2 us
  starting transfers between devices: 5.69 us -> 31.3 us
  waiting for transfers between devices: 15.6 us -> 34 us
    psum x2 -> x0, blocking collectives: 499 us -> none  [local(): lax.psum(partial_sums[item], 'space')]
    ppermute x0 -> x12, waiting for transfers between devices: none -> 34 us  [reduce_space(): values = values + lax.ppermute(values, 'space', pairs)]
    ppermute x0 -> x12, starting transfers between devices: none -> 31.3 us  [reduce_space(): values = values + lax.ppermute(values, 'space', pairs)]
    all_to_all x0 -> x1, blocking collectives: none -> 21.2 us  [local(): lax.all_to_all(outgoing, 'tm', split_axis=0, concat_axis=2, tiled=True)]
    all_to_all x1 -> x0, waiting for transfers between devices: 15.6 us -> none  [local(): lax.all_to_all(outgoing, 'tm', split_axis=0, concat_axis=2, tiled=True)]
    unnamed x15 -> x7, local copies, waits for them, and re-layouts: 16.8 us -> 16.8 us
  transfers between devices with their start and end apart: 1 -> 12, of which waited for: 1 -> 12; matrix products, arithmetic and copies ran while one was open for 0% -> 0% of each run, Pallas kernels for 0% -> 0%
where the time goes in v1:
time: 188 us; the launch traced here: 186 us
  other arithmetic  56.8 us (30%)
  waiting for transfers between devices  34 us (18%)
  starting transfers between devices  31.3 us (17%)
  local copies, waits for them, and re-layouts  24 us (13%)
  blocking collectives  21.2 us (11%)
  matrix products  14 us (7%)
  between operations  5.17 us (3%)
    ppermute x12, waiting for transfers between devices, reduce_space(): values = values + lax.ppermute(values, 'space', pairs)  34 us
    ppermute x12, starting transfers between devices, reduce_space(): values = values + lax.ppermute(values, 'space', pairs)  31.3 us
    another operation x7, other arithmetic, finish_pass(): factor = jnp.linalg.cholesky(gram)  29.6 us
    another operation x5, other arithmetic, finish_pass(): jax.scipy.linalg.solve_triangular(factor, jnp.broadcast_to(identity, gram...  24.8 us
    all_to_all x1, blocking collectives, local(): lax.all_to_all(outgoing, 'tm', split_axis=0, concat_axis=2, tiled=True)  21.2 us
    unnamed x7, local copies, waits for them, and re-layouts  16.8 us
    dot_general x1, matrix products, local(): jnp.einsum('fct,btp->fbcp', table, segments, precision=lax.Precision.HIGH...  7.49 us
  transfers between devices with their start and end apart: 12, of which 12 were waited for; matrix products, arithmetic and copies ran while one was open for 0% of the time, Pallas kernels for 0%

profile of v1, /device:TPU:8, one launch (start us, length us, event | category | flops | bytes accessed | tf_op | source)
XLA Modules:
  0.0 186.4 jit_solution(4175154078504866909)
XLA Ops:
  0.0 1.6 fusion.29
  6.7 0.9 convert_reduce_fusion
  7.6 0.7 multiply_add_fusion.2
  8.3 2.4 %bitcast_dynamic-update-slice_fusion.7 = f32[8,256,1024]{2,1,0:T(8,128)} fusion(f32[1152,1024]{1,0:T(8,128)} %param.6, s32[]{:T(128)S(6)} %select_n.70), kind=kLoop, calls=%fused_computation.10 | loop fusion | bytes 2097156
  10.7 2.4 %bitcast_dynamic-update-slice_fusion.6 = f32[8,256,1024]{2,1,0:T(8,128)} fusion(f32[8,256,1024]{2,1,0:T(8,128)} %bitcast_dynamic-update-slice_fusion.7, f32[1152,1024]{1,0:T(8,128)} %param.6, s32[]{:T(128)S(6)} %select_n.71), kind=kLoop, calls=%fused_computation.9 | loop fusion | bytes 2097156
  13.1 2.4 %bitcast_dynamic-update-slice_fusion.5 = f32[8,256,1024]{2,1,0:T(8,128)} fusion(f32[8,256,1024]{2,1,0:T(8,128)} %bitcast_dynamic-update-slice_fusion.6, f32[1152,1024]{1,0:T(8,128)} %param.6, s32[]{:T(128)S(6)} %select_n.72), kind=kLoop, calls=%fused_computation.8 | loop fusion | bytes 2097156
  15.5 2.4 %bitcast_dynamic-update-slice_fusion.4 = f32[8,256,1024]{2,1,0:T(8,128)} fusion(f32[8,256,1024]{2,1,0:T(8,128)} %bitcast_dynamic-update-slice_fusion.5, f32[1152,1024]{1,0:T(8,128)} %param.6, s32[]{:T(128)S(6)} %select_n.73), kind=kLoop, calls=%fused_computation.7 | loop fusion | bytes 2097156
  17.9 2.4 %bitcast_dynamic-update-slice_fusion.3 = f32[8,256,1024]{2,1,0:T(8,128)} fusion(f32[8,256,1024]{2,1,0:T(8,128)} %bitcast_dynamic-update-slice_fusion.4, f32[1152,1024]{1,0:T(8,128)} %param.6, s32[]{:T(128)S(6)} %select_n.74), kind=kLoop, calls=%fused_computation.6 | loop fusion | bytes 2097156
  20.2 2.4 %bitcast_dynamic-update-slice_fusion.2 = f32[8,256,1024]{2,1,0:T(8,128)} fusion(f32[8,256,1024]{2,1,0:T(8,128)} %bitcast_dynamic-update-slice_fusion.3, f32[1152,1024]{1,0:T(8,128)} %param.6, s32[]{:T(128)S(6)} %select_n.75), kind=kLoop, calls=%fused_computation.5 | loop fusion | bytes 2097156
  22.7 2.4 %bitcast_dynamic-update-slice_fusion.1 = f32[8,256,1024]{2,1,0:T(8,128)} fusion(f32[8,256,1024]{2,1,0:T(8,128)} %bitcast_dynamic-update-slice_fusion.2, f32[1152,1024]{1,0:T(8,128)} %param.6, s32[]{:T(128)S(6)} %select_n.76), kind=kLoop, calls=%fused_computation.4 | loop fusion | bytes 2097156
  25.1 2.4 %bitcast_dynamic-update-slice_fusion = f32[8,256,1024]{2,1,0:T(8,128)} fusion(f32[8,256,1024]{2,1,0:T(8,128)} %bitcast_dynamic-update-slice_fusion.1, f32[1152,1024]{1,0:T(8,128)} %param.6, s32[]{:T(128)S(6)} %select_n.77), kind=kLoop, calls=%fused_computation.3 | loop fusion | bytes 2097156 | tf_op jit(solution)/shard_map/stack | solution.py:66
  27.5 7.5 %fusion.2 = f32[9,8,2,1024]{3,0,2,1:T(8,128)S(1)} fusion(f32[8,256,1024]{2,1,0:T(8,128)} %bitcast_dynamic-update-slice_fusion, f32[9,1,256]{2,0,1:T(8,128)S(1)} %get-tuple-element.15, f32[9,1,256]{2,0,1:T(8,128)S(1)} %get-tuple-element.16), kind=kOutput, calls=%fused_computation.2 | convolution fusion | flops 452989440 | bytes 8996864 | tf_op jit(solution)/shard_map/fct,btp->fbcp/dot_general | solution.py:72
  35.0 0.9 fusion.23
  35.9 0.8 copy.19
  36.7 21.2 %all_to_all.15 = f32[4,5,8,2,1024]{4,2,3,1,0:T(8,128)S(1)} all-to-all(f32[4,5,8,2,1024]{4,2,3,1,0:T(8,128)S(1)} %bitcast.75), channel_id=1, replica_groups=mesh['space'=64,'tm'=4] {'tm'}, dimensions={0} | all-to-all | bytes 2621440 | tf_op jit(solution)/shard_map/all_to_all | solution.py:76
  58.0 1.2 fusion.30
  59.3 1.3 collective-permute-done
  60.6 2.0 %collective-permute-start.1 = (f32[5,32,32]{1,2,0:T(8,128)S(1)}, f32[5,32,32]{1,2,0:T(8,128)S(1)}, u32[]{:S(2)}, u32[]{:S(2)}) collective-permute-start(f32[5,32,32]{1,2,0:T(8,128)S(1)} %add.107), channel_id=1, source_target_pairs={{0,8},{4,12},{8,0},{12,4},{16,24},{20,28},{24,16},{28,20},{32,40},... | collective-permute-start | bytes 61448 | tf_op jit(solution)/shard_map/ppermute | solution.py:52
  62.6 2.8 %collective-permute-done.1 = f32[5,32,32]{1,2,0:T(8,128)S(1)} collective-permute-done((f32[5,32,32]{1,2,0:T(8,128)S(1)}, f32[5,32,32]{1,2,0:T(8,128)S(1)}, u32[]{:S(2)}, u32[]{:S(2)}) %collective-permute-start.1) | collective-permute-done | bytes 20512 | tf_op jit(solution)/shard_map/ppermute | solution.py:52
  65.4 3.4 %collective-permute-start.2 = (f32[5,32,32]{1,2,0:T(8,128)S(1)}, f32[5,32,32]{1,2,0:T(8,128)S(1)}, u32[]{:S(2)}, u32[]{:S(2)}) collective-permute-start(f32[5,32,32]{1,2,0:T(8,128)S(1)} %add.108), channel_id=1, source_target_pairs={{0,16},{4,20},{8,24},{12,28},{16,0},{20,4},{24,8},{28,12},{32,48},... | collective-permute-start | bytes 61448 | tf_op jit(solution)/shard_map/ppermute | solution.py:52
  68.7 4.0 %collective-permute-done.2 = f32[5,32,32]{1,2,0:T(8,128)S(1)} collective-permute-done((f32[5,32,32]{1,2,0:T(8,128)S(1)}, f32[5,32,32]{1,2,0:T(8,128)S(1)}, u32[]{:S(2)}, u32[]{:S(2)}) %collective-permute-start.2) | collective-permute-done | bytes 20512 | tf_op jit(solution)/shard_map/ppermute | solution.py:52
  72.7 6.2 %collective-permute-start.3 = (f32[5,32,32]{1,2,0:T(8,128)S(1)}, f32[5,32,32]{1,2,0:T(8,128)S(1)}, u32[]{:S(2)}, u32[]{:S(2)}) collective-permute-start(f32[5,32,32]{1,2,0:T(8,128)S(1)} %add.109), channel_id=1, source_target_pairs={{0,32},{4,36},{8,40},{12,44},{16,48},{20,52},{24,56},{28,60},{32,0... | collective-permute-start | bytes 61448 | tf_op jit(solution)/shard_map/ppermute | solution.py:52
  78.9 2.4 %collective-permute-done.3 = f32[5,32,32]{1,2,0:T(8,128)S(1)} collective-permute-done((f32[5,32,32]{1,2,0:T(8,128)S(1)}, f32[5,32,32]{1,2,0:T(8,128)S(1)}, u32[]{:S(2)}, u32[]{:S(2)}) %collective-permute-start.3) | collective-permute-done | bytes 20512 | tf_op jit(solution)/shard_map/ppermute | solution.py:52
  81.4 1.6 collective-permute-start.4
  82.9 2.9 %collective-permute-done.4 = f32[5,32,32]{1,2,0:T(8,128)S(1)} collective-permute-done((f32[5,32,32]{1,2,0:T(8,128)S(1)}, f32[5,32,32]{1,2,0:T(8,128)S(1)}, u32[]{:S(2)}, u32[]{:S(2)}) %collective-permute-start.4) | collective-permute-done | bytes 20512 | tf_op jit(solution)/shard_map/ppermute | solution.py:52
  85.9 3.5 %collective-permute-start.5 = (f32[5,32,32]{1,2,0:T(8,128)S(1)}, f32[5,32,32]{1,2,0:T(8,128)S(1)}, u32[]{:S(2)}, u32[]{:S(2)}) collective-permute-start(f32[5,32,32]{1,2,0:T(8,128)S(1)} %add.111), channel_id=1, source_target_pairs={{0,128},{4,132},{8,136},{12,140},{16,144},{20,148},{24,152},{28,15... | collective-permute-start | bytes 61448 | tf_op jit(solution)/shard_map/ppermute | solution.py:52
  89.4 2.7 %collective-permute-done.5 = f32[5,32,32]{1,2,0:T(8,128)S(1)} collective-permute-done((f32[5,32,32]{1,2,0:T(8,128)S(1)}, f32[5,32,32]{1,2,0:T(8,128)S(1)}, u32[]{:S(2)}, u32[]{:S(2)}) %collective-permute-start.5) | collective-permute-done | bytes 20512 | tf_op jit(solution)/shard_map/ppermute | solution.py:52
  92.5 14.7 %custom-call.8 = f32[5,32,32]{2,1,0:T(8,128)S(1)} custom-call(f32[5,32,32]{2,1,0:T(8,128)S(1)} %fusion.10), custom_call_target="Cholesky" | custom-call | tf_op jit(solution)/shard_map/jit(cholesky)/cholesky | solution.py:38
  107.4 12.3 %custom-call.9 = f32[5,1,32,32]{2,3,1,0:T(8,128)S(1)} custom-call(f32[5,1,32,32]{3,2,1,0:T(8,128)S(1)} %select_bitcast_fusion.1), custom_call_target="InvertDiagBlocksLowerTriangular" | custom-call | tf_op jit(solution)/shard_map/jit(_solve_triangular)/vmap()/triangular_solve | solution.py:39
  119.7 0.3 fusion.8
  120.0 1.2 fusion.31
  121.3 1.2 fusion.32
  122.6 1.3 collective-permute-done.6
  123.9 0.6 collective-permute-start.7
  124.5 4.0 %collective-permute-done.7 = f32[5,32,32]{1,2,0:T(8,128)S(1)} collective-permute-done((f32[5,32,32]{1,2,0:T(8,128)S(1)}, f32[5,32,32]{1,2,0:T(8,128)S(1)}, u32[]{:S(2)}, u32[]{:S(2)}) %collective-permute-start.7) | collective-permute-done | bytes 20512 | tf_op jit(solution)/shard_map/ppermute | solution.py:52
  128.5 2.5 %collective-permute-start.8 = (f32[5,32,32]{1,2,0:T(8,128)S(1)}, f32[5,32,32]{1,2,0:T(8,128)S(1)}, u32[]{:S(2)}, u32[]{:S(2)}) collective-permute-start(f32[5,32,32]{1,2,0:T(8,128)S(1)} %add.115), channel_id=1, source_target_pairs={{0,16},{4,20},{8,24},{12,28},{16,0},{20,4},{24,8},{28,12},{32,48},... | collective-permute-start | bytes 61448 | tf_op jit(solution)/shard_map/ppermute | solution.py:52
  130.9 4.0 %collective-permute-done.8 = f32[5,32,32]{1,2,0:T(8,128)S(1)} collective-permute-done((f32[5,32,32]{1,2,0:T(8,128)S(1)}, f32[5,32,32]{1,2,0:T(8,128)S(1)}, u32[]{:S(2)}, u32[]{:S(2)}) %collective-permute-start.8) | collective-permute-done | bytes 20512 | tf_op jit(solution)/shard_map/ppermute | solution.py:52
  135.0 6.0 %collective-permute-start.9 = (f32[5,32,32]{1,2,0:T(8,128)S(1)}, f32[5,32,32]{1,2,0:T(8,128)S(1)}, u32[]{:S(2)}, u32[]{:S(2)}) collective-permute-start(f32[5,32,32]{1,2,0:T(8,128)S(1)} %add.116), channel_id=1, source_target_pairs={{0,32},{4,36},{8,40},{12,44},{16,48},{20,52},{24,56},{28,60},{32,0... | collective-permute-start | bytes 61448 | tf_op jit(solution)/shard_map/ppermute | solution.py:52
  140.9 3.4 %collective-permute-done.9 = f32[5,32,32]{1,2,0:T(8,128)S(1)} collective-permute-done((f32[5,32,32]{1,2,0:T(8,128)S(1)}, f32[5,32,32]{1,2,0:T(8,128)S(1)}, u32[]{:S(2)}, u32[]{:S(2)}) %collective-permute-start.9) | collective-permute-done | bytes 20512 | tf_op jit(solution)/shard_map/ppermute | solution.py:52
  144.3 1.6 collective-permute-start.10
  145.9 2.9 %collective-permute-done.10 = f32[5,32,32]{1,2,0:T(8,128)S(1)} collective-permute-done((f32[5,32,32]{1,2,0:T(8,128)S(1)}, f32[5,32,32]{1,2,0:T(8,128)S(1)}, u32[]{:S(2)}, u32[]{:S(2)}) %collective-permute-start.10) | collective-permute-done | bytes 20512 | tf_op jit(solution)/shard_map/ppermute | solution.py:52
  148.8 3.9 %collective-permute-start.11 = (f32[5,32,32]{1,2,0:T(8,128)S(1)}, f32[5,32,32]{1,2,0:T(8,128)S(1)}, u32[]{:S(2)}, u32[]{:S(2)}) collective-permute-start(f32[5,32,32]{1,2,0:T(8,128)S(1)} %add.118), channel_id=1, source_target_pairs={{0,128},{4,132},{8,136},{12,140},{16,144},{20,148},{24,152},{28,15... | collective-permute-start | bytes 61448 | tf_op jit(solution)/shard_map/ppermute | solution.py:52
  152.7 2.4 %collective-permute-done.11 = f32[5,32,32]{1,2,0:T(8,128)S(1)} collective-permute-done((f32[5,32,32]{1,2,0:T(8,128)S(1)}, f32[5,32,32]{1,2,0:T(8,128)S(1)}, u32[]{:S(2)}, u32[]{:S(2)}) %collective-permute-start.11) | collective-permute-done | bytes 20512 | tf_op jit(solution)/shard_map/ppermute | solution.py:52
  155.5 14.7 %custom-call.10 = f32[5,32,32]{2,1,0:T(8,128)S(1)} custom-call(f32[5,32,32]{2,1,0:T(8,128)S(1)} %fusion.7), custom_call_target="Cholesky" | custom-call | tf_op jit(solution)/shard_map/jit(cholesky)/cholesky | solution.py:38
  170.4 12.3 %custom-call.11 = f32[5,1,32,32]{2,3,1,0:T(8,128)S(1)} custom-call(f32[5,1,32,32]{3,2,1,0:T(8,128)S(1)} %select_bitcast_fusion), custom_call_target="InvertDiagBlocksLowerTriangular" | custom-call | tf_op jit(solution)/shard_map/jit(_solve_triangular)/vmap()/triangular_solve | solution.py:39
  182.7 0.3 fusion.5
  183.0 1.2 fusion.33
  184.3 2.2 %reshape.155 = f32[5,32,2,1024]{3,2,1,0:T(2,128)} reshape(f32[5,32,2048]{2,1,0:T(8,128)S(1)} %fusion.33) | data formatting | bytes 2621440 | tf_op jit(solution)/shard_map/reshape | solution.py:83
  (36 shorter events, 1.7 us)
Async XLA Ops:
  59.2 1.4 collective-permute-start
  60.6 4.8 %collective-permute-start.1 = (f32[5,32,32]{1,2,0:T(8,128)S(1)}, f32[5,32,32]{1,2,0:T(8,128)S(1)}, u32[]{:S(2)}, u32[]{:S(2)}) collective-permute-start(f32[5,32,32]{1,2,0:T(8,128)S(1)} %add.107), channel_id=1, source_target_pairs={{0,8},{4,12},{8,0},{12,4},{16,24},{20,28},{24,16},{28,20},{32,40},... | collective-permute-start | bytes 61448 | tf_op jit(solution)/shard_map/ppermute | solution.py:52
  65.4 7.3 %collective-permute-start.2 = (f32[5,32,32]{1,2,0:T(8,128)S(1)}, f32[5,32,32]{1,2,0:T(8,128)S(1)}, u32[]{:S(2)}, u32[]{:S(2)}) collective-permute-start(f32[5,32,32]{1,2,0:T(8,128)S(1)} %add.108), channel_id=1, source_target_pairs={{0,16},{4,20},{8,24},{12,28},{16,0},{20,4},{24,8},{28,12},{32,48},... | collective-permute-start | bytes 61448 | tf_op jit(solution)/shard_map/ppermute | solution.py:52
  72.7 8.6 %collective-permute-start.3 = (f32[5,32,32]{1,2,0:T(8,128)S(1)}, f32[5,32,32]{1,2,0:T(8,128)S(1)}, u32[]{:S(2)}, u32[]{:S(2)}) collective-permute-start(f32[5,32,32]{1,2,0:T(8,128)S(1)} %add.109), channel_id=1, source_target_pairs={{0,32},{4,36},{8,40},{12,44},{16,48},{20,52},{24,56},{28,60},{32,0... | collective-permute-start | bytes 61448 | tf_op jit(solution)/shard_map/ppermute | solution.py:52
  81.4 4.5 %collective-permute-start.4 = (f32[5,32,32]{1,2,0:T(8,128)S(1)}, f32[5,32,32]{1,2,0:T(8,128)S(1)}, u32[]{:S(2)}, u32[]{:S(2)}) collective-permute-start(f32[5,32,32]{1,2,0:T(8,128)S(1)} %add.110), channel_id=1, source_target_pairs={{0,64},{4,68},{8,72},{12,76},{16,80},{20,84},{24,88},{28,92},{32,9... | collective-permute-start | bytes 61448 | tf_op jit(solution)/shard_map/ppermute | solution.py:52
  85.9 6.2 %collective-permute-start.5 = (f32[5,32,32]{1,2,0:T(8,128)S(1)}, f32[5,32,32]{1,2,0:T(8,128)S(1)}, u32[]{:S(2)}, u32[]{:S(2)}) collective-permute-start(f32[5,32,32]{1,2,0:T(8,128)S(1)} %add.111), channel_id=1, source_target_pairs={{0,128},{4,132},{8,136},{12,140},{16,144},{20,148},{24,152},{28,15... | collective-permute-start | bytes 61448 | tf_op jit(solution)/shard_map/ppermute | solution.py:52
  122.5 1.4 collective-permute-start.6
  123.9 4.6 %collective-permute-start.7 = (f32[5,32,32]{1,2,0:T(8,128)S(1)}, f32[5,32,32]{1,2,0:T(8,128)S(1)}, u32[]{:S(2)}, u32[]{:S(2)}) collective-permute-start(f32[5,32,32]{1,2,0:T(8,128)S(1)} %add.114), channel_id=1, source_target_pairs={{0,8},{4,12},{8,0},{12,4},{16,24},{20,28},{24,16},{28,20},{32,40},... | collective-permute-start | bytes 61448 | tf_op jit(solution)/shard_map/ppermute | solution.py:52
  128.5 6.5 %collective-permute-start.8 = (f32[5,32,32]{1,2,0:T(8,128)S(1)}, f32[5,32,32]{1,2,0:T(8,128)S(1)}, u32[]{:S(2)}, u32[]{:S(2)}) collective-permute-start(f32[5,32,32]{1,2,0:T(8,128)S(1)} %add.115), channel_id=1, source_target_pairs={{0,16},{4,20},{8,24},{12,28},{16,0},{20,4},{24,8},{28,12},{32,48},... | collective-permute-start | bytes 61448 | tf_op jit(solution)/shard_map/ppermute | solution.py:52
  135.0 9.3 %collective-permute-start.9 = (f32[5,32,32]{1,2,0:T(8,128)S(1)}, f32[5,32,32]{1,2,0:T(8,128)S(1)}, u32[]{:S(2)}, u32[]{:S(2)}) collective-permute-start(f32[5,32,32]{1,2,0:T(8,128)S(1)} %add.116), channel_id=1, source_target_pairs={{0,32},{4,36},{8,40},{12,44},{16,48},{20,52},{24,56},{28,60},{32,0... | collective-permute-start | bytes 61448 | tf_op jit(solution)/shard_map/ppermute | solution.py:52
  144.3 4.5 %collective-permute-start.10 = (f32[5,32,32]{1,2,0:T(8,128)S(1)}, f32[5,32,32]{1,2,0:T(8,128)S(1)}, u32[]{:S(2)}, u32[]{:S(2)}) collective-permute-start(f32[5,32,32]{1,2,0:T(8,128)S(1)} %add.117), channel_id=1, source_target_pairs={{0,64},{4,68},{8,72},{12,76},{16,80},{20,84},{24,88},{28,92},{32,9... | collective-permute-start | bytes 61448 | tf_op jit(solution)/shard_map/ppermute | solution.py:52
  148.8 6.3 %collective-permute-start.11 = (f32[5,32,32]{1,2,0:T(8,128)S(1)}, f32[5,32,32]{1,2,0:T(8,128)S(1)}, u32[]{:S(2)}, u32[]{:S(2)}) collective-permute-start(f32[5,32,32]{1,2,0:T(8,128)S(1)} %add.118), channel_id=1, source_target_pairs={{0,128},{4,132},{8,136},{12,140},{16,144},{20,148},{24,152},{28,15... | collective-permute-start | bytes 61448 | tf_op jit(solution)/shard_map/ppermute | solution.py:52

commit v2 on v1

--- a/solution.py
+++ b/solution.py
@@ -1,6 +1,10 @@
+import functools
+
 import jax
 import jax.numpy as jnp
 from jax import lax
+from jax.experimental import pallas as pl
+from jax.experimental.pallas import tpu as pltpu
 from jax.sharding import PartitionSpec as P
 
 NFFT = 256
@@ -17,6 +21,20 @@
     return jnp.stack([window * jnp.cos(angle), -window * jnp.sin(angle)], axis=1)
 
 
+def windowed_spectra(snapshots, starts):
+    samples = snapshots.shape[0]
+    lag = jnp.arange(samples, dtype=jnp.int32)[None, :] - starts[:, None]
+    inside = (lag >= 0) & (lag < NFFT)
+    times = jnp.clip(lag, 0, NFFT - 1)
+    freqs = jnp.arange(NF, dtype=jnp.int32)
+    phase = freqs[:, None, None] * times[None] % NFFT
+    angle = 2.0 * jnp.pi / NFFT * phase.astype(jnp.float32)
+    window = 0.5 - 0.5 * jnp.cos(2.0 * jnp.pi / NFFT * times.astype(jnp.float32))
+    placed = jnp.stack([window * jnp.cos(angle), -window * jnp.sin(angle)], axis=2)
+    placed = jnp.where(inside[None, :, None, :], placed, 0.0)
+    return jnp.einsum("fbcs,sp->fbcp", placed, snapshots, precision=lax.Precision.HIGHEST)
+
+
 def slot_selector(owner, slot_count):
     freq_ids = jnp.arange(owner.shape[0], dtype=jnp.int32)
     before = (owner[None, :] == owner[:, None]) & (freq_ids[None, :] < freq_ids[:, None])
@@ -30,27 +48,62 @@
     return jnp.einsum("kip,kjp->kij", matrices, matrices, precision=lax.Precision.HIGHEST)
 
 
+def _inverse_factor_kernel(totals_ref, out_ref, *, rows_total):
+    gram = totals_ref[...] / rows_total
+    batch, size, _ = gram.shape
+    row = lax.broadcasted_iota(jnp.int32, gram.shape, 1)
+    col = lax.broadcasted_iota(jnp.int32, gram.shape, 2)
+    diagonal = row == col
+    trace = jnp.sum(jnp.sum(jnp.where(diagonal, gram, 0.0), axis=2, keepdims=True), axis=1, keepdims=True)
+    gram = gram + jnp.where(trace == 0.0, 1.0, 0.0) * diagonal.astype(jnp.float32)
+    row_of = lax.broadcasted_iota(jnp.int32, (batch, size, 1), 1)
+    col_of = lax.broadcasted_iota(jnp.int32, (batch, 1, size), 2)
+
+    def step(j, carry):
+        schur, elim, pivots = carry
+        column = jnp.sum(jnp.where(col == j, schur, 0.0), axis=2, keepdims=True)
+        pivot_row = jnp.sum(jnp.where(row == j, schur, 0.0), axis=1, keepdims=True)
+        elim_row = jnp.sum(jnp.where(row == j, elim, 0.0), axis=1, keepdims=True)
+        pivot = jnp.sum(jnp.where(col_of == j, pivot_row, 0.0), axis=2, keepdims=True)
+        factor = jnp.where(row_of > j, column / pivot, 0.0)
+        schur = schur - factor * pivot_row
+        elim = elim - factor * elim_row
+        pivots = jnp.where(row_of == j, pivot, pivots)
+        return schur, elim, pivots
+
+    start = (gram, diagonal.astype(jnp.float32), jnp.ones((batch, size, 1), jnp.float32))
+    _, elim, pivots = lax.fori_loop(0, size, step, start)
+    out_ref[...] = elim / jnp.sqrt(pivots)
+
+
+def inverse_factor(totals, rows_total):
+    return pl.pallas_call(
+        functools.partial(_inverse_factor_kernel, rows_total=rows_total),
+        out_shape=jax.ShapeDtypeStruct(totals.shape, jnp.float32),
+        in_specs=[pl.BlockSpec(memory_space=pltpu.VMEM)],
+        out_specs=pl.BlockSpec(memory_space=pltpu.VMEM),
+    )(totals)
+
+
 def finish_pass(matrices, totals, rows_total):
-    gram = totals / rows_total
-    identity = jnp.eye(gram.shape[-1], dtype=jnp.float32)
-    diagonal_sum = jnp.trace(gram, axis1=1, axis2=2)
-    gram = gram + jnp.where(diagonal_sum == 0.0, 1.0, 0.0)[:, None, None] * identity
-    factor = jnp.linalg.cholesky(gram)
-    inverse = jax.scipy.linalg.solve_triangular(
-        factor, jnp.broadcast_to(identity, gram.shape), lower=True
-    )
+    inverse = inverse_factor(totals, rows_total)
     return jnp.einsum("kij,kjp->kip", inverse, matrices, precision=lax.Precision.HIGHEST)
 
 
 def reduce_space(values):
     count = lax.axis_size("space")
-    if count & (count - 1):
-        return lax.psum(values, "space")
+    radix = 4
     distance = 1
     while distance < count:
-        pairs = [(index, index ^ distance) for index in range(count)]
-        values = values + lax.ppermute(values, "space", pairs)
-        distance *= 2
+        width = min(radix, count // distance)
+        leaves = [values]
+        for step in range(1, width):
+            pairs = [(index, index ^ (step * distance)) for index in range(count)]
+            leaves.append(lax.ppermute(values, "space", pairs))
+        while len(leaves) > 1:
+            leaves = [leaves[i] + leaves[i + 1] for i in range(0, len(leaves), 2)]
+        values = leaves[0]
+        distance *= width
     return values
 
 
@@ -63,13 +116,7 @@
     rows_total = 2.0 * points * space_count
     column_count = block_count * tm_count
     offset = lax.axis_index("tm") * samples
-    segments = jnp.stack(
-        [
-            lax.dynamic_slice_in_dim(snapshots, block_starts[block] - offset, NFFT, 0)
-            for block in range(block_count)
-        ]
-    )
-    spectra = jnp.einsum("fct,btp->fbcp", table, segments, precision=lax.Precision.HIGHEST)
+    spectra = windowed_spectra(snapshots, block_starts - offset)
     selector = slot_selector(owner, tm_count * FCAP)
     outgoing = jnp.einsum("lf,fbcp->lbcp", selector, spectra, precision=lax.Precision.HIGHEST)
     outgoing = outgoing.reshape(tm_count, FCAP, block_count, 2, points)

time: 188 us -> 118 us (0.63)
  other arithmetic: 56.8 us -> 6.36 us
  local copies, waits for them, and re-layouts: 24 us -> 3.07 us
  Pallas kernels: 0 us -> 11.8 us
  between operations: 5.17 us -> 0.1 us
  starting transfers between devices: 31.3 us -> 27 us
    another operation x12 -> x0, other arithmetic: 54.4 us -> none  [the longest x7 29.6 us: finish_pass(): factor = jnp.linalg.cholesky(gram)]
    unnamed x7 -> x0, local copies, waits for them, and re-layouts: 16.8 us -> none
    pallas_call x0 -> x2, Pallas kernels: none -> 11.8 us  [inverse_factor(): pl.pallas_call(functools.partial(_inverse_factor_kernel, rows_total=rows_...]
    ppermute x12 -> x18, starting transfers between devices: 31.3 us -> 27 us  [reduce_space(): leaves.append(lax.ppermute(values, 'space', pairs))]
    another operation x1 -> x0, local copies, waits for them, and re-layouts: 2.37 us -> none  [local(): jnp.stack([lax.dynamic_slice_in_dim(snapshots, block_starts[block] - offs...]
    mul x1, other arithmetic: 0.09 us -> 2.34 us  [windowed_spectra(): window * jnp.cos(angle)]
    ppermute x12 -> x18, waiting for transfers between devices: 34 us -> 33.4 us  [reduce_space(): leaves.append(lax.ppermute(values, 'space', pairs))]
  transfers between devices with their start and end apart: 12 -> 18, of which waited for: 12 -> 13; matrix products, arithmetic and copies ran while one was open for 0% -> 0% of each run, Pallas kernels for 0% -> 0%
where the time goes in v2:
time: 118 us; the launch traced here: 117 us
  waiting for transfers between devices  33.4 us (28%)
  starting transfers between devices  27 us (23%)
  blocking collectives  21.2 us (18%)
  matrix products  14.4 us (12%)
  Pallas kernels  11.8 us (10%)
  other arithmetic  6.36 us (5%)
  local copies, waits for them, and re-layouts  3.07 us (3%)
    ppermute x18, waiting for transfers between devices, reduce_space(): leaves.append(lax.ppermute(values, 'space', pairs))  33.4 us
    ppermute x18, starting transfers between devices, reduce_space(): leaves.append(lax.ppermute(values, 'space', pairs))  27 us
    all_to_all x1, blocking collectives, local(): lax.all_to_all(outgoing, 'tm', split_axis=0, concat_axis=2, tiled=True)  21.2 us
    pallas_call x2, Pallas kernels, inverse_factor(): pl.pallas_call(functools.partial(_inverse_factor_kernel, rows_total=rows_...  11.8 us
    dot_general x1, matrix products, windowed_spectra(): jnp.einsum('fbcs,sp->fbcp', placed, snapshots, precision=lax.Precision.HI...  6.68 us
    dot_general x2, matrix products, finish_pass(): jnp.einsum('kij,kjp->kip', inverse, matrices, precision=lax.Precision.HIG...  4.24 us
    dot_general x2, matrix products, partial_gram(): jnp.einsum('kip,kjp->kij', matrices, matrices, precision=lax.Precision.HI...  2.6 us
  transfers between devices with their start and end apart: 18, of which 13 were waited for; matrix products, arithmetic and copies ran while one was open for 0% of the time, Pallas kernels for 0%

profile of v2, /device:TPU:8, one launch (start us, length us, event | category | flops | bytes accessed | tf_op | source)
XLA Modules:
  0.0 117.4 jit_solution(2185954415394547342)
XLA Ops:
  0.0 0.7 broadcast_subtract_fusion
  0.8 0.2 multiply_subtract_fusion
  1.0 0.9 convert_reduce_fusion
  2.0 0.7 multiply_add_fusion
  2.6 2.3 %cosine_multiply_fusion = (f32[9,8,1,1152]{3,0,2,1:T(8,128)S(1)}, f32[9,8,1,1152]{3,0,2,1:T(8,128)S(1)}) fusion(s32[8,1152]{1,0:T(8,128)S(1)} %fusion.12, f32[8,1152]{1,0:T(8,128)S(1)} %get-tuple-element.7, f32[8,1152]{1,0:T(8,128)S(1)} %get-tuple-element.8), kind=kLoop, calls=%fused_computation.13 | loop fusion | flops 1327104 | bytes 774144 | tf_op jit(solution)/shard_map/mul | solution.py:33
  5.0 6.7 %fusion = f32[9,8,2,1024]{3,0,2,1:T(8,128)S(1)} fusion(f32[1152,1024]{1,0:T(8,128)} %param.3, f32[9,8,1,1152]{3,0,2,1:T(8,128)S(1)} %get-tuple-element.6, f32[9,8,1,1152]{3,0,2,1:T(8,128)S(1)} %get-tuple-element.5, pred[8,1152]{1,0:T(8,128)(4,1)S(1)} %fusion.15), kind=kOutput, calls=%fused_computation | convolution fusion | flops 2038763520 | bytes 5981184 | tf_op jit(solution)/shard_map/fbcs,sp->fbcp/dot_general | solution.py:35
  11.6 0.9 fusion.19
  12.5 0.8 copy.7
  13.3 21.2 %all_to_all.15 = f32[4,5,8,2,1024]{4,2,3,1,0:T(8,128)S(1)} all-to-all(f32[4,5,8,2,1024]{4,2,3,1,0:T(8,128)S(1)} %bitcast.26), channel_id=1, replica_groups=mesh['space'=64,'tm'=4] {'tm'}, dimensions={0} | all-to-all | bytes 2621440 | tf_op jit(solution)/shard_map/all_to_all | solution.py:123
  34.5 0.1 copy.8
  34.6 1.3 %fusion.24 = f32[5,32,32]{2,1,0:T(8,128)S(1)} fusion(f32[5,32,2048]{2,1,0:T(8,128)S(1)} %bitcast.24), kind=kOutput, calls=%fused_computation.42 | convolution fusion | flops 125829120 | bytes 1331200 | tf_op jit(solution)/shard_map/kip,kjp->kij/dot_general | solution.py:48
  35.9 0.2 collective-permute-start.2
  36.2 1.9 %collective-permute-start.1 = (f32[5,32,32]{2,1,0:T(8,128)S(1)}, f32[5,32,32]{2,1,0:T(8,128)S(1)}, u32[]{:S(2)}, u32[]{:S(2)}) collective-permute-start(f32[5,32,32]{2,1,0:T(8,128)S(1)} %fusion.24), channel_id=1, source_target_pairs={{0,8},{4,12},{8,0},{12,4},{16,24},{20,28},{24,16},{28,20},{32,40},... | collective-permute-start | bytes 61448 | tf_op jit(solution)/shard_map/ppermute | solution.py:102
  38.0 2.3 %collective-permute-done.2 = f32[5,32,32]{2,1,0:T(8,128)S(1)} collective-permute-done((f32[5,32,32]{2,1,0:T(8,128)S(1)}, f32[5,32,32]{2,1,0:T(8,128)S(1)}, u32[]{:S(2)}, u32[]{:S(2)}) %collective-permute-start.2) | collective-permute-done | bytes 20512 | tf_op jit(solution)/shard_map/ppermute | solution.py:102
  40.3 2.1 %collective-permute-done.1 = f32[5,32,32]{2,1,0:T(8,128)S(1)} collective-permute-done((f32[5,32,32]{2,1,0:T(8,128)S(1)}, f32[5,32,32]{2,1,0:T(8,128)S(1)}, u32[]{:S(2)}, u32[]{:S(2)}) %collective-permute-start.1) | collective-permute-done | bytes 20512 | tf_op jit(solution)/shard_map/ppermute | solution.py:102
  42.5 5.6 %collective-permute-start.5 = (f32[5,32,32]{2,1,0:T(8,128)S(1)}, f32[5,32,32]{2,1,0:T(8,128)S(1)}, u32[]{:S(2)}, u32[]{:S(2)}) collective-permute-start(f32[5,32,32]{2,1,0:T(8,128)S(1)} %add_add_fusion.5), channel_id=1, source_target_pairs={{0,48},{4,52},{8,56},{12,60},{16,32},{20,36},{24,40},{28,44},{32,1... | collective-permute-start | bytes 61448 | tf_op jit(solution)/shard_map/ppermute | solution.py:102
  48.1 1.3 %collective-permute-start.4 = (f32[5,32,32]{2,1,0:T(8,128)S(1)}, f32[5,32,32]{2,1,0:T(8,128)S(1)}, u32[]{:S(2)}, u32[]{:S(2)}) collective-permute-start(f32[5,32,32]{2,1,0:T(8,128)S(1)} %add_add_fusion.5), channel_id=1, source_target_pairs={{0,32},{4,36},{8,40},{12,44},{16,48},{20,52},{24,56},{28,60},{32,0... | collective-permute-start | bytes 61448 | tf_op jit(solution)/shard_map/ppermute | solution.py:102
  49.5 1.1 collective-permute-start.3
  50.6 4.8 %collective-permute-done.5 = f32[5,32,32]{2,1,0:T(8,128)S(1)} collective-permute-done((f32[5,32,32]{2,1,0:T(8,128)S(1)}, f32[5,32,32]{2,1,0:T(8,128)S(1)}, u32[]{:S(2)}, u32[]{:S(2)}) %collective-permute-start.5) | collective-permute-done | bytes 20512 | tf_op jit(solution)/shard_map/ppermute | solution.py:102
  55.4 4.5 %collective-permute-done.4 = f32[5,32,32]{2,1,0:T(8,128)S(1)} collective-permute-done((f32[5,32,32]{2,1,0:T(8,128)S(1)}, f32[5,32,32]{2,1,0:T(8,128)S(1)}, u32[]{:S(2)}, u32[]{:S(2)}) %collective-permute-start.4) | collective-permute-done | bytes 20512 | tf_op jit(solution)/shard_map/ppermute | solution.py:102
  59.9 2.8 %collective-permute-start.8 = (f32[5,32,32]{2,1,0:T(8,128)S(1)}, f32[5,32,32]{2,1,0:T(8,128)S(1)}, u32[]{:S(2)}, u32[]{:S(2)}) collective-permute-start(f32[5,32,32]{2,1,0:T(8,128)S(1)} %add_add_fusion.4), channel_id=1, source_target_pairs={{0,192},{4,196},{8,200},{12,204},{16,208},{20,212},{24,216},{28,22... | collective-permute-start | bytes 61448 | tf_op jit(solution)/shard_map/ppermute | solution.py:102
  62.7 0.8 collective-permute-start.7
  63.5 0.5 collective-permute-start.6
  64.0 1.6 %collective-permute-done.8 = f32[5,32,32]{2,1,0:T(8,128)S(1)} collective-permute-done((f32[5,32,32]{2,1,0:T(8,128)S(1)}, f32[5,32,32]{2,1,0:T(8,128)S(1)}, u32[]{:S(2)}, u32[]{:S(2)}) %collective-permute-start.8) | collective-permute-done | bytes 20512 | tf_op jit(solution)/shard_map/ppermute | solution.py:102
  65.6 3.1 %collective-permute-done.7 = f32[5,32,32]{2,1,0:T(8,128)S(1)} collective-permute-done((f32[5,32,32]{2,1,0:T(8,128)S(1)}, f32[5,32,32]{2,1,0:T(8,128)S(1)}, u32[]{:S(2)}, u32[]{:S(2)}) %collective-permute-start.7) | collective-permute-done | bytes 20512 | tf_op jit(solution)/shard_map/ppermute | solution.py:102
  68.7 0.7 add_add_fusion.3.totals_ref
  69.3 5.9 %shard_map.37 = f32[5,32,32]{2,1,0:T(8,128)} custom-call(f32[5,32,32]{2,1,0:T(8,128)} %add_add_fusion.3.totals_ref), custom_call_target="tpu_custom_call" | custom-call | tf_op jit(solution)/shard_map/pallas_call | solution.py:80
  75.2 2.1 %fusion.25 = f32[5,32,2048]{2,1,0:T(8,128)S(1)} fusion(f32[5,32,32]{2,1,0:T(8,128)} %shard_map.37, f32[5,32,2048]{2,1,0:T(8,128)S(1)} %bitcast.25), kind=kOutput, calls=%fused_computation.43 | convolution fusion | flops 125829120 | bytes 2641920 | tf_op jit(solution)/shard_map/kij,kjp->kip/dot_general | solution.py:90
  77.4 1.3 %fusion.26 = f32[5,32,32]{2,1,0:T(8,128)S(1)} fusion(f32[5,32,2048]{2,1,0:T(8,128)S(1)} %fusion.25), kind=kOutput, calls=%fused_computation.44 | convolution fusion | flops 125829120 | bytes 1331200 | tf_op jit(solution)/shard_map/kip,kjp->kij/dot_general | solution.py:48
  78.7 0.1 collective-permute-start.10
  78.8 1.7 %collective-permute-start.9 = (f32[5,32,32]{2,1,0:T(8,128)S(1)}, f32[5,32,32]{2,1,0:T(8,128)S(1)}, u32[]{:S(2)}, u32[]{:S(2)}) collective-permute-start(f32[5,32,32]{2,1,0:T(8,128)S(1)} %fusion.26), channel_id=1, source_target_pairs={{0,4},{4,0},{8,12},{12,8},{16,20},{20,16},{24,28},{28,24},{32,36},... | collective-permute-start | bytes 61448 | tf_op jit(solution)/shard_map/ppermute | solution.py:102
  80.6 2.3 %collective-permute-done.11 = f32[5,32,32]{2,1,0:T(8,128)S(1)} collective-permute-done((f32[5,32,32]{2,1,0:T(8,128)S(1)}, f32[5,32,32]{2,1,0:T(8,128)S(1)}, u32[]{:S(2)}, u32[]{:S(2)}) %collective-permute-start.11) | collective-permute-done | bytes 20512 | tf_op jit(solution)/shard_map/ppermute | solution.py:102
  82.8 1.3 %collective-permute-done.10 = f32[5,32,32]{2,1,0:T(8,128)S(1)} collective-permute-done((f32[5,32,32]{2,1,0:T(8,128)S(1)}, f32[5,32,32]{2,1,0:T(8,128)S(1)}, u32[]{:S(2)}, u32[]{:S(2)}) %collective-permute-start.10) | collective-permute-done | bytes 20512 | tf_op jit(solution)/shard_map/ppermute | solution.py:102
  84.1 2.7 %collective-permute-start.14 = (f32[5,32,32]{2,1,0:T(8,128)S(1)}, f32[5,32,32]{2,1,0:T(8,128)S(1)}, u32[]{:S(2)}, u32[]{:S(2)}) collective-permute-start(f32[5,32,32]{2,1,0:T(8,128)S(1)} %add_add_fusion.2), channel_id=1, source_target_pairs={{0,48},{4,52},{8,56},{12,60},{16,32},{20,36},{24,40},{28,44},{32,1... | collective-permute-start | bytes 61448 | tf_op jit(solution)/shard_map/ppermute | solution.py:102
  86.8 2.6 %collective-permute-start.13 = (f32[5,32,32]{2,1,0:T(8,128)S(1)}, f32[5,32,32]{2,1,0:T(8,128)S(1)}, u32[]{:S(2)}, u32[]{:S(2)}) collective-permute-start(f32[5,32,32]{2,1,0:T(8,128)S(1)} %add_add_fusion.2), channel_id=1, source_target_pairs={{0,32},{4,36},{8,40},{12,44},{16,48},{20,52},{24,56},{28,60},{32,0... | collective-permute-start | bytes 61448 | tf_op jit(solution)/shard_map/ppermute | solution.py:102
  89.4 1.3 %collective-permute-start.12 = (f32[5,32,32]{2,1,0:T(8,128)S(1)}, f32[5,32,32]{2,1,0:T(8,128)S(1)}, u32[]{:S(2)}, u32[]{:S(2)}) collective-permute-start(f32[5,32,32]{2,1,0:T(8,128)S(1)} %add_add_fusion.2), channel_id=1, source_target_pairs={{0,16},{4,20},{8,24},{12,28},{16,0},{20,4},{24,8},{28,12},{32,48},... | collective-permute-start | bytes 61448 | tf_op jit(solution)/shard_map/ppermute | solution.py:102
  90.7 1.5 %collective-permute-done.14 = f32[5,32,32]{2,1,0:T(8,128)S(1)} collective-permute-done((f32[5,32,32]{2,1,0:T(8,128)S(1)}, f32[5,32,32]{2,1,0:T(8,128)S(1)}, u32[]{:S(2)}, u32[]{:S(2)}) %collective-permute-start.14) | collective-permute-done | bytes 20512 | tf_op jit(solution)/shard_map/ppermute | solution.py:102
  92.2 6.5 %collective-permute-done.13 = f32[5,32,32]{2,1,0:T(8,128)S(1)} collective-permute-done((f32[5,32,32]{2,1,0:T(8,128)S(1)}, f32[5,32,32]{2,1,0:T(8,128)S(1)}, u32[]{:S(2)}, u32[]{:S(2)}) %collective-permute-start.13) | collective-permute-done | bytes 20512 | tf_op jit(solution)/shard_map/ppermute | solution.py:102
  98.6 0.4 collective-permute-done.12
  99.1 1.5 %collective-permute-start.17 = (f32[5,32,32]{2,1,0:T(8,128)S(1)}, f32[5,32,32]{2,1,0:T(8,128)S(1)}, u32[]{:S(2)}, u32[]{:S(2)}) collective-permute-start(f32[5,32,32]{2,1,0:T(8,128)S(1)} %add_add_fusion.1), channel_id=1, source_target_pairs={{0,192},{4,196},{8,200},{12,204},{16,208},{20,212},{24,216},{28,22... | collective-permute-start | bytes 61448 | tf_op jit(solution)/shard_map/ppermute | solution.py:102
  100.6 0.8 collective-permute-start.16
  101.4 1.8 %collective-permute-start.15 = (f32[5,32,32]{2,1,0:T(8,128)S(1)}, f32[5,32,32]{2,1,0:T(8,128)S(1)}, u32[]{:S(2)}, u32[]{:S(2)}) collective-permute-start(f32[5,32,32]{2,1,0:T(8,128)S(1)} %add_add_fusion.1), channel_id=1, source_target_pairs={{0,64},{4,68},{8,72},{12,76},{16,80},{20,84},{24,88},{28,92},{32,9... | collective-permute-start | bytes 61448 | tf_op jit(solution)/shard_map/ppermute | solution.py:102
  103.2 1.6 %collective-permute-done.17 = f32[5,32,32]{2,1,0:T(8,128)S(1)} collective-permute-done((f32[5,32,32]{2,1,0:T(8,128)S(1)}, f32[5,32,32]{2,1,0:T(8,128)S(1)}, u32[]{:S(2)}, u32[]{:S(2)}) %collective-permute-start.17) | collective-permute-done | bytes 20512 | tf_op jit(solution)/shard_map/ppermute | solution.py:102
  104.8 1.7 %collective-permute-done.16 = f32[5,32,32]{2,1,0:T(8,128)S(1)} collective-permute-done((f32[5,32,32]{2,1,0:T(8,128)S(1)}, f32[5,32,32]{2,1,0:T(8,128)S(1)}, u32[]{:S(2)}, u32[]{:S(2)}) %collective-permute-start.16) | collective-permute-done | bytes 20512 | tf_op jit(solution)/shard_map/ppermute | solution.py:102
  106.5 0.7 add_add_fusion.totals_ref
  107.2 5.9 %shard_map.38 = f32[5,32,32]{2,1,0:T(8,128)} custom-call(f32[5,32,32]{2,1,0:T(8,128)} %add_add_fusion.totals_ref), custom_call_target="tpu_custom_call" | custom-call | tf_op jit(solution)/shard_map/pallas_call | solution.py:80
  113.1 2.1 %fusion.27 = f32[5,32,2048]{2,1,0:T(8,128)S(1)} fusion(f32[5,32,32]{2,1,0:T(8,128)} %shard_map.38, f32[5,32,2048]{2,1,0:T(8,128)S(1)} %fusion.25), kind=kOutput, calls=%fused_computation.45 | convolution fusion | flops 125829120 | bytes 2641920 | tf_op jit(solution)/shard_map/kij,kjp->kip/dot_general | solution.py:90
  115.2 2.2 %reshape.140 = f32[5,32,2,1024]{3,2,1,0:T(2,128)} reshape(f32[5,32,2048]{2,1,0:T(8,128)S(1)} %fusion.27) | data formatting | bytes 2621440 | tf_op jit(solution)/shard_map/reshape | solution.py:130
  (13 shorter events, 0.4 us)
Async XLA Ops:
  35.9 4.4 %collective-permute-start.2 = (f32[5,32,32]{2,1,0:T(8,128)S(1)}, f32[5,32,32]{2,1,0:T(8,128)S(1)}, u32[]{:S(2)}, u32[]{:S(2)}) collective-permute-start(f32[5,32,32]{2,1,0:T(8,128)S(1)} %fusion.24), channel_id=1, source_target_pairs={{0,12},{4,8},{8,4},{12,0},{16,28},{20,24},{24,20},{28,16},{32,44},... | collective-permute-start | bytes 61448 | tf_op jit(solution)/shard_map/ppermute | solution.py:102
  36.2 6.3 %collective-permute-start.1 = (f32[5,32,32]{2,1,0:T(8,128)S(1)}, f32[5,32,32]{2,1,0:T(8,128)S(1)}, u32[]{:S(2)}, u32[]{:S(2)}) collective-permute-start(f32[5,32,32]{2,1,0:T(8,128)S(1)} %fusion.24), channel_id=1, source_target_pairs={{0,8},{4,12},{8,0},{12,4},{16,24},{20,28},{24,16},{28,20},{32,40},... | collective-permute-start | bytes 61448 | tf_op jit(solution)/shard_map/ppermute | solution.py:102
  38.0 4.5 %collective-permute-start = (f32[5,32,32]{2,1,0:T(8,128)S(1)}, f32[5,32,32]{2,1,0:T(8,128)S(1)}, u32[]{:S(2)}, u32[]{:S(2)}) collective-permute-start(f32[5,32,32]{2,1,0:T(8,128)S(1)} %fusion.24), channel_id=1, source_target_pairs={{0,4},{4,0},{8,12},{12,8},{16,20},{20,16},{24,28},{28,24},{32,36},... | collective-permute-start | bytes 61448 | tf_op jit(solution)/shard_map/ppermute | solution.py:102
  42.5 12.8 %collective-permute-start.5 = (f32[5,32,32]{2,1,0:T(8,128)S(1)}, f32[5,32,32]{2,1,0:T(8,128)S(1)}, u32[]{:S(2)}, u32[]{:S(2)}) collective-permute-start(f32[5,32,32]{2,1,0:T(8,128)S(1)} %add_add_fusion.5), channel_id=1, source_target_pairs={{0,48},{4,52},{8,56},{12,60},{16,32},{20,36},{24,40},{28,44},{32,1... | collective-permute-start | bytes 61448 | tf_op jit(solution)/shard_map/ppermute | solution.py:102
  48.1 11.7 %collective-permute-start.4 = (f32[5,32,32]{2,1,0:T(8,128)S(1)}, f32[5,32,32]{2,1,0:T(8,128)S(1)}, u32[]{:S(2)}, u32[]{:S(2)}) collective-permute-start(f32[5,32,32]{2,1,0:T(8,128)S(1)} %add_add_fusion.5), channel_id=1, source_target_pairs={{0,32},{4,36},{8,40},{12,44},{16,48},{20,52},{24,56},{28,60},{32,0... | collective-permute-start | bytes 61448 | tf_op jit(solution)/shard_map/ppermute | solution.py:102
  49.5 10.4 %collective-permute-start.3 = (f32[5,32,32]{2,1,0:T(8,128)S(1)}, f32[5,32,32]{2,1,0:T(8,128)S(1)}, u32[]{:S(2)}, u32[]{:S(2)}) collective-permute-start(f32[5,32,32]{2,1,0:T(8,128)S(1)} %add_add_fusion.5), channel_id=1, source_target_pairs={{0,16},{4,20},{8,24},{12,28},{16,0},{20,4},{24,8},{28,12},{32,48},... | collective-permute-start | bytes 61448 | tf_op jit(solution)/shard_map/ppermute | solution.py:102
  59.9 5.7 %collective-permute-start.8 = (f32[5,32,32]{2,1,0:T(8,128)S(1)}, f32[5,32,32]{2,1,0:T(8,128)S(1)}, u32[]{:S(2)}, u32[]{:S(2)}) collective-permute-start(f32[5,32,32]{2,1,0:T(8,128)S(1)} %add_add_fusion.4), channel_id=1, source_target_pairs={{0,192},{4,196},{8,200},{12,204},{16,208},{20,212},{24,216},{28,22... | collective-permute-start | bytes 61448 | tf_op jit(solution)/shard_map/ppermute | solution.py:102
  62.7 5.9 %collective-permute-start.7 = (f32[5,32,32]{2,1,0:T(8,128)S(1)}, f32[5,32,32]{2,1,0:T(8,128)S(1)}, u32[]{:S(2)}, u32[]{:S(2)}) collective-permute-start(f32[5,32,32]{2,1,0:T(8,128)S(1)} %add_add_fusion.4), channel_id=1, source_target_pairs={{0,128},{4,132},{8,136},{12,140},{16,144},{20,148},{24,152},{28,15... | collective-permute-start | bytes 61448 | tf_op jit(solution)/shard_map/ppermute | solution.py:102
  63.5 5.2 %collective-permute-start.6 = (f32[5,32,32]{2,1,0:T(8,128)S(1)}, f32[5,32,32]{2,1,0:T(8,128)S(1)}, u32[]{:S(2)}, u32[]{:S(2)}) collective-permute-start(f32[5,32,32]{2,1,0:T(8,128)S(1)} %add_add_fusion.4), channel_id=1, source_target_pairs={{0,64},{4,68},{8,72},{12,76},{16,80},{20,84},{24,88},{28,92},{32,9... | collective-permute-start | bytes 61448 | tf_op jit(solution)/shard_map/ppermute | solution.py:102
  78.7 4.2 %collective-permute-start.11 = (f32[5,32,32]{2,1,0:T(8,128)S(1)}, f32[5,32,32]{2,1,0:T(8,128)S(1)}, u32[]{:S(2)}, u32[]{:S(2)}) collective-permute-start(f32[5,32,32]{2,1,0:T(8,128)S(1)} %fusion.26), channel_id=1, source_target_pairs={{0,12},{4,8},{8,4},{12,0},{16,28},{20,24},{24,20},{28,16},{32,44},... | collective-permute-start | bytes 61448 | tf_op jit(solution)/shard_map/ppermute | solution.py:102
  78.7 5.4 %collective-permute-start.10 = (f32[5,32,32]{2,1,0:T(8,128)S(1)}, f32[5,32,32]{2,1,0:T(8,128)S(1)}, u32[]{:S(2)}, u32[]{:S(2)}) collective-permute-start(f32[5,32,32]{2,1,0:T(8,128)S(1)} %fusion.26), channel_id=1, source_target_pairs={{0,8},{4,12},{8,0},{12,4},{16,24},{20,28},{24,16},{28,20},{32,40},... | collective-permute-start | bytes 61448 | tf_op jit(solution)/shard_map/ppermute | solution.py:102
  78.8 5.3 %collective-permute-start.9 = (f32[5,32,32]{2,1,0:T(8,128)S(1)}, f32[5,32,32]{2,1,0:T(8,128)S(1)}, u32[]{:S(2)}, u32[]{:S(2)}) collective-permute-start(f32[5,32,32]{2,1,0:T(8,128)S(1)} %fusion.26), channel_id=1, source_target_pairs={{0,4},{4,0},{8,12},{12,8},{16,20},{20,16},{24,28},{28,24},{32,36},... | collective-permute-start | bytes 61448 | tf_op jit(solution)/shard_map/ppermute | solution.py:102
  84.1 8.0 %collective-permute-start.14 = (f32[5,32,32]{2,1,0:T(8,128)S(1)}, f32[5,32,32]{2,1,0:T(8,128)S(1)}, u32[]{:S(2)}, u32[]{:S(2)}) collective-permute-start(f32[5,32,32]{2,1,0:T(8,128)S(1)} %add_add_fusion.2), channel_id=1, source_target_pairs={{0,48},{4,52},{8,56},{12,60},{16,32},{20,36},{24,40},{28,44},{32,1... | collective-permute-start | bytes 61448 | tf_op jit(solution)/shard_map/ppermute | solution.py:102
  86.8 11.8 %collective-permute-start.13 = (f32[5,32,32]{2,1,0:T(8,128)S(1)}, f32[5,32,32]{2,1,0:T(8,128)S(1)}, u32[]{:S(2)}, u32[]{:S(2)}) collective-permute-start(f32[5,32,32]{2,1,0:T(8,128)S(1)} %add_add_fusion.2), channel_id=1, source_target_pairs={{0,32},{4,36},{8,40},{12,44},{16,48},{20,52},{24,56},{28,60},{32,0... | collective-permute-start | bytes 61448 | tf_op jit(solution)/shard_map/ppermute | solution.py:102
  89.4 9.6 %collective-permute-start.12 = (f32[5,32,32]{2,1,0:T(8,128)S(1)}, f32[5,32,32]{2,1,0:T(8,128)S(1)}, u32[]{:S(2)}, u32[]{:S(2)}) collective-permute-start(f32[5,32,32]{2,1,0:T(8,128)S(1)} %add_add_fusion.2), channel_id=1, source_target_pairs={{0,16},{4,20},{8,24},{12,28},{16,0},{20,4},{24,8},{28,12},{32,48},... | collective-permute-start | bytes 61448 | tf_op jit(solution)/shard_map/ppermute | solution.py:102
  99.1 5.7 %collective-permute-start.17 = (f32[5,32,32]{2,1,0:T(8,128)S(1)}, f32[5,32,32]{2,1,0:T(8,128)S(1)}, u32[]{:S(2)}, u32[]{:S(2)}) collective-permute-start(f32[5,32,32]{2,1,0:T(8,128)S(1)} %add_add_fusion.1), channel_id=1, source_target_pairs={{0,192},{4,196},{8,200},{12,204},{16,208},{20,212},{24,216},{28,22... | collective-permute-start | bytes 61448 | tf_op jit(solution)/shard_map/ppermute | solution.py:102
  100.6 5.9 %collective-permute-start.16 = (f32[5,32,32]{2,1,0:T(8,128)S(1)}, f32[5,32,32]{2,1,0:T(8,128)S(1)}, u32[]{:S(2)}, u32[]{:S(2)}) collective-permute-start(f32[5,32,32]{2,1,0:T(8,128)S(1)} %add_add_fusion.1), channel_id=1, source_target_pairs={{0,128},{4,132},{8,136},{12,140},{16,144},{20,148},{24,152},{28,15... | collective-permute-start | bytes 61448 | tf_op jit(solution)/shard_map/ppermute | solution.py:102
  101.4 5.1 %collective-permute-start.15 = (f32[5,32,32]{2,1,0:T(8,128)S(1)}, f32[5,32,32]{2,1,0:T(8,128)S(1)}, u32[]{:S(2)}, u32[]{:S(2)}) collective-permute-start(f32[5,32,32]{2,1,0:T(8,128)S(1)} %add_add_fusion.1), channel_id=1, source_target_pairs={{0,64},{4,68},{8,72},{12,76},{16,80},{20,84},{24,88},{28,92},{32,9... | collective-permute-start | bytes 61448 | tf_op jit(solution)/shard_map/ppermute | solution.py:102

commit v3 on v2

--- a/solution.py
+++ b/solution.py
@@ -72,7 +72,7 @@
         return schur, elim, pivots
 
     start = (gram, diagonal.astype(jnp.float32), jnp.ones((batch, size, 1), jnp.float32))
-    _, elim, pivots = lax.fori_loop(0, size, step, start)
+    _, elim, pivots = lax.fori_loop(0, size, step, start, unroll=True)
     out_ref[...] = elim / jnp.sqrt(pivots)
 
 

time: 118 us -> 116 us (0.983)
  Pallas kernels: 11.8 us -> 9.68 us
    pallas_call x2, Pallas kernels: 11.8 us -> 9.68 us  [inverse_factor(): pl.pallas_call(functools.partial(_inverse_factor_kernel, rows_total=rows_...]
where the time goes in v3:
time: 116 us; the launch traced here: 115 us
  waiting for transfers between devices  33.5 us (29%)
  starting transfers between devices  27 us (23%)
  blocking collectives  21.2 us (18%)
  matrix products  14.4 us (12%)
  Pallas kernels  9.68 us (8%)
  other arithmetic  6.36 us (5%)
  local copies, waits for them, and re-layouts  3.07 us (3%)
    ppermute x18, waiting for transfers between devices, reduce_space(): leaves.append(lax.ppermute(values, 'space', pairs))  33.5 us
    ppermute x18, starting transfers between devices, reduce_space(): leaves.append(lax.ppermute(values, 'space', pairs))  27 us
    all_to_all x1, blocking collectives, local(): lax.all_to_all(outgoing, 'tm', split_axis=0, concat_axis=2, tiled=True)  21.2 us
    pallas_call x2, Pallas kernels, inverse_factor(): pl.pallas_call(functools.partial(_inverse_factor_kernel, rows_total=rows_...  9.68 us
    dot_general x1, matrix products, windowed_spectra(): jnp.einsum('fbcs,sp->fbcp', placed, snapshots, precision=lax.Precision.HI...  6.68 us
    dot_general x2, matrix products, finish_pass(): jnp.einsum('kij,kjp->kip', inverse, matrices, precision=lax.Precision.HIG...  4.24 us
    dot_general x2, matrix products, partial_gram(): jnp.einsum('kip,kjp->kij', matrices, matrices, precision=lax.Precision.HI...  2.6 us
    mul x1, other arithmetic, windowed_spectra(): window * jnp.cos(angle)  2.34 us
  transfers between devices with their start and end apart: 18, of which 13 were waited for; matrix products, arithmetic and copies ran while one was open for 0% of the time, Pallas kernels for 0%

profile of v3, /device:TPU:8, one launch (start us, length us, event | category | flops | bytes accessed | tf_op | source)
XLA Modules:
  0.0 115.3 jit_solution(10943662702251533677)
XLA Ops:
  0.0 0.7 broadcast_subtract_fusion
  0.8 0.2 multiply_subtract_fusion
  1.0 0.9 convert_reduce_fusion
  2.0 0.7 multiply_add_fusion
  2.6 2.3 %cosine_multiply_fusion = (f32[9,8,1,1152]{3,0,2,1:T(8,128)S(1)}, f32[9,8,1,1152]{3,0,2,1:T(8,128)S(1)}) fusion(s32[8,1152]{1,0:T(8,128)S(1)} %fusion.12, f32[8,1152]{1,0:T(8,128)S(1)} %get-tuple-element.7, f32[8,1152]{1,0:T(8,128)S(1)} %get-tuple-element.8), kind=kLoop, calls=%fused_computation.13 | loop fusion | flops 1327104 | bytes 774144 | tf_op jit(solution)/shard_map/mul | solution.py:33
  5.0 6.7 %fusion = f32[9,8,2,1024]{3,0,2,1:T(8,128)S(1)} fusion(f32[1152,1024]{1,0:T(8,128)} %param.3, f32[9,8,1,1152]{3,0,2,1:T(8,128)S(1)} %get-tuple-element.6, f32[9,8,1,1152]{3,0,2,1:T(8,128)S(1)} %get-tuple-element.5, pred[8,1152]{1,0:T(8,128)(4,1)S(1)} %fusion.15), kind=kOutput, calls=%fused_computation | convolution fusion | flops 2038763520 | bytes 5981184 | tf_op jit(solution)/shard_map/fbcs,sp->fbcp/dot_general | solution.py:35
  11.6 0.9 fusion.19
  12.5 0.8 copy.7
  13.3 21.2 %all_to_all.15 = f32[4,5,8,2,1024]{4,2,3,1,0:T(8,128)S(1)} all-to-all(f32[4,5,8,2,1024]{4,2,3,1,0:T(8,128)S(1)} %bitcast.26), channel_id=1, replica_groups=mesh['space'=64,'tm'=4] {'tm'}, dimensions={0} | all-to-all | bytes 2621440 | tf_op jit(solution)/shard_map/all_to_all | solution.py:123
  34.5 0.1 copy.8
  34.6 1.3 %fusion.24 = f32[5,32,32]{2,1,0:T(8,128)S(1)} fusion(f32[5,32,2048]{2,1,0:T(8,128)S(1)} %bitcast.24), kind=kOutput, calls=%fused_computation.42 | convolution fusion | flops 125829120 | bytes 1331200 | tf_op jit(solution)/shard_map/kip,kjp->kij/dot_general | solution.py:48
  35.9 0.2 collective-permute-start.2
  36.2 1.9 %collective-permute-start.1 = (f32[5,32,32]{2,1,0:T(8,128)S(1)}, f32[5,32,32]{2,1,0:T(8,128)S(1)}, u32[]{:S(2)}, u32[]{:S(2)}) collective-permute-start(f32[5,32,32]{2,1,0:T(8,128)S(1)} %fusion.24), channel_id=1, source_target_pairs={{0,8},{4,12},{8,0},{12,4},{16,24},{20,28},{24,16},{28,20},{32,40},... | collective-permute-start | bytes 61448 | tf_op jit(solution)/shard_map/ppermute | solution.py:102
  38.0 2.3 %collective-permute-done.2 = f32[5,32,32]{2,1,0:T(8,128)S(1)} collective-permute-done((f32[5,32,32]{2,1,0:T(8,128)S(1)}, f32[5,32,32]{2,1,0:T(8,128)S(1)}, u32[]{:S(2)}, u32[]{:S(2)}) %collective-permute-start.2) | collective-permute-done | bytes 20512 | tf_op jit(solution)/shard_map/ppermute | solution.py:102
  40.3 2.1 %collective-permute-done.1 = f32[5,32,32]{2,1,0:T(8,128)S(1)} collective-permute-done((f32[5,32,32]{2,1,0:T(8,128)S(1)}, f32[5,32,32]{2,1,0:T(8,128)S(1)}, u32[]{:S(2)}, u32[]{:S(2)}) %collective-permute-start.1) | collective-permute-done | bytes 20512 | tf_op jit(solution)/shard_map/ppermute | solution.py:102
  42.5 5.6 %collective-permute-start.5 = (f32[5,32,32]{2,1,0:T(8,128)S(1)}, f32[5,32,32]{2,1,0:T(8,128)S(1)}, u32[]{:S(2)}, u32[]{:S(2)}) collective-permute-start(f32[5,32,32]{2,1,0:T(8,128)S(1)} %add_add_fusion.5), channel_id=1, source_target_pairs={{0,48},{4,52},{8,56},{12,60},{16,32},{20,36},{24,40},{28,44},{32,1... | collective-permute-start | bytes 61448 | tf_op jit(solution)/shard_map/ppermute | solution.py:102
  48.1 1.3 %collective-permute-start.4 = (f32[5,32,32]{2,1,0:T(8,128)S(1)}, f32[5,32,32]{2,1,0:T(8,128)S(1)}, u32[]{:S(2)}, u32[]{:S(2)}) collective-permute-start(f32[5,32,32]{2,1,0:T(8,128)S(1)} %add_add_fusion.5), channel_id=1, source_target_pairs={{0,32},{4,36},{8,40},{12,44},{16,48},{20,52},{24,56},{28,60},{32,0... | collective-permute-start | bytes 61448 | tf_op jit(solution)/shard_map/ppermute | solution.py:102
  49.5 1.1 collective-permute-start.3
  50.6 4.8 %collective-permute-done.5 = f32[5,32,32]{2,1,0:T(8,128)S(1)} collective-permute-done((f32[5,32,32]{2,1,0:T(8,128)S(1)}, f32[5,32,32]{2,1,0:T(8,128)S(1)}, u32[]{:S(2)}, u32[]{:S(2)}) %collective-permute-start.5) | collective-permute-done | bytes 20512 | tf_op jit(solution)/shard_map/ppermute | solution.py:102
  55.4 4.5 %collective-permute-done.4 = f32[5,32,32]{2,1,0:T(8,128)S(1)} collective-permute-done((f32[5,32,32]{2,1,0:T(8,128)S(1)}, f32[5,32,32]{2,1,0:T(8,128)S(1)}, u32[]{:S(2)}, u32[]{:S(2)}) %collective-permute-start.4) | collective-permute-done | bytes 20512 | tf_op jit(solution)/shard_map/ppermute | solution.py:102
  59.9 2.8 %collective-permute-start.8 = (f32[5,32,32]{2,1,0:T(8,128)S(1)}, f32[5,32,32]{2,1,0:T(8,128)S(1)}, u32[]{:S(2)}, u32[]{:S(2)}) collective-permute-start(f32[5,32,32]{2,1,0:T(8,128)S(1)} %add_add_fusion.4), channel_id=1, source_target_pairs={{0,192},{4,196},{8,200},{12,204},{16,208},{20,212},{24,216},{28,22... | collective-permute-start | bytes 61448 | tf_op jit(solution)/shard_map/ppermute | solution.py:102
  62.7 0.8 collective-permute-start.7
  63.5 0.5 collective-permute-start.6
  64.0 1.6 %collective-permute-done.8 = f32[5,32,32]{2,1,0:T(8,128)S(1)} collective-permute-done((f32[5,32,32]{2,1,0:T(8,128)S(1)}, f32[5,32,32]{2,1,0:T(8,128)S(1)}, u32[]{:S(2)}, u32[]{:S(2)}) %collective-permute-start.8) | collective-permute-done | bytes 20512 | tf_op jit(solution)/shard_map/ppermute | solution.py:102
  65.6 3.1 %collective-permute-done.7 = f32[5,32,32]{2,1,0:T(8,128)S(1)} collective-permute-done((f32[5,32,32]{2,1,0:T(8,128)S(1)}, f32[5,32,32]{2,1,0:T(8,128)S(1)}, u32[]{:S(2)}, u32[]{:S(2)}) %collective-permute-start.7) | collective-permute-done | bytes 20512 | tf_op jit(solution)/shard_map/ppermute | solution.py:102
  68.7 0.7 add_add_fusion.3.totals_ref
  69.3 4.8 %shard_map.37 = f32[5,32,32]{2,1,0:T(8,128)} custom-call(f32[5,32,32]{2,1,0:T(8,128)} %add_add_fusion.3.totals_ref), custom_call_target="tpu_custom_call" | custom-call | tf_op jit(solution)/shard_map/pallas_call | solution.py:80
  74.2 2.1 %fusion.25 = f32[5,32,2048]{2,1,0:T(8,128)S(1)} fusion(f32[5,32,32]{2,1,0:T(8,128)} %shard_map.37, f32[5,32,2048]{2,1,0:T(8,128)S(1)} %bitcast.25), kind=kOutput, calls=%fused_computation.43 | convolution fusion | flops 125829120 | bytes 2641920 | tf_op jit(solution)/shard_map/kij,kjp->kip/dot_general | solution.py:90
  76.3 1.3 %fusion.26 = f32[5,32,32]{2,1,0:T(8,128)S(1)} fusion(f32[5,32,2048]{2,1,0:T(8,128)S(1)} %fusion.25), kind=kOutput, calls=%fused_computation.44 | convolution fusion | flops 125829120 | bytes 1331200 | tf_op jit(solution)/shard_map/kip,kjp->kij/dot_general | solution.py:48
  77.7 0.1 collective-permute-start.10
  77.8 1.7 %collective-permute-start.9 = (f32[5,32,32]{2,1,0:T(8,128)S(1)}, f32[5,32,32]{2,1,0:T(8,128)S(1)}, u32[]{:S(2)}, u32[]{:S(2)}) collective-permute-start(f32[5,32,32]{2,1,0:T(8,128)S(1)} %fusion.26), channel_id=1, source_target_pairs={{0,4},{4,0},{8,12},{12,8},{16,20},{20,16},{24,28},{28,24},{32,36},... | collective-permute-start | bytes 61448 | tf_op jit(solution)/shard_map/ppermute | solution.py:102
  79.5 2.3 %collective-permute-done.11 = f32[5,32,32]{2,1,0:T(8,128)S(1)} collective-permute-done((f32[5,32,32]{2,1,0:T(8,128)S(1)}, f32[5,32,32]{2,1,0:T(8,128)S(1)}, u32[]{:S(2)}, u32[]{:S(2)}) %collective-permute-start.11) | collective-permute-done | bytes 20512 | tf_op jit(solution)/shard_map/ppermute | solution.py:102
  81.8 1.3 %collective-permute-done.10 = f32[5,32,32]{2,1,0:T(8,128)S(1)} collective-permute-done((f32[5,32,32]{2,1,0:T(8,128)S(1)}, f32[5,32,32]{2,1,0:T(8,128)S(1)}, u32[]{:S(2)}, u32[]{:S(2)}) %collective-permute-start.10) | collective-permute-done | bytes 20512 | tf_op jit(solution)/shard_map/ppermute | solution.py:102
  83.1 2.7 %collective-permute-start.14 = (f32[5,32,32]{2,1,0:T(8,128)S(1)}, f32[5,32,32]{2,1,0:T(8,128)S(1)}, u32[]{:S(2)}, u32[]{:S(2)}) collective-permute-start(f32[5,32,32]{2,1,0:T(8,128)S(1)} %add_add_fusion.2), channel_id=1, source_target_pairs={{0,48},{4,52},{8,56},{12,60},{16,32},{20,36},{24,40},{28,44},{32,1... | collective-permute-start | bytes 61448 | tf_op jit(solution)/shard_map/ppermute | solution.py:102
  85.8 2.6 %collective-permute-start.13 = (f32[5,32,32]{2,1,0:T(8,128)S(1)}, f32[5,32,32]{2,1,0:T(8,128)S(1)}, u32[]{:S(2)}, u32[]{:S(2)}) collective-permute-start(f32[5,32,32]{2,1,0:T(8,128)S(1)} %add_add_fusion.2), channel_id=1, source_target_pairs={{0,32},{4,36},{8,40},{12,44},{16,48},{20,52},{24,56},{28,60},{32,0... | collective-permute-start | bytes 61448 | tf_op jit(solution)/shard_map/ppermute | solution.py:102
  88.3 1.3 %collective-permute-start.12 = (f32[5,32,32]{2,1,0:T(8,128)S(1)}, f32[5,32,32]{2,1,0:T(8,128)S(1)}, u32[]{:S(2)}, u32[]{:S(2)}) collective-permute-start(f32[5,32,32]{2,1,0:T(8,128)S(1)} %add_add_fusion.2), channel_id=1, source_target_pairs={{0,16},{4,20},{8,24},{12,28},{16,0},{20,4},{24,8},{28,12},{32,48},... | collective-permute-start | bytes 61448 | tf_op jit(solution)/shard_map/ppermute | solution.py:102
  89.6 1.5 %collective-permute-done.14 = f32[5,32,32]{2,1,0:T(8,128)S(1)} collective-permute-done((f32[5,32,32]{2,1,0:T(8,128)S(1)}, f32[5,32,32]{2,1,0:T(8,128)S(1)}, u32[]{:S(2)}, u32[]{:S(2)}) %collective-permute-start.14) | collective-permute-done | bytes 20512 | tf_op jit(solution)/shard_map/ppermute | solution.py:102
  91.1 6.5 %collective-permute-done.13 = f32[5,32,32]{2,1,0:T(8,128)S(1)} collective-permute-done((f32[5,32,32]{2,1,0:T(8,128)S(1)}, f32[5,32,32]{2,1,0:T(8,128)S(1)}, u32[]{:S(2)}, u32[]{:S(2)}) %collective-permute-start.13) | collective-permute-done | bytes 20512 | tf_op jit(solution)/shard_map/ppermute | solution.py:102
  97.6 0.4 collective-permute-done.12
  98.0 1.5 %collective-permute-start.17 = (f32[5,32,32]{2,1,0:T(8,128)S(1)}, f32[5,32,32]{2,1,0:T(8,128)S(1)}, u32[]{:S(2)}, u32[]{:S(2)}) collective-permute-start(f32[5,32,32]{2,1,0:T(8,128)S(1)} %add_add_fusion.1), channel_id=1, source_target_pairs={{0,192},{4,196},{8,200},{12,204},{16,208},{20,212},{24,216},{28,22... | collective-permute-start | bytes 61448 | tf_op jit(solution)/shard_map/ppermute | solution.py:102
  99.5 0.8 collective-permute-start.16
  100.4 1.8 %collective-permute-start.15 = (f32[5,32,32]{2,1,0:T(8,128)S(1)}, f32[5,32,32]{2,1,0:T(8,128)S(1)}, u32[]{:S(2)}, u32[]{:S(2)}) collective-permute-start(f32[5,32,32]{2,1,0:T(8,128)S(1)} %add_add_fusion.1), channel_id=1, source_target_pairs={{0,64},{4,68},{8,72},{12,76},{16,80},{20,84},{24,88},{28,92},{32,9... | collective-permute-start | bytes 61448 | tf_op jit(solution)/shard_map/ppermute | solution.py:102
  102.2 1.6 %collective-permute-done.17 = f32[5,32,32]{2,1,0:T(8,128)S(1)} collective-permute-done((f32[5,32,32]{2,1,0:T(8,128)S(1)}, f32[5,32,32]{2,1,0:T(8,128)S(1)}, u32[]{:S(2)}, u32[]{:S(2)}) %collective-permute-start.17) | collective-permute-done | bytes 20512 | tf_op jit(solution)/shard_map/ppermute | solution.py:102
  103.7 1.7 %collective-permute-done.16 = f32[5,32,32]{2,1,0:T(8,128)S(1)} collective-permute-done((f32[5,32,32]{2,1,0:T(8,128)S(1)}, f32[5,32,32]{2,1,0:T(8,128)S(1)}, u32[]{:S(2)}, u32[]{:S(2)}) %collective-permute-start.16) | collective-permute-done | bytes 20512 | tf_op jit(solution)/shard_map/ppermute | solution.py:102
  105.5 0.7 add_add_fusion.totals_ref
  106.1 4.8 %shard_map.38 = f32[5,32,32]{2,1,0:T(8,128)} custom-call(f32[5,32,32]{2,1,0:T(8,128)} %add_add_fusion.totals_ref), custom_call_target="tpu_custom_call" | custom-call | tf_op jit(solution)/shard_map/pallas_call | solution.py:80
  111.0 2.1 %fusion.27 = f32[5,32,2048]{2,1,0:T(8,128)S(1)} fusion(f32[5,32,32]{2,1,0:T(8,128)} %shard_map.38, f32[5,32,2048]{2,1,0:T(8,128)S(1)} %fusion.25), kind=kOutput, calls=%fused_computation.45 | convolution fusion | flops 125829120 | bytes 2641920 | tf_op jit(solution)/shard_map/kij,kjp->kip/dot_general | solution.py:90
  113.1 2.2 %reshape.140 = f32[5,32,2,1024]{3,2,1,0:T(2,128)} reshape(f32[5,32,2048]{2,1,0:T(8,128)S(1)} %fusion.27) | data formatting | bytes 2621440 | tf_op jit(solution)/shard_map/reshape | solution.py:130
  (13 shorter events, 0.4 us)
Async XLA Ops:
  35.9 4.4 %collective-permute-start.2 = (f32[5,32,32]{2,1,0:T(8,128)S(1)}, f32[5,32,32]{2,1,0:T(8,128)S(1)}, u32[]{:S(2)}, u32[]{:S(2)}) collective-permute-start(f32[5,32,32]{2,1,0:T(8,128)S(1)} %fusion.24), channel_id=1, source_target_pairs={{0,12},{4,8},{8,4},{12,0},{16,28},{20,24},{24,20},{28,16},{32,44},... | collective-permute-start | bytes 61448 | tf_op jit(solution)/shard_map/ppermute | solution.py:102
  36.2 6.3 %collective-permute-start.1 = (f32[5,32,32]{2,1,0:T(8,128)S(1)}, f32[5,32,32]{2,1,0:T(8,128)S(1)}, u32[]{:S(2)}, u32[]{:S(2)}) collective-permute-start(f32[5,32,32]{2,1,0:T(8,128)S(1)} %fusion.24), channel_id=1, source_target_pairs={{0,8},{4,12},{8,0},{12,4},{16,24},{20,28},{24,16},{28,20},{32,40},... | collective-permute-start | bytes 61448 | tf_op jit(solution)/shard_map/ppermute | solution.py:102
  38.0 4.5 %collective-permute-start = (f32[5,32,32]{2,1,0:T(8,128)S(1)}, f32[5,32,32]{2,1,0:T(8,128)S(1)}, u32[]{:S(2)}, u32[]{:S(2)}) collective-permute-start(f32[5,32,32]{2,1,0:T(8,128)S(1)} %fusion.24), channel_id=1, source_target_pairs={{0,4},{4,0},{8,12},{12,8},{16,20},{20,16},{24,28},{28,24},{32,36},... | collective-permute-start | bytes 61448 | tf_op jit(solution)/shard_map/ppermute | solution.py:102
  42.5 12.8 %collective-permute-start.5 = (f32[5,32,32]{2,1,0:T(8,128)S(1)}, f32[5,32,32]{2,1,0:T(8,128)S(1)}, u32[]{:S(2)}, u32[]{:S(2)}) collective-permute-start(f32[5,32,32]{2,1,0:T(8,128)S(1)} %add_add_fusion.5), channel_id=1, source_target_pairs={{0,48},{4,52},{8,56},{12,60},{16,32},{20,36},{24,40},{28,44},{32,1... | collective-permute-start | bytes 61448 | tf_op jit(solution)/shard_map/ppermute | solution.py:102
  48.1 11.7 %collective-permute-start.4 = (f32[5,32,32]{2,1,0:T(8,128)S(1)}, f32[5,32,32]{2,1,0:T(8,128)S(1)}, u32[]{:S(2)}, u32[]{:S(2)}) collective-permute-start(f32[5,32,32]{2,1,0:T(8,128)S(1)} %add_add_fusion.5), channel_id=1, source_target_pairs={{0,32},{4,36},{8,40},{12,44},{16,48},{20,52},{24,56},{28,60},{32,0... | collective-permute-start | bytes 61448 | tf_op jit(solution)/shard_map/ppermute | solution.py:102
  49.5 10.4 %collective-permute-start.3 = (f32[5,32,32]{2,1,0:T(8,128)S(1)}, f32[5,32,32]{2,1,0:T(8,128)S(1)}, u32[]{:S(2)}, u32[]{:S(2)}) collective-permute-start(f32[5,32,32]{2,1,0:T(8,128)S(1)} %add_add_fusion.5), channel_id=1, source_target_pairs={{0,16},{4,20},{8,24},{12,28},{16,0},{20,4},{24,8},{28,12},{32,48},... | collective-permute-start | bytes 61448 | tf_op jit(solution)/shard_map/ppermute | solution.py:102
  59.9 5.7 %collective-permute-start.8 = (f32[5,32,32]{2,1,0:T(8,128)S(1)}, f32[5,32,32]{2,1,0:T(8,128)S(1)}, u32[]{:S(2)}, u32[]{:S(2)}) collective-permute-start(f32[5,32,32]{2,1,0:T(8,128)S(1)} %add_add_fusion.4), channel_id=1, source_target_pairs={{0,192},{4,196},{8,200},{12,204},{16,208},{20,212},{24,216},{28,22... | collective-permute-start | bytes 61448 | tf_op jit(solution)/shard_map/ppermute | solution.py:102
  62.7 5.9 %collective-permute-start.7 = (f32[5,32,32]{2,1,0:T(8,128)S(1)}, f32[5,32,32]{2,1,0:T(8,128)S(1)}, u32[]{:S(2)}, u32[]{:S(2)}) collective-permute-start(f32[5,32,32]{2,1,0:T(8,128)S(1)} %add_add_fusion.4), channel_id=1, source_target_pairs={{0,128},{4,132},{8,136},{12,140},{16,144},{20,148},{24,152},{28,15... | collective-permute-start | bytes 61448 | tf_op jit(solution)/shard_map/ppermute | solution.py:102
  63.5 5.2 %collective-permute-start.6 = (f32[5,32,32]{2,1,0:T(8,128)S(1)}, f32[5,32,32]{2,1,0:T(8,128)S(1)}, u32[]{:S(2)}, u32[]{:S(2)}) collective-permute-start(f32[5,32,32]{2,1,0:T(8,128)S(1)} %add_add_fusion.4), channel_id=1, source_target_pairs={{0,64},{4,68},{8,72},{12,76},{16,80},{20,84},{24,88},{28,92},{32,9... | collective-permute-start | bytes 61448 | tf_op jit(solution)/shard_map/ppermute | solution.py:102
  77.6 4.2 %collective-permute-start.11 = (f32[5,32,32]{2,1,0:T(8,128)S(1)}, f32[5,32,32]{2,1,0:T(8,128)S(1)}, u32[]{:S(2)}, u32[]{:S(2)}) collective-permute-start(f32[5,32,32]{2,1,0:T(8,128)S(1)} %fusion.26), channel_id=1, source_target_pairs={{0,12},{4,8},{8,4},{12,0},{16,28},{20,24},{24,20},{28,16},{32,44},... | collective-permute-start | bytes 61448 | tf_op jit(solution)/shard_map/ppermute | solution.py:102
  77.7 5.4 %collective-permute-start.10 = (f32[5,32,32]{2,1,0:T(8,128)S(1)}, f32[5,32,32]{2,1,0:T(8,128)S(1)}, u32[]{:S(2)}, u32[]{:S(2)}) collective-permute-start(f32[5,32,32]{2,1,0:T(8,128)S(1)} %fusion.26), channel_id=1, source_target_pairs={{0,8},{4,12},{8,0},{12,4},{16,24},{20,28},{24,16},{28,20},{32,40},... | collective-permute-start | bytes 61448 | tf_op jit(solution)/shard_map/ppermute | solution.py:102
  77.8 5.3 %collective-permute-start.9 = (f32[5,32,32]{2,1,0:T(8,128)S(1)}, f32[5,32,32]{2,1,0:T(8,128)S(1)}, u32[]{:S(2)}, u32[]{:S(2)}) collective-permute-start(f32[5,32,32]{2,1,0:T(8,128)S(1)} %fusion.26), channel_id=1, source_target_pairs={{0,4},{4,0},{8,12},{12,8},{16,20},{20,16},{24,28},{28,24},{32,36},... | collective-permute-start | bytes 61448 | tf_op jit(solution)/shard_map/ppermute | solution.py:102
  83.1 8.1 %collective-permute-start.14 = (f32[5,32,32]{2,1,0:T(8,128)S(1)}, f32[5,32,32]{2,1,0:T(8,128)S(1)}, u32[]{:S(2)}, u32[]{:S(2)}) collective-permute-start(f32[5,32,32]{2,1,0:T(8,128)S(1)} %add_add_fusion.2), channel_id=1, source_target_pairs={{0,48},{4,52},{8,56},{12,60},{16,32},{20,36},{24,40},{28,44},{32,1... | collective-permute-start | bytes 61448 | tf_op jit(solution)/shard_map/ppermute | solution.py:102
  85.8 11.8 %collective-permute-start.13 = (f32[5,32,32]{2,1,0:T(8,128)S(1)}, f32[5,32,32]{2,1,0:T(8,128)S(1)}, u32[]{:S(2)}, u32[]{:S(2)}) collective-permute-start(f32[5,32,32]{2,1,0:T(8,128)S(1)} %add_add_fusion.2), channel_id=1, source_target_pairs={{0,32},{4,36},{8,40},{12,44},{16,48},{20,52},{24,56},{28,60},{32,0... | collective-permute-start | bytes 61448 | tf_op jit(solution)/shard_map/ppermute | solution.py:102
  88.3 9.6 %collective-permute-start.12 = (f32[5,32,32]{2,1,0:T(8,128)S(1)}, f32[5,32,32]{2,1,0:T(8,128)S(1)}, u32[]{:S(2)}, u32[]{:S(2)}) collective-permute-start(f32[5,32,32]{2,1,0:T(8,128)S(1)} %add_add_fusion.2), channel_id=1, source_target_pairs={{0,16},{4,20},{8,24},{12,28},{16,0},{20,4},{24,8},{28,12},{32,48},... | collective-permute-start | bytes 61448 | tf_op jit(solution)/shard_map/ppermute | solution.py:102
  98.0 5.7 %collective-permute-start.17 = (f32[5,32,32]{2,1,0:T(8,128)S(1)}, f32[5,32,32]{2,1,0:T(8,128)S(1)}, u32[]{:S(2)}, u32[]{:S(2)}) collective-permute-start(f32[5,32,32]{2,1,0:T(8,128)S(1)} %add_add_fusion.1), channel_id=1, source_target_pairs={{0,192},{4,196},{8,200},{12,204},{16,208},{20,212},{24,216},{28,22... | collective-permute-start | bytes 61448 | tf_op jit(solution)/shard_map/ppermute | solution.py:102
  99.5 5.9 %collective-permute-start.16 = (f32[5,32,32]{2,1,0:T(8,128)S(1)}, f32[5,32,32]{2,1,0:T(8,128)S(1)}, u32[]{:S(2)}, u32[]{:S(2)}) collective-permute-start(f32[5,32,32]{2,1,0:T(8,128)S(1)} %add_add_fusion.1), channel_id=1, source_target_pairs={{0,128},{4,132},{8,136},{12,140},{16,144},{20,148},{24,152},{28,15... | collective-permute-start | bytes 61448 | tf_op jit(solution)/shard_map/ppermute | solution.py:102
  100.4 5.1 %collective-permute-start.15 = (f32[5,32,32]{2,1,0:T(8,128)S(1)}, f32[5,32,32]{2,1,0:T(8,128)S(1)}, u32[]{:S(2)}, u32[]{:S(2)}) collective-permute-start(f32[5,32,32]{2,1,0:T(8,128)S(1)} %add_add_fusion.1), channel_id=1, source_target_pairs={{0,64},{4,68},{8,72},{12,76},{16,80},{20,84},{24,88},{28,92},{32,9... | collective-permute-start | bytes 61448 | tf_op jit(solution)/shard_map/ppermute | solution.py:102

commit v4 on v3

--- a/solution.py
+++ b/solution.py
@@ -92,18 +92,14 @@
 
 def reduce_space(values):
     count = lax.axis_size("space")
-    radix = 4
-    distance = 1
-    while distance < count:
-        width = min(radix, count // distance)
+    for masks in [[4, 8, 12], [1, 2, 3], [16, 32, 48]]:
         leaves = [values]
-        for step in range(1, width):
-            pairs = [(index, index ^ (step * distance)) for index in range(count)]
+        for mask in masks:
+            pairs = [(index, index ^ mask) for index in range(count)]
             leaves.append(lax.ppermute(values, "space", pairs))
         while len(leaves) > 1:
             leaves = [leaves[i] + leaves[i + 1] for i in range(0, len(leaves), 2)]
         values = leaves[0]
-        distance *= width
     return values
 
 

time: 116 us -> 114 us (0.983)
  waiting for transfers between devices: 33.5 us -> 31.2 us
    ppermute x18, waiting for transfers between devices: 33.5 us -> 31.2 us  [reduce_space(): leaves.append(lax.ppermute(values, 'space', pairs))]
where the time goes in v4:
time: 114 us
  waiting for transfers between devices  31.2 us (27%)
  starting transfers between devices  27.6 us (24%)
  blocking collectives  21.2 us (19%)
  matrix products  14.4 us (13%)
  Pallas kernels  9.68 us (8%)
  other arithmetic  6.36 us (6%)
  local copies, waits for them, and re-layouts  3.07 us (3%)
    ppermute x18, waiting for transfers between devices, reduce_space(): leaves.append(lax.ppermute(values, 'space', pairs))  31.2 us
    ppermute x18, starting transfers between devices, reduce_space(): leaves.append(lax.ppermute(values, 'space', pairs))  27.6 us
    all_to_all x1, blocking collectives, local(): lax.all_to_all(outgoing, 'tm', split_axis=0, concat_axis=2, tiled=True)  21.2 us
    pallas_call x2, Pallas kernels, inverse_factor(): pl.pallas_call(functools.partial(_inverse_factor_kernel, rows_total=rows_...  9.68 us
    dot_general x1, matrix products, windowed_spectra(): jnp.einsum('fbcs,sp->fbcp', placed, snapshots, precision=lax.Precision.HI...  6.68 us
    dot_general x2, matrix products, finish_pass(): jnp.einsum('kij,kjp->kip', inverse, matrices, precision=lax.Precision.HIG...  4.24 us
    dot_general x2, matrix products, partial_gram(): jnp.einsum('kip,kjp->kij', matrices, matrices, precision=lax.Precision.HI...  2.6 us
    mul x1, other arithmetic, windowed_spectra(): window * jnp.cos(angle)  2.34 us
  transfers between devices with their start and end apart: 18, of which 13 were waited for; matrix products, arithmetic and copies ran while one was open for 0% of the time, Pallas kernels for 0%

profile of v4, /device:TPU:8, one launch (start us, length us, event | category | flops | bytes accessed | tf_op | source)
XLA Modules:
  0.0 113.6 jit_solution(4280587956057866351)
XLA Ops:
  0.0 0.7 broadcast_subtract_fusion
  0.8 0.2 multiply_subtract_fusion
  1.0 0.9 convert_reduce_fusion
  2.0 0.7 multiply_add_fusion
  2.6 2.3 %cosine_multiply_fusion = (f32[9,8,1,1152]{3,0,2,1:T(8,128)S(1)}, f32[9,8,1,1152]{3,0,2,1:T(8,128)S(1)}) fusion(s32[8,1152]{1,0:T(8,128)S(1)} %fusion.12, f32[8,1152]{1,0:T(8,128)S(1)} %get-tuple-element.7, f32[8,1152]{1,0:T(8,128)S(1)} %get-tuple-element.8), kind=kLoop, calls=%fused_computation.13 | loop fusion | flops 1327104 | bytes 774144 | tf_op jit(solution)/shard_map/mul | solution.py:33
  5.0 6.7 %fusion = f32[9,8,2,1024]{3,0,2,1:T(8,128)S(1)} fusion(f32[1152,1024]{1,0:T(8,128)} %param.3, f32[9,8,1,1152]{3,0,2,1:T(8,128)S(1)} %get-tuple-element.6, f32[9,8,1,1152]{3,0,2,1:T(8,128)S(1)} %get-tuple-element.5, pred[8,1152]{1,0:T(8,128)(4,1)S(1)} %fusion.15), kind=kOutput, calls=%fused_computation | convolution fusion | flops 2038763520 | bytes 5981184 | tf_op jit(solution)/shard_map/fbcs,sp->fbcp/dot_general | solution.py:35
  11.6 0.9 fusion.19
  12.5 0.8 copy.7
  13.3 21.2 %all_to_all.15 = f32[4,5,8,2,1024]{4,2,3,1,0:T(8,128)S(1)} all-to-all(f32[4,5,8,2,1024]{4,2,3,1,0:T(8,128)S(1)} %bitcast.26), channel_id=1, replica_groups=mesh['space'=64,'tm'=4] {'tm'}, dimensions={0} | all-to-all | bytes 2621440 | tf_op jit(solution)/shard_map/all_to_all | solution.py:119
  34.5 0.1 copy.8
  34.6 1.3 %fusion.24 = f32[5,32,32]{2,1,0:T(8,128)S(1)} fusion(f32[5,32,2048]{2,1,0:T(8,128)S(1)} %bitcast.24), kind=kOutput, calls=%fused_computation.42 | convolution fusion | flops 125829120 | bytes 1331200 | tf_op jit(solution)/shard_map/kip,kjp->kij/dot_general | solution.py:48
  35.9 6.4 %collective-permute-start.2 = (f32[5,32,32]{2,1,0:T(8,128)S(1)}, f32[5,32,32]{2,1,0:T(8,128)S(1)}, u32[]{:S(2)}, u32[]{:S(2)}) collective-permute-start(f32[5,32,32]{2,1,0:T(8,128)S(1)} %fusion.24), channel_id=1, source_target_pairs={{0,48},{4,52},{8,56},{12,60},{16,32},{20,36},{24,40},{28,44},{32,1... | collective-permute-start | bytes 61448 | tf_op jit(solution)/shard_map/ppermute | solution.py:99
  42.3 1.0 collective-permute-start.1
  43.3 1.5 %collective-permute-start = (f32[5,32,32]{2,1,0:T(8,128)S(1)}, f32[5,32,32]{2,1,0:T(8,128)S(1)}, u32[]{:S(2)}, u32[]{:S(2)}) collective-permute-start(f32[5,32,32]{2,1,0:T(8,128)S(1)} %fusion.24), channel_id=1, source_target_pairs={{0,16},{4,20},{8,24},{12,28},{16,0},{20,4},{24,8},{28,12},{32,48},... | collective-permute-start | bytes 61448 | tf_op jit(solution)/shard_map/ppermute | solution.py:99
  44.7 3.1 %collective-permute-done.2 = f32[5,32,32]{2,1,0:T(8,128)S(1)} collective-permute-done((f32[5,32,32]{2,1,0:T(8,128)S(1)}, f32[5,32,32]{2,1,0:T(8,128)S(1)}, u32[]{:S(2)}, u32[]{:S(2)}) %collective-permute-start.2) | collective-permute-done | bytes 20512 | tf_op jit(solution)/shard_map/ppermute | solution.py:99
  47.8 4.5 %collective-permute-done.1 = f32[5,32,32]{2,1,0:T(8,128)S(1)} collective-permute-done((f32[5,32,32]{2,1,0:T(8,128)S(1)}, f32[5,32,32]{2,1,0:T(8,128)S(1)}, u32[]{:S(2)}, u32[]{:S(2)}) %collective-permute-start.1) | collective-permute-done | bytes 20512 | tf_op jit(solution)/shard_map/ppermute | solution.py:99
  52.4 0.4 collective-permute-start.4
  52.8 1.5 %collective-permute-start.3 = (f32[5,32,32]{2,1,0:T(8,128)S(1)}, f32[5,32,32]{2,1,0:T(8,128)S(1)}, u32[]{:S(2)}, u32[]{:S(2)}) collective-permute-start(f32[5,32,32]{2,1,0:T(8,128)S(1)} %add_add_fusion.5), channel_id=1, source_target_pairs={{0,4},{4,0},{8,12},{12,8},{16,20},{20,16},{24,28},{28,24},{32,36},... | collective-permute-start | bytes 61448 | tf_op jit(solution)/shard_map/ppermute | solution.py:99
  54.3 2.3 %collective-permute-done.5 = f32[5,32,32]{2,1,0:T(8,128)S(1)} collective-permute-done((f32[5,32,32]{2,1,0:T(8,128)S(1)}, f32[5,32,32]{2,1,0:T(8,128)S(1)}, u32[]{:S(2)}, u32[]{:S(2)}) %collective-permute-start.5) | collective-permute-done | bytes 20512 | tf_op jit(solution)/shard_map/ppermute | solution.py:99
  56.5 1.3 %collective-permute-done.4 = f32[5,32,32]{2,1,0:T(8,128)S(1)} collective-permute-done((f32[5,32,32]{2,1,0:T(8,128)S(1)}, f32[5,32,32]{2,1,0:T(8,128)S(1)}, u32[]{:S(2)}, u32[]{:S(2)}) %collective-permute-start.4) | collective-permute-done | bytes 20512 | tf_op jit(solution)/shard_map/ppermute | solution.py:99
  57.8 2.9 %collective-permute-start.8 = (f32[5,32,32]{2,1,0:T(8,128)S(1)}, f32[5,32,32]{2,1,0:T(8,128)S(1)}, u32[]{:S(2)}, u32[]{:S(2)}) collective-permute-start(f32[5,32,32]{2,1,0:T(8,128)S(1)} %add_add_fusion.4), channel_id=1, source_target_pairs={{0,192},{4,196},{8,200},{12,204},{16,208},{20,212},{24,216},{28,22... | collective-permute-start | bytes 61448 | tf_op jit(solution)/shard_map/ppermute | solution.py:99
  60.7 0.8 collective-permute-start.7
  61.5 0.5 collective-permute-start.6
  62.0 2.4 %collective-permute-done.8 = f32[5,32,32]{2,1,0:T(8,128)S(1)} collective-permute-done((f32[5,32,32]{2,1,0:T(8,128)S(1)}, f32[5,32,32]{2,1,0:T(8,128)S(1)}, u32[]{:S(2)}, u32[]{:S(2)}) %collective-permute-start.8) | collective-permute-done | bytes 20512 | tf_op jit(solution)/shard_map/ppermute | solution.py:99
  64.4 2.8 %collective-permute-done.7 = f32[5,32,32]{2,1,0:T(8,128)S(1)} collective-permute-done((f32[5,32,32]{2,1,0:T(8,128)S(1)}, f32[5,32,32]{2,1,0:T(8,128)S(1)}, u32[]{:S(2)}, u32[]{:S(2)}) %collective-permute-start.7) | collective-permute-done | bytes 20512 | tf_op jit(solution)/shard_map/ppermute | solution.py:99
  67.2 0.7 add_add_fusion.3.totals_ref
  67.9 4.8 %shard_map.37 = f32[5,32,32]{2,1,0:T(8,128)} custom-call(f32[5,32,32]{2,1,0:T(8,128)} %add_add_fusion.3.totals_ref), custom_call_target="tpu_custom_call" | custom-call | tf_op jit(solution)/shard_map/pallas_call | solution.py:80
  72.7 2.1 %fusion.25 = f32[5,32,2048]{2,1,0:T(8,128)S(1)} fusion(f32[5,32,32]{2,1,0:T(8,128)} %shard_map.37, f32[5,32,2048]{2,1,0:T(8,128)S(1)} %bitcast.25), kind=kOutput, calls=%fused_computation.43 | convolution fusion | flops 125829120 | bytes 2641920 | tf_op jit(solution)/shard_map/kij,kjp->kip/dot_general | solution.py:90
  74.9 1.3 %fusion.26 = f32[5,32,32]{2,1,0:T(8,128)S(1)} fusion(f32[5,32,2048]{2,1,0:T(8,128)S(1)} %fusion.25), kind=kOutput, calls=%fused_computation.44 | convolution fusion | flops 125829120 | bytes 1331200 | tf_op jit(solution)/shard_map/kip,kjp->kij/dot_general | solution.py:48
  76.2 2.8 %collective-permute-start.11 = (f32[5,32,32]{2,1,0:T(8,128)S(1)}, f32[5,32,32]{2,1,0:T(8,128)S(1)}, u32[]{:S(2)}, u32[]{:S(2)}) collective-permute-start(f32[5,32,32]{2,1,0:T(8,128)S(1)} %fusion.26), channel_id=1, source_target_pairs={{0,48},{4,52},{8,56},{12,60},{16,32},{20,36},{24,40},{28,44},{32,1... | collective-permute-start | bytes 61448 | tf_op jit(solution)/shard_map/ppermute | solution.py:99
  79.0 2.0 %collective-permute-start.10 = (f32[5,32,32]{2,1,0:T(8,128)S(1)}, f32[5,32,32]{2,1,0:T(8,128)S(1)}, u32[]{:S(2)}, u32[]{:S(2)}) collective-permute-start(f32[5,32,32]{2,1,0:T(8,128)S(1)} %fusion.26), channel_id=1, source_target_pairs={{0,32},{4,36},{8,40},{12,44},{16,48},{20,52},{24,56},{28,60},{32,0... | collective-permute-start | bytes 61448 | tf_op jit(solution)/shard_map/ppermute | solution.py:99
  81.1 1.7 %collective-permute-start.9 = (f32[5,32,32]{2,1,0:T(8,128)S(1)}, f32[5,32,32]{2,1,0:T(8,128)S(1)}, u32[]{:S(2)}, u32[]{:S(2)}) collective-permute-start(f32[5,32,32]{2,1,0:T(8,128)S(1)} %fusion.26), channel_id=1, source_target_pairs={{0,16},{4,20},{8,24},{12,28},{16,0},{20,4},{24,8},{28,12},{32,48},... | collective-permute-start | bytes 61448 | tf_op jit(solution)/shard_map/ppermute | solution.py:99
  82.7 0.2 collective-permute-done.11
  82.9 5.0 %collective-permute-done.10 = f32[5,32,32]{2,1,0:T(8,128)S(1)} collective-permute-done((f32[5,32,32]{2,1,0:T(8,128)S(1)}, f32[5,32,32]{2,1,0:T(8,128)S(1)}, u32[]{:S(2)}, u32[]{:S(2)}) %collective-permute-start.10) | collective-permute-done | bytes 20512 | tf_op jit(solution)/shard_map/ppermute | solution.py:99
  87.9 0.9 collective-permute-done.9
  88.9 0.6 collective-permute-start.13
  89.4 1.3 %collective-permute-start.12 = (f32[5,32,32]{2,1,0:T(8,128)S(1)}, f32[5,32,32]{2,1,0:T(8,128)S(1)}, u32[]{:S(2)}, u32[]{:S(2)}) collective-permute-start(f32[5,32,32]{2,1,0:T(8,128)S(1)} %add_add_fusion.2), channel_id=1, source_target_pairs={{0,4},{4,0},{8,12},{12,8},{16,20},{20,16},{24,28},{28,24},{32,36},... | collective-permute-start | bytes 61448 | tf_op jit(solution)/shard_map/ppermute | solution.py:99
  90.7 2.3 %collective-permute-done.14 = f32[5,32,32]{2,1,0:T(8,128)S(1)} collective-permute-done((f32[5,32,32]{2,1,0:T(8,128)S(1)}, f32[5,32,32]{2,1,0:T(8,128)S(1)}, u32[]{:S(2)}, u32[]{:S(2)}) %collective-permute-start.14) | collective-permute-done | bytes 20512 | tf_op jit(solution)/shard_map/ppermute | solution.py:99
  93.0 1.3 %collective-permute-done.13 = f32[5,32,32]{2,1,0:T(8,128)S(1)} collective-permute-done((f32[5,32,32]{2,1,0:T(8,128)S(1)}, f32[5,32,32]{2,1,0:T(8,128)S(1)}, u32[]{:S(2)}, u32[]{:S(2)}) %collective-permute-start.13) | collective-permute-done | bytes 20512 | tf_op jit(solution)/shard_map/ppermute | solution.py:99
  94.3 3.0 %collective-permute-start.17 = (f32[5,32,32]{2,1,0:T(8,128)S(1)}, f32[5,32,32]{2,1,0:T(8,128)S(1)}, u32[]{:S(2)}, u32[]{:S(2)}) collective-permute-start(f32[5,32,32]{2,1,0:T(8,128)S(1)} %add_add_fusion.1), channel_id=1, source_target_pairs={{0,192},{4,196},{8,200},{12,204},{16,208},{20,212},{24,216},{28,22... | collective-permute-start | bytes 61448 | tf_op jit(solution)/shard_map/ppermute | solution.py:99
  97.2 0.5 collective-permute-start.16
  97.7 0.7 collective-permute-start.15
  98.4 2.6 %collective-permute-done.17 = f32[5,32,32]{2,1,0:T(8,128)S(1)} collective-permute-done((f32[5,32,32]{2,1,0:T(8,128)S(1)}, f32[5,32,32]{2,1,0:T(8,128)S(1)}, u32[]{:S(2)}, u32[]{:S(2)}) %collective-permute-start.17) | collective-permute-done | bytes 20512 | tf_op jit(solution)/shard_map/ppermute | solution.py:99
  101.0 2.8 %collective-permute-done.16 = f32[5,32,32]{2,1,0:T(8,128)S(1)} collective-permute-done((f32[5,32,32]{2,1,0:T(8,128)S(1)}, f32[5,32,32]{2,1,0:T(8,128)S(1)}, u32[]{:S(2)}, u32[]{:S(2)}) %collective-permute-start.16) | collective-permute-done | bytes 20512 | tf_op jit(solution)/shard_map/ppermute | solution.py:99
  103.8 0.7 add_add_fusion.totals_ref
  104.5 4.8 %shard_map.38 = f32[5,32,32]{2,1,0:T(8,128)} custom-call(f32[5,32,32]{2,1,0:T(8,128)} %add_add_fusion.totals_ref), custom_call_target="tpu_custom_call" | custom-call | tf_op jit(solution)/shard_map/pallas_call | solution.py:80
  109.3 2.1 %fusion.27 = f32[5,32,2048]{2,1,0:T(8,128)S(1)} fusion(f32[5,32,32]{2,1,0:T(8,128)} %shard_map.38, f32[5,32,2048]{2,1,0:T(8,128)S(1)} %fusion.25), kind=kOutput, calls=%fused_computation.45 | convolution fusion | flops 125829120 | bytes 2641920 | tf_op jit(solution)/shard_map/kij,kjp->kip/dot_general | solution.py:90
  111.4 2.2 %reshape.140 = f32[5,32,2,1024]{3,2,1,0:T(2,128)} reshape(f32[5,32,2048]{2,1,0:T(8,128)S(1)} %fusion.27) | data formatting | bytes 2621440 | tf_op jit(solution)/shard_map/reshape | solution.py:126
  (13 shorter events, 0.5 us)
Async XLA Ops:
  35.9 11.9 %collective-permute-start.2 = (f32[5,32,32]{2,1,0:T(8,128)S(1)}, f32[5,32,32]{2,1,0:T(8,128)S(1)}, u32[]{:S(2)}, u32[]{:S(2)}) collective-permute-start(f32[5,32,32]{2,1,0:T(8,128)S(1)} %fusion.24), channel_id=1, source_target_pairs={{0,48},{4,52},{8,56},{12,60},{16,32},{20,36},{24,40},{28,44},{32,1... | collective-permute-start | bytes 61448 | tf_op jit(solution)/shard_map/ppermute | solution.py:99
  42.3 10.0 %collective-permute-start.1 = (f32[5,32,32]{2,1,0:T(8,128)S(1)}, f32[5,32,32]{2,1,0:T(8,128)S(1)}, u32[]{:S(2)}, u32[]{:S(2)}) collective-permute-start(f32[5,32,32]{2,1,0:T(8,128)S(1)} %fusion.24), channel_id=1, source_target_pairs={{0,32},{4,36},{8,40},{12,44},{16,48},{20,52},{24,56},{28,60},{32,0... | collective-permute-start | bytes 61448 | tf_op jit(solution)/shard_map/ppermute | solution.py:99
  43.3 9.0 %collective-permute-start = (f32[5,32,32]{2,1,0:T(8,128)S(1)}, f32[5,32,32]{2,1,0:T(8,128)S(1)}, u32[]{:S(2)}, u32[]{:S(2)}) collective-permute-start(f32[5,32,32]{2,1,0:T(8,128)S(1)} %fusion.24), channel_id=1, source_target_pairs={{0,16},{4,20},{8,24},{12,28},{16,0},{20,4},{24,8},{28,12},{32,48},... | collective-permute-start | bytes 61448 | tf_op jit(solution)/shard_map/ppermute | solution.py:99
  52.3 4.2 %collective-permute-start.5 = (f32[5,32,32]{2,1,0:T(8,128)S(1)}, f32[5,32,32]{2,1,0:T(8,128)S(1)}, u32[]{:S(2)}, u32[]{:S(2)}) collective-permute-start(f32[5,32,32]{2,1,0:T(8,128)S(1)} %add_add_fusion.5), channel_id=1, source_target_pairs={{0,12},{4,8},{8,4},{12,0},{16,28},{20,24},{24,20},{28,16},{32,44},... | collective-permute-start | bytes 61448 | tf_op jit(solution)/shard_map/ppermute | solution.py:99
  52.4 5.4 %collective-permute-start.4 = (f32[5,32,32]{2,1,0:T(8,128)S(1)}, f32[5,32,32]{2,1,0:T(8,128)S(1)}, u32[]{:S(2)}, u32[]{:S(2)}) collective-permute-start(f32[5,32,32]{2,1,0:T(8,128)S(1)} %add_add_fusion.5), channel_id=1, source_target_pairs={{0,8},{4,12},{8,0},{12,4},{16,24},{20,28},{24,16},{28,20},{32,40},... | collective-permute-start | bytes 61448 | tf_op jit(solution)/shard_map/ppermute | solution.py:99
  52.8 5.0 %collective-permute-start.3 = (f32[5,32,32]{2,1,0:T(8,128)S(1)}, f32[5,32,32]{2,1,0:T(8,128)S(1)}, u32[]{:S(2)}, u32[]{:S(2)}) collective-permute-start(f32[5,32,32]{2,1,0:T(8,128)S(1)} %add_add_fusion.5), channel_id=1, source_target_pairs={{0,4},{4,0},{8,12},{12,8},{16,20},{20,16},{24,28},{28,24},{32,36},... | collective-permute-start | bytes 61448 | tf_op jit(solution)/shard_map/ppermute | solution.py:99
  57.8 6.6 %collective-permute-start.8 = (f32[5,32,32]{2,1,0:T(8,128)S(1)}, f32[5,32,32]{2,1,0:T(8,128)S(1)}, u32[]{:S(2)}, u32[]{:S(2)}) collective-permute-start(f32[5,32,32]{2,1,0:T(8,128)S(1)} %add_add_fusion.4), channel_id=1, source_target_pairs={{0,192},{4,196},{8,200},{12,204},{16,208},{20,212},{24,216},{28,22... | collective-permute-start | bytes 61448 | tf_op jit(solution)/shard_map/ppermute | solution.py:99
  60.7 6.6 %collective-permute-start.7 = (f32[5,32,32]{2,1,0:T(8,128)S(1)}, f32[5,32,32]{2,1,0:T(8,128)S(1)}, u32[]{:S(2)}, u32[]{:S(2)}) collective-permute-start(f32[5,32,32]{2,1,0:T(8,128)S(1)} %add_add_fusion.4), channel_id=1, source_target_pairs={{0,128},{4,132},{8,136},{12,140},{16,144},{20,148},{24,152},{28,15... | collective-permute-start | bytes 61448 | tf_op jit(solution)/shard_map/ppermute | solution.py:99
  61.5 5.8 %collective-permute-start.6 = (f32[5,32,32]{2,1,0:T(8,128)S(1)}, f32[5,32,32]{2,1,0:T(8,128)S(1)}, u32[]{:S(2)}, u32[]{:S(2)}) collective-permute-start(f32[5,32,32]{2,1,0:T(8,128)S(1)} %add_add_fusion.4), channel_id=1, source_target_pairs={{0,64},{4,68},{8,72},{12,76},{16,80},{20,84},{24,88},{28,92},{32,9... | collective-permute-start | bytes 61448 | tf_op jit(solution)/shard_map/ppermute | solution.py:99
  76.2 6.7 %collective-permute-start.11 = (f32[5,32,32]{2,1,0:T(8,128)S(1)}, f32[5,32,32]{2,1,0:T(8,128)S(1)}, u32[]{:S(2)}, u32[]{:S(2)}) collective-permute-start(f32[5,32,32]{2,1,0:T(8,128)S(1)} %fusion.26), channel_id=1, source_target_pairs={{0,48},{4,52},{8,56},{12,60},{16,32},{20,36},{24,40},{28,44},{32,1... | collective-permute-start | bytes 61448 | tf_op jit(solution)/shard_map/ppermute | solution.py:99
  79.0 8.8 %collective-permute-start.10 = (f32[5,32,32]{2,1,0:T(8,128)S(1)}, f32[5,32,32]{2,1,0:T(8,128)S(1)}, u32[]{:S(2)}, u32[]{:S(2)}) collective-permute-start(f32[5,32,32]{2,1,0:T(8,128)S(1)} %fusion.26), channel_id=1, source_target_pairs={{0,32},{4,36},{8,40},{12,44},{16,48},{20,52},{24,56},{28,60},{32,0... | collective-permute-start | bytes 61448 | tf_op jit(solution)/shard_map/ppermute | solution.py:99
  81.1 7.7 %collective-permute-start.9 = (f32[5,32,32]{2,1,0:T(8,128)S(1)}, f32[5,32,32]{2,1,0:T(8,128)S(1)}, u32[]{:S(2)}, u32[]{:S(2)}) collective-permute-start(f32[5,32,32]{2,1,0:T(8,128)S(1)} %fusion.26), channel_id=1, source_target_pairs={{0,16},{4,20},{8,24},{12,28},{16,0},{20,4},{24,8},{28,12},{32,48},... | collective-permute-start | bytes 61448 | tf_op jit(solution)/shard_map/ppermute | solution.py:99
  88.8 4.2 %collective-permute-start.14 = (f32[5,32,32]{2,1,0:T(8,128)S(1)}, f32[5,32,32]{2,1,0:T(8,128)S(1)}, u32[]{:S(2)}, u32[]{:S(2)}) collective-permute-start(f32[5,32,32]{2,1,0:T(8,128)S(1)} %add_add_fusion.2), channel_id=1, source_target_pairs={{0,12},{4,8},{8,4},{12,0},{16,28},{20,24},{24,20},{28,16},{32,44},... | collective-permute-start | bytes 61448 | tf_op jit(solution)/shard_map/ppermute | solution.py:99
  88.9 5.4 %collective-permute-start.13 = (f32[5,32,32]{2,1,0:T(8,128)S(1)}, f32[5,32,32]{2,1,0:T(8,128)S(1)}, u32[]{:S(2)}, u32[]{:S(2)}) collective-permute-start(f32[5,32,32]{2,1,0:T(8,128)S(1)} %add_add_fusion.2), channel_id=1, source_target_pairs={{0,8},{4,12},{8,0},{12,4},{16,24},{20,28},{24,16},{28,20},{32,40},... | collective-permute-start | bytes 61448 | tf_op jit(solution)/shard_map/ppermute | solution.py:99
  89.4 4.8 %collective-permute-start.12 = (f32[5,32,32]{2,1,0:T(8,128)S(1)}, f32[5,32,32]{2,1,0:T(8,128)S(1)}, u32[]{:S(2)}, u32[]{:S(2)}) collective-permute-start(f32[5,32,32]{2,1,0:T(8,128)S(1)} %add_add_fusion.2), channel_id=1, source_target_pairs={{0,4},{4,0},{8,12},{12,8},{16,20},{20,16},{24,28},{28,24},{32,36},... | collective-permute-start | bytes 61448 | tf_op jit(solution)/shard_map/ppermute | solution.py:99
  94.3 6.8 %collective-permute-start.17 = (f32[5,32,32]{2,1,0:T(8,128)S(1)}, f32[5,32,32]{2,1,0:T(8,128)S(1)}, u32[]{:S(2)}, u32[]{:S(2)}) collective-permute-start(f32[5,32,32]{2,1,0:T(8,128)S(1)} %add_add_fusion.1), channel_id=1, source_target_pairs={{0,192},{4,196},{8,200},{12,204},{16,208},{20,212},{24,216},{28,22... | collective-permute-start | bytes 61448 | tf_op jit(solution)/shard_map/ppermute | solution.py:99
  97.2 6.6 %collective-permute-start.16 = (f32[5,32,32]{2,1,0:T(8,128)S(1)}, f32[5,32,32]{2,1,0:T(8,128)S(1)}, u32[]{:S(2)}, u32[]{:S(2)}) collective-permute-start(f32[5,32,32]{2,1,0:T(8,128)S(1)} %add_add_fusion.1), channel_id=1, source_target_pairs={{0,128},{4,132},{8,136},{12,140},{16,144},{20,148},{24,152},{28,15... | collective-permute-start | bytes 61448 | tf_op jit(solution)/shard_map/ppermute | solution.py:99
  97.7 6.1 %collective-permute-start.15 = (f32[5,32,32]{2,1,0:T(8,128)S(1)}, f32[5,32,32]{2,1,0:T(8,128)S(1)}, u32[]{:S(2)}, u32[]{:S(2)}) collective-permute-start(f32[5,32,32]{2,1,0:T(8,128)S(1)} %add_add_fusion.1), channel_id=1, source_target_pairs={{0,64},{4,68},{8,72},{12,76},{16,80},{20,84},{24,88},{28,92},{32,9... | collective-permute-start | bytes 61448 | tf_op jit(solution)/shard_map/ppermute | solution.py:99

commit v5 on v4

--- a/solution.py
+++ b/solution.py
@@ -35,21 +35,23 @@
     return jnp.einsum("fbcs,sp->fbcp", placed, snapshots, precision=lax.Precision.HIGHEST)
 
 
-def slot_selector(owner, slot_count):
+def slot_sources(owner, slot_count):
     freq_ids = jnp.arange(owner.shape[0], dtype=jnp.int32)
     before = (owner[None, :] == owner[:, None]) & (freq_ids[None, :] < freq_ids[:, None])
     rank_in = jnp.sum(before.astype(jnp.int32), axis=1)
     slot_of = owner * FCAP + rank_in
-    targets = jnp.arange(slot_count, dtype=jnp.int32)
-    return (slot_of[None, :] == targets[:, None]).astype(jnp.float32)
+    hits = slot_of[None, :] == jnp.arange(slot_count, dtype=jnp.int32)[:, None]
+    chosen = jnp.sum(jnp.where(hits, freq_ids[None, :], 0), axis=1)
+    return chosen, jnp.any(hits, axis=1)
 
 
 def partial_gram(matrices):
     return jnp.einsum("kip,kjp->kij", matrices, matrices, precision=lax.Precision.HIGHEST)
 
 
-def _inverse_factor_kernel(totals_ref, out_ref, *, rows_total):
-    gram = totals_ref[...] / rows_total
+def _inverse_factor_kernel(own_ref, first_ref, second_ref, third_ref, out_ref, *, rows_total):
+    totals = (own_ref[...] + first_ref[...]) + (second_ref[...] + third_ref[...])
+    gram = totals / rows_total
     batch, size, _ = gram.shape
     row = lax.broadcasted_iota(jnp.int32, gram.shape, 1)
     col = lax.broadcasted_iota(jnp.int32, gram.shape, 2)
@@ -76,31 +78,31 @@
     out_ref[...] = elim / jnp.sqrt(pivots)
 
 
-def inverse_factor(totals, rows_total):
+def inverse_factor(leaves, rows_total):
     return pl.pallas_call(
         functools.partial(_inverse_factor_kernel, rows_total=rows_total),
-        out_shape=jax.ShapeDtypeStruct(totals.shape, jnp.float32),
-        in_specs=[pl.BlockSpec(memory_space=pltpu.VMEM)],
+        out_shape=jax.ShapeDtypeStruct(leaves[0].shape, jnp.float32),
+        in_specs=[pl.BlockSpec(memory_space=pltpu.VMEM)] * 4,
         out_specs=pl.BlockSpec(memory_space=pltpu.VMEM),
-    )(totals)
+    )(*leaves)
 
 
-def finish_pass(matrices, totals, rows_total):
-    inverse = inverse_factor(totals, rows_total)
+def finish_pass(matrices, leaves, rows_total):
+    inverse = inverse_factor(leaves, rows_total)
     return jnp.einsum("kij,kjp->kip", inverse, matrices, precision=lax.Precision.HIGHEST)
 
 
 def reduce_space(values):
     count = lax.axis_size("space")
-    for masks in [[4, 8, 12], [1, 2, 3], [16, 32, 48]]:
+    rounds = [[4, 8, 12], [1, 2, 3], [16, 32, 48]]
+    for number, masks in enumerate(rounds):
         leaves = [values]
         for mask in masks:
             pairs = [(index, index ^ mask) for index in range(count)]
             leaves.append(lax.ppermute(values, "space", pairs))
-        while len(leaves) > 1:
-            leaves = [leaves[i] + leaves[i + 1] for i in range(0, len(leaves), 2)]
-        values = leaves[0]
-    return values
+        if number == len(rounds) - 1:
+            return leaves
+        values = (leaves[0] + leaves[1]) + (leaves[2] + leaves[3])
 
 
 def local(snapshots, block_starts, owner):
@@ -113,16 +115,16 @@
     column_count = block_count * tm_count
     offset = lax.axis_index("tm") * samples
     spectra = windowed_spectra(snapshots, block_starts - offset)
-    selector = slot_selector(owner, tm_count * FCAP)
-    outgoing = jnp.einsum("lf,fbcp->lbcp", selector, spectra, precision=lax.Precision.HIGHEST)
+    chosen, filled = slot_sources(owner, tm_count * FCAP)
+    outgoing = jnp.where(filled[:, None, None, None], jnp.take(spectra, chosen, axis=0), 0.0)
     outgoing = outgoing.reshape(tm_count, FCAP, block_count, 2, points)
     received = lax.all_to_all(outgoing, "tm", split_axis=0, concat_axis=2, tiled=True)
     count = received.shape[1]
     matrices = received[0].reshape(count, column_count, 2 * points)
     for turn in range(2):
         partial_sums = partial_gram(matrices)
-        totals = reduce_space(partial_sums)
-        matrices = finish_pass(matrices, totals, rows_total)
+        leaves = reduce_space(partial_sums)
+        matrices = finish_pass(matrices, leaves, rows_total)
     return matrices.reshape(count, column_count, 2, points)
 
 

time: 114 us -> 113 us (level)
  local copies, waits for them, and re-layouts: 3.07 us -> 5.59 us
  matrix products: 14.4 us -> 12.2 us
  other arithmetic: 6.36 us -> 4.31 us
    unnamed x0 -> x16, local copies, waits for them, and re-layouts: none -> 2.48 us
    dot_general x1, matrix products: 6.68 us -> 5.33 us  [windowed_spectra(): jnp.einsum('fbcs,sp->fbcp', placed, snapshots, precision=lax.Precision.HI...]
    add x7 -> x5, other arithmetic: 2.08 us -> 0.76 us  [the longest x1 0.66 us: slot_sources(): slot_of = owner * FCAP + rank_in]
    mul x1, other arithmetic: 2.34 us -> 1.18 us  [windowed_spectra(): window * jnp.cos(angle)]
where the time goes in v5:
time: 113 us; the launch traced here: 112 us
  waiting for transfers between devices  31.4 us (28%)
  starting transfers between devices  27.7 us (25%)
  blocking collectives  21.2 us (19%)
  matrix products  12.2 us (11%)
  Pallas kernels  9.9 us (9%)
  local copies, waits for them, and re-layouts  5.59 us (5%)
  other arithmetic  4.31 us (4%)
    ppermute x18, waiting for transfers between devices, reduce_space(): leaves.append(lax.ppermute(values, 'space', pairs))  31.4 us
    ppermute x18, starting transfers between devices, reduce_space(): leaves.append(lax.ppermute(values, 'space', pairs))  27.7 us
    all_to_all x1, blocking collectives, local(): lax.all_to_all(outgoing, 'tm', split_axis=0, concat_axis=2, tiled=True)  21.2 us
    pallas_call x2, Pallas kernels, inverse_factor(): pl.pallas_call(functools.partial(_inverse_factor_kernel, rows_total=rows_...  9.9 us
    dot_general x1, matrix products, windowed_spectra(): jnp.einsum('fbcs,sp->fbcp', placed, snapshots, precision=lax.Precision.HI...  5.33 us
    dot_general x2, matrix products, finish_pass(): jnp.einsum('kij,kjp->kip', inverse, matrices, precision=lax.Precision.HIG...  4.24 us
    dot_general x2, matrix products, partial_gram(): jnp.einsum('kip,kjp->kij', matrices, matrices, precision=lax.Precision.HI...  2.6 us
    unnamed x16, local copies, waits for them, and re-layouts  2.48 us
  transfers between devices with their start and end apart: 18, of which 13 were waited for; matrix products, arithmetic and copies ran while one was open for 0% of the time, Pallas kernels for 0%

profile of v5, /device:TPU:8, one launch (start us, length us, event | category | flops | bytes accessed | tf_op | source)
XLA Modules:
  0.0 112.3 jit_solution(5967160634596127894)
XLA Ops:
  0.0 0.9 convert_reduce_fusion
  0.9 0.7 multiply_add_fusion
  1.8 0.7 broadcast_subtract_fusion
  2.7 0.2 multiply_subtract_fusion
  3.0 1.2 %cosine_multiply_fusion = (f32[9,8,1,1152]{3,1,2,0:T(8,128)S(1)}, f32[9,8,1,1152]{3,1,2,0:T(8,128)S(1)}) fusion(s32[8,1152]{1,0:T(8,128)S(1)} %fusion.12, f32[8,1152]{1,0:T(8,128)S(1)} %get-tuple-element.7, f32[8,1152]{1,0:T(8,128)S(1)} %get-tuple-element.8), kind=kLoop, calls=%fused_computation.15 | loop fusion | flops 1327104 | bytes 774144 | tf_op jit(solution)/shard_map/mul | solution.py:33
  4.2 5.3 %fusion = f32[9,8,2,1024]{3,1,2,0:T(8,128)S(1)} fusion(f32[1152,1024]{1,0:T(8,128)} %param.3, f32[9,8,1,1152]{3,1,2,0:T(8,128)S(1)} %get-tuple-element.6, f32[9,8,1,1152]{3,1,2,0:T(8,128)S(1)} %get-tuple-element.5, pred[8,1152]{1,0:T(8,128)(4,1)S(1)} %fusion.15), kind=kOutput, calls=%fused_computation.1 | convolution fusion | flops 2038763520 | bytes 5981184 | tf_op jit(solution)/shard_map/fbcs,sp->fbcp/dot_general | solution.py:35
  9.5 0.6 gather_fusion
  10.2 0.2 select_select_fusion
  10.4 21.2 %all_to_all.15 = f32[4,5,8,2,1024]{4,2,3,1,0:T(8,128)S(1)} all-to-all(f32[4,5,8,2,1024]{4,2,3,1,0:T(8,128)S(1)} %select_select_fusion), channel_id=1, replica_groups=mesh['space'=64,'tm'=4] {'tm'}, dimensions={0} | all-to-all | bytes 2621440 | tf_op jit(solution)/shard_map/all_to_all | solution.py:121
  31.7 1.3 %fusion.22 = f32[5,32,32]{2,1,0:T(8,128)S(1)} fusion(f32[5,32,2048]{2,1,0:T(8,128)S(1)} %bitcast.22), kind=kOutput, calls=%fused_computation.46 | convolution fusion | flops 125829120 | bytes 1331200 | tf_op jit(solution)/shard_map/kip,kjp->kij/dot_general | solution.py:49
  33.0 6.4 %collective-permute-start.2 = (f32[5,32,32]{2,1,0:T(8,128)S(1)}, f32[5,32,32]{2,1,0:T(8,128)S(1)}, u32[]{:S(2)}, u32[]{:S(2)}) collective-permute-start(f32[5,32,32]{2,1,0:T(8,128)S(1)} %fusion.22), channel_id=1, source_target_pairs={{0,48},{4,52},{8,56},{12,60},{16,32},{20,36},{24,40},{28,44},{32,1... | collective-permute-start | bytes 61448 | tf_op jit(solution)/shard_map/ppermute | solution.py:102
  39.4 1.0 collective-permute-start.1
  40.4 1.5 %collective-permute-start = (f32[5,32,32]{2,1,0:T(8,128)S(1)}, f32[5,32,32]{2,1,0:T(8,128)S(1)}, u32[]{:S(2)}, u32[]{:S(2)}) collective-permute-start(f32[5,32,32]{2,1,0:T(8,128)S(1)} %fusion.22), channel_id=1, source_target_pairs={{0,16},{4,20},{8,24},{12,28},{16,0},{20,4},{24,8},{28,12},{32,48},... | collective-permute-start | bytes 61448 | tf_op jit(solution)/shard_map/ppermute | solution.py:102
  41.8 3.1 %collective-permute-done.2 = f32[5,32,32]{2,1,0:T(8,128)S(1)} collective-permute-done((f32[5,32,32]{2,1,0:T(8,128)S(1)}, f32[5,32,32]{2,1,0:T(8,128)S(1)}, u32[]{:S(2)}, u32[]{:S(2)}) %collective-permute-start.2) | collective-permute-done | bytes 20512 | tf_op jit(solution)/shard_map/ppermute | solution.py:102
  44.9 4.5 %collective-permute-done.1 = f32[5,32,32]{2,1,0:T(8,128)S(1)} collective-permute-done((f32[5,32,32]{2,1,0:T(8,128)S(1)}, f32[5,32,32]{2,1,0:T(8,128)S(1)}, u32[]{:S(2)}, u32[]{:S(2)}) %collective-permute-start.1) | collective-permute-done | bytes 20512 | tf_op jit(solution)/shard_map/ppermute | solution.py:102
  49.5 0.4 collective-permute-start.4
  49.9 1.5 %collective-permute-start.3 = (f32[5,32,32]{2,1,0:T(8,128)S(1)}, f32[5,32,32]{2,1,0:T(8,128)S(1)}, u32[]{:S(2)}, u32[]{:S(2)}) collective-permute-start(f32[5,32,32]{2,1,0:T(8,128)S(1)} %add_add_fusion.3), channel_id=1, source_target_pairs={{0,4},{4,0},{8,12},{12,8},{16,20},{20,16},{24,28},{28,24},{32,36},... | collective-permute-start | bytes 61448 | tf_op jit(solution)/shard_map/ppermute | solution.py:102
  51.4 2.3 %collective-permute-done.5 = f32[5,32,32]{2,1,0:T(8,128)S(1)} collective-permute-done((f32[5,32,32]{2,1,0:T(8,128)S(1)}, f32[5,32,32]{2,1,0:T(8,128)S(1)}, u32[]{:S(2)}, u32[]{:S(2)}) %collective-permute-start.5) | collective-permute-done | bytes 20512 | tf_op jit(solution)/shard_map/ppermute | solution.py:102
  53.6 1.3 %collective-permute-done.4 = f32[5,32,32]{2,1,0:T(8,128)S(1)} collective-permute-done((f32[5,32,32]{2,1,0:T(8,128)S(1)}, f32[5,32,32]{2,1,0:T(8,128)S(1)}, u32[]{:S(2)}, u32[]{:S(2)}) %collective-permute-start.4) | collective-permute-done | bytes 20512 | tf_op jit(solution)/shard_map/ppermute | solution.py:102
  54.9 2.8 %collective-permute-start.8 = (f32[5,32,32]{2,1,0:T(8,128)S(1)}, f32[5,32,32]{2,1,0:T(8,128)S(1)}, u32[]{:S(2)}, u32[]{:S(2)}) collective-permute-start(f32[5,32,32]{2,1,0:T(8,128)S(1)} %add_add_fusion.2.own_ref), channel_id=1, source_target_pairs={{0,192},{4,196},{8,200},{12,204},{16,208},{20,212},{24,216},{28,22... | collective-permute-start | bytes 61448 | tf_op jit(solution)/shard_map/ppermute | solution.py:102
  57.7 0.8 collective-permute-start.7
  58.6 0.5 collective-permute-start.6
  59.1 2.4 %collective-permute-done.8.third_ref = f32[5,32,32]{2,1,0:T(8,128)S(1)} collective-permute-done((f32[5,32,32]{2,1,0:T(8,128)S(1)}, f32[5,32,32]{2,1,0:T(8,128)S(1)}, u32[]{:S(2)}, u32[]{:S(2)}) %collective-permute-start.8) | collective-permute-done | bytes 20512 | tf_op jit(solution)/shard_map/ppermute | solution.py:102
  61.5 2.8 %collective-permute-done.7.second_ref = f32[5,32,32]{2,1,0:T(8,128)S(1)} collective-permute-done((f32[5,32,32]{2,1,0:T(8,128)S(1)}, f32[5,32,32]{2,1,0:T(8,128)S(1)}, u32[]{:S(2)}, u32[]{:S(2)}) %collective-permute-start.7) | collective-permute-done | bytes 20512 | tf_op jit(solution)/shard_map/ppermute | solution.py:102
  64.3 0.6 copy-done.4
  64.9 0.6 copy-done.6
  65.5 5.0 %shard_map.37 = f32[5,32,32]{2,1,0:T(8,128)} custom-call(f32[5,32,32]{2,1,0:T(8,128)} %copy-done, f32[5,32,32]{2,1,0:T(8,128)} %copy-done.6, f32[5,32,32]{2,1,0:T(8,128)} %copy-done.4, f32[5,32,32]{2,1,0:T(8,128)} %copy-done.2), custom_call_target="tpu_custom_call" | custom-call | tf_op jit(solution)/shard_map/pallas_call | solution.py:82
  70.5 2.1 %fusion.23 = f32[5,32,2048]{2,1,0:T(8,128)S(1)} fusion(f32[5,32,32]{2,1,0:T(8,128)} %shard_map.37, f32[5,32,2048]{2,1,0:T(8,128)S(1)} %bitcast.23), kind=kOutput, calls=%fused_computation.47 | convolution fusion | flops 125829120 | bytes 2641920 | tf_op jit(solution)/shard_map/kij,kjp->kip/dot_general | solution.py:92
  72.6 1.3 %fusion.24 = f32[5,32,32]{2,1,0:T(8,128)S(1)} fusion(f32[5,32,2048]{2,1,0:T(8,128)S(1)} %fusion.23), kind=kOutput, calls=%fused_computation.48 | convolution fusion | flops 125829120 | bytes 1331200 | tf_op jit(solution)/shard_map/kip,kjp->kij/dot_general | solution.py:49
  73.9 2.8 %collective-permute-start.11 = (f32[5,32,32]{2,1,0:T(8,128)S(1)}, f32[5,32,32]{2,1,0:T(8,128)S(1)}, u32[]{:S(2)}, u32[]{:S(2)}) collective-permute-start(f32[5,32,32]{2,1,0:T(8,128)S(1)} %fusion.24), channel_id=1, source_target_pairs={{0,48},{4,52},{8,56},{12,60},{16,32},{20,36},{24,40},{28,44},{32,1... | collective-permute-start | bytes 61448 | tf_op jit(solution)/shard_map/ppermute | solution.py:102
  76.8 2.1 %collective-permute-start.10 = (f32[5,32,32]{2,1,0:T(8,128)S(1)}, f32[5,32,32]{2,1,0:T(8,128)S(1)}, u32[]{:S(2)}, u32[]{:S(2)}) collective-permute-start(f32[5,32,32]{2,1,0:T(8,128)S(1)} %fusion.24), channel_id=1, source_target_pairs={{0,32},{4,36},{8,40},{12,44},{16,48},{20,52},{24,56},{28,60},{32,0... | collective-permute-start | bytes 61448 | tf_op jit(solution)/shard_map/ppermute | solution.py:102
  78.9 1.6 %collective-permute-start.9 = (f32[5,32,32]{2,1,0:T(8,128)S(1)}, f32[5,32,32]{2,1,0:T(8,128)S(1)}, u32[]{:S(2)}, u32[]{:S(2)}) collective-permute-start(f32[5,32,32]{2,1,0:T(8,128)S(1)} %fusion.24), channel_id=1, source_target_pairs={{0,16},{4,20},{8,24},{12,28},{16,0},{20,4},{24,8},{28,12},{32,48},... | collective-permute-start | bytes 61448 | tf_op jit(solution)/shard_map/ppermute | solution.py:102
  80.6 5.0 %collective-permute-done.10 = f32[5,32,32]{2,1,0:T(8,128)S(1)} collective-permute-done((f32[5,32,32]{2,1,0:T(8,128)S(1)}, f32[5,32,32]{2,1,0:T(8,128)S(1)}, u32[]{:S(2)}, u32[]{:S(2)}) %collective-permute-start.10) | collective-permute-done | bytes 20512 | tf_op jit(solution)/shard_map/ppermute | solution.py:102
  85.6 0.8 collective-permute-done.9
  86.5 1.3 %collective-permute-start.13 = (f32[5,32,32]{2,1,0:T(8,128)S(1)}, f32[5,32,32]{2,1,0:T(8,128)S(1)}, u32[]{:S(2)}, u32[]{:S(2)}) collective-permute-start(f32[5,32,32]{2,1,0:T(8,128)S(1)} %add_add_fusion.1), channel_id=1, source_target_pairs={{0,8},{4,12},{8,0},{12,4},{16,24},{20,28},{24,16},{28,20},{32,40},... | collective-permute-start | bytes 61448 | tf_op jit(solution)/shard_map/ppermute | solution.py:102
  87.9 0.5 collective-permute-start.12
  88.4 2.9 %collective-permute-done.14 = f32[5,32,32]{2,1,0:T(8,128)S(1)} collective-permute-done((f32[5,32,32]{2,1,0:T(8,128)S(1)}, f32[5,32,32]{2,1,0:T(8,128)S(1)}, u32[]{:S(2)}, u32[]{:S(2)}) %collective-permute-start.14) | collective-permute-done | bytes 20512 | tf_op jit(solution)/shard_map/ppermute | solution.py:102
  91.3 1.4 %collective-permute-done.13 = f32[5,32,32]{2,1,0:T(8,128)S(1)} collective-permute-done((f32[5,32,32]{2,1,0:T(8,128)S(1)}, f32[5,32,32]{2,1,0:T(8,128)S(1)}, u32[]{:S(2)}, u32[]{:S(2)}) %collective-permute-start.13) | collective-permute-done | bytes 20512 | tf_op jit(solution)/shard_map/ppermute | solution.py:102
  92.7 2.6 %collective-permute-start.17 = (f32[5,32,32]{2,1,0:T(8,128)S(1)}, f32[5,32,32]{2,1,0:T(8,128)S(1)}, u32[]{:S(2)}, u32[]{:S(2)}) collective-permute-start(f32[5,32,32]{2,1,0:T(8,128)S(1)} %add_add_fusion.own_ref), channel_id=1, source_target_pairs={{0,192},{4,196},{8,200},{12,204},{16,208},{20,212},{24,216},{28,22... | collective-permute-start | bytes 61448 | tf_op jit(solution)/shard_map/ppermute | solution.py:102
  95.3 0.2 collective-permute-start.16
  95.5 1.4 %collective-permute-start.15 = (f32[5,32,32]{2,1,0:T(8,128)S(1)}, f32[5,32,32]{2,1,0:T(8,128)S(1)}, u32[]{:S(2)}, u32[]{:S(2)}) collective-permute-start(f32[5,32,32]{2,1,0:T(8,128)S(1)} %add_add_fusion.own_ref), channel_id=1, source_target_pairs={{0,64},{4,68},{8,72},{12,76},{16,80},{20,84},{24,88},{28,92},{32,9... | collective-permute-start | bytes 61448 | tf_op jit(solution)/shard_map/ppermute | solution.py:102
  96.9 1.8 %collective-permute-done.17.third_ref = f32[5,32,32]{2,1,0:T(8,128)S(1)} collective-permute-done((f32[5,32,32]{2,1,0:T(8,128)S(1)}, f32[5,32,32]{2,1,0:T(8,128)S(1)}, u32[]{:S(2)}, u32[]{:S(2)}) %collective-permute-start.17) | collective-permute-done | bytes 20512 | tf_op jit(solution)/shard_map/ppermute | solution.py:102
  98.7 3.1 %collective-permute-done.16.second_ref = f32[5,32,32]{2,1,0:T(8,128)S(1)} collective-permute-done((f32[5,32,32]{2,1,0:T(8,128)S(1)}, f32[5,32,32]{2,1,0:T(8,128)S(1)}, u32[]{:S(2)}, u32[]{:S(2)}) %collective-permute-start.16) | collective-permute-done | bytes 20512 | tf_op jit(solution)/shard_map/ppermute | solution.py:102
  101.9 0.6 copy-done.5
  102.5 0.6 copy-done.7
  103.1 5.0 %shard_map.38 = f32[5,32,32]{2,1,0:T(8,128)} custom-call(f32[5,32,32]{2,1,0:T(8,128)} %copy-done.1, f32[5,32,32]{2,1,0:T(8,128)} %copy-done.7, f32[5,32,32]{2,1,0:T(8,128)} %copy-done.5, f32[5,32,32]{2,1,0:T(8,128)} %copy-done.3), custom_call_target="tpu_custom_call" | custom-call | tf_op jit(solution)/shard_map/pallas_call | solution.py:82
  108.0 2.1 %fusion.25 = f32[5,32,2048]{2,1,0:T(8,128)S(1)} fusion(f32[5,32,32]{2,1,0:T(8,128)} %shard_map.38, f32[5,32,2048]{2,1,0:T(8,128)S(1)} %fusion.23), kind=kOutput, calls=%fused_computation.49 | convolution fusion | flops 125829120 | bytes 2641920 | tf_op jit(solution)/shard_map/kij,kjp->kip/dot_general | solution.py:92
  110.2 2.2 %reshape.161 = f32[5,32,2,1024]{3,2,1,0:T(2,128)} reshape(f32[5,32,2048]{2,1,0:T(8,128)S(1)} %fusion.25) | data formatting | bytes 2621440 | tf_op jit(solution)/shard_map/reshape | solution.py:128
  (34 shorter events, 1.1 us)
Async XLA Ops:
  33.0 11.9 %collective-permute-start.2 = (f32[5,32,32]{2,1,0:T(8,128)S(1)}, f32[5,32,32]{2,1,0:T(8,128)S(1)}, u32[]{:S(2)}, u32[]{:S(2)}) collective-permute-start(f32[5,32,32]{2,1,0:T(8,128)S(1)} %fusion.22), channel_id=1, source_target_pairs={{0,48},{4,52},{8,56},{12,60},{16,32},{20,36},{24,40},{28,44},{32,1... | collective-permute-start | bytes 61448 | tf_op jit(solution)/shard_map/ppermute | solution.py:102
  39.4 10.0 %collective-permute-start.1 = (f32[5,32,32]{2,1,0:T(8,128)S(1)}, f32[5,32,32]{2,1,0:T(8,128)S(1)}, u32[]{:S(2)}, u32[]{:S(2)}) collective-permute-start(f32[5,32,32]{2,1,0:T(8,128)S(1)} %fusion.22), channel_id=1, source_target_pairs={{0,32},{4,36},{8,40},{12,44},{16,48},{20,52},{24,56},{28,60},{32,0... | collective-permute-start | bytes 61448 | tf_op jit(solution)/shard_map/ppermute | solution.py:102
  40.4 9.0 %collective-permute-start = (f32[5,32,32]{2,1,0:T(8,128)S(1)}, f32[5,32,32]{2,1,0:T(8,128)S(1)}, u32[]{:S(2)}, u32[]{:S(2)}) collective-permute-start(f32[5,32,32]{2,1,0:T(8,128)S(1)} %fusion.22), channel_id=1, source_target_pairs={{0,16},{4,20},{8,24},{12,28},{16,0},{20,4},{24,8},{28,12},{32,48},... | collective-permute-start | bytes 61448 | tf_op jit(solution)/shard_map/ppermute | solution.py:102
  49.4 4.2 %collective-permute-start.5 = (f32[5,32,32]{2,1,0:T(8,128)S(1)}, f32[5,32,32]{2,1,0:T(8,128)S(1)}, u32[]{:S(2)}, u32[]{:S(2)}) collective-permute-start(f32[5,32,32]{2,1,0:T(8,128)S(1)} %add_add_fusion.3), channel_id=1, source_target_pairs={{0,12},{4,8},{8,4},{12,0},{16,28},{20,24},{24,20},{28,16},{32,44},... | collective-permute-start | bytes 61448 | tf_op jit(solution)/shard_map/ppermute | solution.py:102
  49.5 5.4 %collective-permute-start.4 = (f32[5,32,32]{2,1,0:T(8,128)S(1)}, f32[5,32,32]{2,1,0:T(8,128)S(1)}, u32[]{:S(2)}, u32[]{:S(2)}) collective-permute-start(f32[5,32,32]{2,1,0:T(8,128)S(1)} %add_add_fusion.3), channel_id=1, source_target_pairs={{0,8},{4,12},{8,0},{12,4},{16,24},{20,28},{24,16},{28,20},{32,40},... | collective-permute-start | bytes 61448 | tf_op jit(solution)/shard_map/ppermute | solution.py:102
  49.9 5.0 %collective-permute-start.3 = (f32[5,32,32]{2,1,0:T(8,128)S(1)}, f32[5,32,32]{2,1,0:T(8,128)S(1)}, u32[]{:S(2)}, u32[]{:S(2)}) collective-permute-start(f32[5,32,32]{2,1,0:T(8,128)S(1)} %add_add_fusion.3), channel_id=1, source_target_pairs={{0,4},{4,0},{8,12},{12,8},{16,20},{20,16},{24,28},{28,24},{32,36},... | collective-permute-start | bytes 61448 | tf_op jit(solution)/shard_map/ppermute | solution.py:102
  54.9 9.4 %copy-start = (f32[5,32,32]{2,1,0:T(8,128)}, f32[5,32,32]{2,1,0:T(8,128)S(1)}, u32[]{:S(2)}) copy-start(f32[5,32,32]{2,1,0:T(8,128)S(1)} %add_add_fusion.2.own_ref) | copy-start | bytes 61444
  54.9 6.6 %collective-permute-start.8 = (f32[5,32,32]{2,1,0:T(8,128)S(1)}, f32[5,32,32]{2,1,0:T(8,128)S(1)}, u32[]{:S(2)}, u32[]{:S(2)}) collective-permute-start(f32[5,32,32]{2,1,0:T(8,128)S(1)} %add_add_fusion.2.own_ref), channel_id=1, source_target_pairs={{0,192},{4,196},{8,200},{12,204},{16,208},{20,212},{24,216},{28,22... | collective-permute-start | bytes 61448 | tf_op jit(solution)/shard_map/ppermute | solution.py:102
  57.7 6.6 %collective-permute-start.7 = (f32[5,32,32]{2,1,0:T(8,128)S(1)}, f32[5,32,32]{2,1,0:T(8,128)S(1)}, u32[]{:S(2)}, u32[]{:S(2)}) collective-permute-start(f32[5,32,32]{2,1,0:T(8,128)S(1)} %add_add_fusion.2.own_ref), channel_id=1, source_target_pairs={{0,128},{4,132},{8,136},{12,140},{16,144},{20,148},{24,152},{28,15... | collective-permute-start | bytes 61448 | tf_op jit(solution)/shard_map/ppermute | solution.py:102
  58.6 5.7 %collective-permute-start.6 = (f32[5,32,32]{2,1,0:T(8,128)S(1)}, f32[5,32,32]{2,1,0:T(8,128)S(1)}, u32[]{:S(2)}, u32[]{:S(2)}) collective-permute-start(f32[5,32,32]{2,1,0:T(8,128)S(1)} %add_add_fusion.2.own_ref), channel_id=1, source_target_pairs={{0,64},{4,68},{8,72},{12,76},{16,80},{20,84},{24,88},{28,92},{32,9... | collective-permute-start | bytes 61448 | tf_op jit(solution)/shard_map/ppermute | solution.py:102
  61.5 2.8 %copy-start.2 = (f32[5,32,32]{2,1,0:T(8,128)}, f32[5,32,32]{2,1,0:T(8,128)S(1)}, u32[]{:S(2)}) copy-start(f32[5,32,32]{2,1,0:T(8,128)S(1)} %collective-permute-done.8.third_ref) | copy-start | bytes 61444
  64.3 0.6 copy-start.4
  64.9 0.6 copy-start.6
  73.9 6.7 %collective-permute-start.11 = (f32[5,32,32]{2,1,0:T(8,128)S(1)}, f32[5,32,32]{2,1,0:T(8,128)S(1)}, u32[]{:S(2)}, u32[]{:S(2)}) collective-permute-start(f32[5,32,32]{2,1,0:T(8,128)S(1)} %fusion.24), channel_id=1, source_target_pairs={{0,48},{4,52},{8,56},{12,60},{16,32},{20,36},{24,40},{28,44},{32,1... | collective-permute-start | bytes 61448 | tf_op jit(solution)/shard_map/ppermute | solution.py:102
  76.8 8.8 %collective-permute-start.10 = (f32[5,32,32]{2,1,0:T(8,128)S(1)}, f32[5,32,32]{2,1,0:T(8,128)S(1)}, u32[]{:S(2)}, u32[]{:S(2)}) collective-permute-start(f32[5,32,32]{2,1,0:T(8,128)S(1)} %fusion.24), channel_id=1, source_target_pairs={{0,32},{4,36},{8,40},{12,44},{16,48},{20,52},{24,56},{28,60},{32,0... | collective-permute-start | bytes 61448 | tf_op jit(solution)/shard_map/ppermute | solution.py:102
  78.9 7.5 %collective-permute-start.9 = (f32[5,32,32]{2,1,0:T(8,128)S(1)}, f32[5,32,32]{2,1,0:T(8,128)S(1)}, u32[]{:S(2)}, u32[]{:S(2)}) collective-permute-start(f32[5,32,32]{2,1,0:T(8,128)S(1)} %fusion.24), channel_id=1, source_target_pairs={{0,16},{4,20},{8,24},{12,28},{16,0},{20,4},{24,8},{28,12},{32,48},... | collective-permute-start | bytes 61448 | tf_op jit(solution)/shard_map/ppermute | solution.py:102
  86.4 4.8 %collective-permute-start.14 = (f32[5,32,32]{2,1,0:T(8,128)S(1)}, f32[5,32,32]{2,1,0:T(8,128)S(1)}, u32[]{:S(2)}, u32[]{:S(2)}) collective-permute-start(f32[5,32,32]{2,1,0:T(8,128)S(1)} %add_add_fusion.1), channel_id=1, source_target_pairs={{0,12},{4,8},{8,4},{12,0},{16,28},{20,24},{24,20},{28,16},{32,44},... | collective-permute-start | bytes 61448 | tf_op jit(solution)/shard_map/ppermute | solution.py:102
  86.5 6.1 %collective-permute-start.13 = (f32[5,32,32]{2,1,0:T(8,128)S(1)}, f32[5,32,32]{2,1,0:T(8,128)S(1)}, u32[]{:S(2)}, u32[]{:S(2)}) collective-permute-start(f32[5,32,32]{2,1,0:T(8,128)S(1)} %add_add_fusion.1), channel_id=1, source_target_pairs={{0,8},{4,12},{8,0},{12,4},{16,24},{20,28},{24,16},{28,20},{32,40},... | collective-permute-start | bytes 61448 | tf_op jit(solution)/shard_map/ppermute | solution.py:102
  87.9 4.8 %collective-permute-start.12 = (f32[5,32,32]{2,1,0:T(8,128)S(1)}, f32[5,32,32]{2,1,0:T(8,128)S(1)}, u32[]{:S(2)}, u32[]{:S(2)}) collective-permute-start(f32[5,32,32]{2,1,0:T(8,128)S(1)} %add_add_fusion.1), channel_id=1, source_target_pairs={{0,4},{4,0},{8,12},{12,8},{16,20},{20,16},{24,28},{28,24},{32,36},... | collective-permute-start | bytes 61448 | tf_op jit(solution)/shard_map/ppermute | solution.py:102
  92.7 9.2 %copy-start.1 = (f32[5,32,32]{2,1,0:T(8,128)}, f32[5,32,32]{2,1,0:T(8,128)S(1)}, u32[]{:S(2)}) copy-start(f32[5,32,32]{2,1,0:T(8,128)S(1)} %add_add_fusion.own_ref) | copy-start | bytes 61444
  92.7 6.0 %collective-permute-start.17 = (f32[5,32,32]{2,1,0:T(8,128)S(1)}, f32[5,32,32]{2,1,0:T(8,128)S(1)}, u32[]{:S(2)}, u32[]{:S(2)}) collective-permute-start(f32[5,32,32]{2,1,0:T(8,128)S(1)} %add_add_fusion.own_ref), channel_id=1, source_target_pairs={{0,192},{4,196},{8,200},{12,204},{16,208},{20,212},{24,216},{28,22... | collective-permute-start | bytes 61448 | tf_op jit(solution)/shard_map/ppermute | solution.py:102
  95.3 6.6 %collective-permute-start.16 = (f32[5,32,32]{2,1,0:T(8,128)S(1)}, f32[5,32,32]{2,1,0:T(8,128)S(1)}, u32[]{:S(2)}, u32[]{:S(2)}) collective-permute-start(f32[5,32,32]{2,1,0:T(8,128)S(1)} %add_add_fusion.own_ref), channel_id=1, source_target_pairs={{0,128},{4,132},{8,136},{12,140},{16,144},{20,148},{24,152},{28,15... | collective-permute-start | bytes 61448 | tf_op jit(solution)/shard_map/ppermute | solution.py:102
  95.5 6.4 %collective-permute-start.15 = (f32[5,32,32]{2,1,0:T(8,128)S(1)}, f32[5,32,32]{2,1,0:T(8,128)S(1)}, u32[]{:S(2)}, u32[]{:S(2)}) collective-permute-start(f32[5,32,32]{2,1,0:T(8,128)S(1)} %add_add_fusion.own_ref), channel_id=1, source_target_pairs={{0,64},{4,68},{8,72},{12,76},{16,80},{20,84},{24,88},{28,92},{32,9... | collective-permute-start | bytes 61448 | tf_op jit(solution)/shard_map/ppermute | solution.py:102
  98.7 3.1 %copy-start.3 = (f32[5,32,32]{2,1,0:T(8,128)}, f32[5,32,32]{2,1,0:T(8,128)S(1)}, u32[]{:S(2)}) copy-start(f32[5,32,32]{2,1,0:T(8,128)S(1)} %collective-permute-done.17.third_ref) | copy-start | bytes 61444
  101.8 0.6 copy-start.5
  102.5 0.6 copy-start.7

commit v6 on v5

--- a/solution.py
+++ b/solution.py
@@ -94,7 +94,7 @@
 
 def reduce_space(values):
     count = lax.axis_size("space")
-    rounds = [[4, 8, 12], [1, 2, 3], [16, 32, 48]]
+    rounds = [[8, 4, 12], [2, 1, 3], [32, 16, 48]]
     for number, masks in enumerate(rounds):
         leaves = [values]
         for mask in masks:

time: 113 us -> 111 us (0.982)
  waiting for transfers between devices: 31.4 us -> 27.7 us
  starting transfers between devices: 27.7 us -> 29.4 us
  local copies, waits for them, and re-layouts: 5.59 us -> 4.38 us
    ppermute x18, waiting for transfers between devices: 31.4 us -> 27.7 us  [reduce_space(): leaves.append(lax.ppermute(values, 'space', pairs))]
    ppermute x18, starting transfers between devices: 27.7 us -> 29.4 us  [reduce_space(): leaves.append(lax.ppermute(values, 'space', pairs))]
    unnamed x16, local copies, waits for them, and re-layouts: 2.48 us -> 1.27 us
  transfers between devices with their start and end apart: 18 -> 18, of which waited for: 13 -> 16; matrix products, arithmetic and copies ran while one was open for 0% -> 0% of each run, Pallas kernels for 0% -> 0%
where the time goes in v6:
time: 111 us; the launch traced here: 109 us
  starting transfers between devices  29.4 us (26%)
  waiting for transfers between devices  27.7 us (25%)
  blocking collectives  21.2 us (19%)
  matrix products  12.2 us (11%)
  Pallas kernels  9.9 us (9%)
  local copies, waits for them, and re-layouts  4.38 us (4%)
  other arithmetic  4.31 us (4%)
    ppermute x18, starting transfers between devices, reduce_space(): leaves.append(lax.ppermute(values, 'space', pairs))  29.4 us
    ppermute x18, waiting for transfers between devices, reduce_space(): leaves.append(lax.ppermute(values, 'space', pairs))  27.7 us
    all_to_all x1, blocking collectives, local(): lax.all_to_all(outgoing, 'tm', split_axis=0, concat_axis=2, tiled=True)  21.2 us
    pallas_call x2, Pallas kernels, inverse_factor(): pl.pallas_call(functools.partial(_inverse_factor_kernel, rows_total=rows_...  9.9 us
    dot_general x1, matrix products, windowed_spectra(): jnp.einsum('fbcs,sp->fbcp', placed, snapshots, precision=lax.Precision.HI...  5.33 us
    dot_general x2, matrix products, finish_pass(): jnp.einsum('kij,kjp->kip', inverse, matrices, precision=lax.Precision.HIG...  4.24 us
    dot_general x2, matrix products, partial_gram(): jnp.einsum('kip,kjp->kij', matrices, matrices, precision=lax.Precision.HI...  2.6 us
  transfers between devices with their start and end apart: 18, of which 16 were waited for; matrix products, arithmetic and copies ran while one was open for 0% of the time, Pallas kernels for 0%

profile of v6, /device:TPU:8, one launch (start us, length us, event | category | flops | bytes accessed | tf_op | source)
XLA Modules:
  0.0 109.2 jit_solution(2140916652458956525)
XLA Ops:
  0.0 0.9 convert_reduce_fusion
  0.9 0.7 multiply_add_fusion
  1.8 0.7 broadcast_subtract_fusion
  2.7 0.2 multiply_subtract_fusion
  3.0 1.2 %cosine_multiply_fusion = (f32[9,8,1,1152]{3,1,2,0:T(8,128)S(1)}, f32[9,8,1,1152]{3,1,2,0:T(8,128)S(1)}) fusion(s32[8,1152]{1,0:T(8,128)S(1)} %fusion.12, f32[8,1152]{1,0:T(8,128)S(1)} %get-tuple-element.7, f32[8,1152]{1,0:T(8,128)S(1)} %get-tuple-element.8), kind=kLoop, calls=%fused_computation.15 | loop fusion | flops 1327104 | bytes 774144 | tf_op jit(solution)/shard_map/mul | solution.py:33
  4.2 5.3 %fusion = f32[9,8,2,1024]{3,1,2,0:T(8,128)S(1)} fusion(f32[1152,1024]{1,0:T(8,128)} %param.3, f32[9,8,1,1152]{3,1,2,0:T(8,128)S(1)} %get-tuple-element.6, f32[9,8,1,1152]{3,1,2,0:T(8,128)S(1)} %get-tuple-element.5, pred[8,1152]{1,0:T(8,128)(4,1)S(1)} %fusion.15), kind=kOutput, calls=%fused_computation.1 | convolution fusion | flops 2038763520 | bytes 5981184 | tf_op jit(solution)/shard_map/fbcs,sp->fbcp/dot_general | solution.py:35
  9.5 0.6 gather_fusion
  10.2 0.2 select_select_fusion
  10.4 21.2 %all_to_all.15 = f32[4,5,8,2,1024]{4,2,3,1,0:T(8,128)S(1)} all-to-all(f32[4,5,8,2,1024]{4,2,3,1,0:T(8,128)S(1)} %select_select_fusion), channel_id=1, replica_groups=mesh['space'=64,'tm'=4] {'tm'}, dimensions={0} | all-to-all | bytes 2621440 | tf_op jit(solution)/shard_map/all_to_all | solution.py:121
  31.7 1.3 %fusion.22 = f32[5,32,32]{2,1,0:T(8,128)S(1)} fusion(f32[5,32,2048]{2,1,0:T(8,128)S(1)} %bitcast.22), kind=kOutput, calls=%fused_computation.46 | convolution fusion | flops 125829120 | bytes 1331200 | tf_op jit(solution)/shard_map/kip,kjp->kij/dot_general | solution.py:49
  33.0 6.4 %collective-permute-start.2 = (f32[5,32,32]{2,1,0:T(8,128)S(1)}, f32[5,32,32]{2,1,0:T(8,128)S(1)}, u32[]{:S(2)}, u32[]{:S(2)}) collective-permute-start(f32[5,32,32]{2,1,0:T(8,128)S(1)} %fusion.22), channel_id=1, source_target_pairs={{0,48},{4,52},{8,56},{12,60},{16,32},{20,36},{24,40},{28,44},{32,1... | collective-permute-start | bytes 61448 | tf_op jit(solution)/shard_map/ppermute | solution.py:102
  39.4 1.5 %collective-permute-start.1 = (f32[5,32,32]{2,1,0:T(8,128)S(1)}, f32[5,32,32]{2,1,0:T(8,128)S(1)}, u32[]{:S(2)}, u32[]{:S(2)}) collective-permute-start(f32[5,32,32]{2,1,0:T(8,128)S(1)} %fusion.22), channel_id=1, source_target_pairs={{0,16},{4,20},{8,24},{12,28},{16,0},{20,4},{24,8},{28,12},{32,48},... | collective-permute-start | bytes 61448 | tf_op jit(solution)/shard_map/ppermute | solution.py:102
  40.8 1.0 collective-permute-start
  41.8 1.8 %collective-permute-done.2 = f32[5,32,32]{2,1,0:T(8,128)S(1)} collective-permute-done((f32[5,32,32]{2,1,0:T(8,128)S(1)}, f32[5,32,32]{2,1,0:T(8,128)S(1)}, u32[]{:S(2)}, u32[]{:S(2)}) %collective-permute-start.2) | collective-permute-done | bytes 20512 | tf_op jit(solution)/shard_map/ppermute | solution.py:102
  43.6 4.2 %collective-permute-done.1 = f32[5,32,32]{2,1,0:T(8,128)S(1)} collective-permute-done((f32[5,32,32]{2,1,0:T(8,128)S(1)}, f32[5,32,32]{2,1,0:T(8,128)S(1)}, u32[]{:S(2)}, u32[]{:S(2)}) %collective-permute-start.1) | collective-permute-done | bytes 20512 | tf_op jit(solution)/shard_map/ppermute | solution.py:102
  47.8 2.4 %collective-permute-done = f32[5,32,32]{2,1,0:T(8,128)S(1)} collective-permute-done((f32[5,32,32]{2,1,0:T(8,128)S(1)}, f32[5,32,32]{2,1,0:T(8,128)S(1)}, u32[]{:S(2)}, u32[]{:S(2)}) %collective-permute-start) | collective-permute-done | bytes 20512 | tf_op jit(solution)/shard_map/ppermute | solution.py:102
  50.4 2.0 %collective-permute-start.3 = (f32[5,32,32]{2,1,0:T(8,128)S(1)}, f32[5,32,32]{2,1,0:T(8,128)S(1)}, u32[]{:S(2)}, u32[]{:S(2)}) collective-permute-start(f32[5,32,32]{2,1,0:T(8,128)S(1)} %add_add_fusion.3), channel_id=1, source_target_pairs={{0,8},{4,12},{8,0},{12,4},{16,24},{20,28},{24,16},{28,20},{32,40},... | collective-permute-start | bytes 61448 | tf_op jit(solution)/shard_map/ppermute | solution.py:102
  52.4 1.9 %collective-permute-done.5 = f32[5,32,32]{2,1,0:T(8,128)S(1)} collective-permute-done((f32[5,32,32]{2,1,0:T(8,128)S(1)}, f32[5,32,32]{2,1,0:T(8,128)S(1)}, u32[]{:S(2)}, u32[]{:S(2)}) %collective-permute-start.5) | collective-permute-done | bytes 20512 | tf_op jit(solution)/shard_map/ppermute | solution.py:102
  54.3 1.5 %collective-permute-done.3 = f32[5,32,32]{2,1,0:T(8,128)S(1)} collective-permute-done((f32[5,32,32]{2,1,0:T(8,128)S(1)}, f32[5,32,32]{2,1,0:T(8,128)S(1)}, u32[]{:S(2)}, u32[]{:S(2)}) %collective-permute-start.3) | collective-permute-done | bytes 20512 | tf_op jit(solution)/shard_map/ppermute | solution.py:102
  55.8 2.8 %collective-permute-start.8 = (f32[5,32,32]{2,1,0:T(8,128)S(1)}, f32[5,32,32]{2,1,0:T(8,128)S(1)}, u32[]{:S(2)}, u32[]{:S(2)}) collective-permute-start(f32[5,32,32]{2,1,0:T(8,128)S(1)} %add_add_fusion.2.own_ref), channel_id=1, source_target_pairs={{0,192},{4,196},{8,200},{12,204},{16,208},{20,212},{24,216},{28,22... | collective-permute-start | bytes 61448 | tf_op jit(solution)/shard_map/ppermute | solution.py:102
  58.7 0.2 collective-permute-start.7
  58.9 1.7 %collective-permute-start.6 = (f32[5,32,32]{2,1,0:T(8,128)S(1)}, f32[5,32,32]{2,1,0:T(8,128)S(1)}, u32[]{:S(2)}, u32[]{:S(2)}) collective-permute-start(f32[5,32,32]{2,1,0:T(8,128)S(1)} %add_add_fusion.2.own_ref), channel_id=1, source_target_pairs={{0,128},{4,132},{8,136},{12,140},{16,144},{20,148},{24,152},{28,15... | collective-permute-start | bytes 61448 | tf_op jit(solution)/shard_map/ppermute | solution.py:102
  60.6 1.0 collective-permute-done.8.third_ref
  61.6 2.1 %collective-permute-done.7.second_ref = f32[5,32,32]{2,1,0:T(8,128)S(1)} collective-permute-done((f32[5,32,32]{2,1,0:T(8,128)S(1)}, f32[5,32,32]{2,1,0:T(8,128)S(1)}, u32[]{:S(2)}, u32[]{:S(2)}) %collective-permute-start.7) | collective-permute-done | bytes 20512 | tf_op jit(solution)/shard_map/ppermute | solution.py:102
  63.7 1.1 %collective-permute-done.6.first_ref = f32[5,32,32]{2,1,0:T(8,128)S(1)} collective-permute-done((f32[5,32,32]{2,1,0:T(8,128)S(1)}, f32[5,32,32]{2,1,0:T(8,128)S(1)}, u32[]{:S(2)}, u32[]{:S(2)}) %collective-permute-start.6) | collective-permute-done | bytes 20512 | tf_op jit(solution)/shard_map/ppermute | solution.py:102
  64.8 0.6 copy-done.6
  65.5 5.0 %shard_map.37 = f32[5,32,32]{2,1,0:T(8,128)} custom-call(f32[5,32,32]{2,1,0:T(8,128)} %copy-done, f32[5,32,32]{2,1,0:T(8,128)} %copy-done.6, f32[5,32,32]{2,1,0:T(8,128)} %copy-done.4, f32[5,32,32]{2,1,0:T(8,128)} %copy-done.2), custom_call_target="tpu_custom_call" | custom-call | tf_op jit(solution)/shard_map/pallas_call | solution.py:82
  70.4 2.1 %fusion.23 = f32[5,32,2048]{2,1,0:T(8,128)S(1)} fusion(f32[5,32,32]{2,1,0:T(8,128)} %shard_map.37, f32[5,32,2048]{2,1,0:T(8,128)S(1)} %bitcast.23), kind=kOutput, calls=%fused_computation.47 | convolution fusion | flops 125829120 | bytes 2641920 | tf_op jit(solution)/shard_map/kij,kjp->kip/dot_general | solution.py:92
  72.5 1.3 %fusion.24 = f32[5,32,32]{2,1,0:T(8,128)S(1)} fusion(f32[5,32,2048]{2,1,0:T(8,128)S(1)} %fusion.23), kind=kOutput, calls=%fused_computation.48 | convolution fusion | flops 125829120 | bytes 1331200 | tf_op jit(solution)/shard_map/kip,kjp->kij/dot_general | solution.py:49
  73.8 1.1 collective-permute-start.11
  74.9 1.4 %collective-permute-start.10 = (f32[5,32,32]{2,1,0:T(8,128)S(1)}, f32[5,32,32]{2,1,0:T(8,128)S(1)}, u32[]{:S(2)}, u32[]{:S(2)}) collective-permute-start(f32[5,32,32]{2,1,0:T(8,128)S(1)} %fusion.24), channel_id=1, source_target_pairs={{0,16},{4,20},{8,24},{12,28},{16,0},{20,4},{24,8},{28,12},{32,48},... | collective-permute-start | bytes 61448 | tf_op jit(solution)/shard_map/ppermute | solution.py:102
  76.3 4.1 %collective-permute-start.9 = (f32[5,32,32]{2,1,0:T(8,128)S(1)}, f32[5,32,32]{2,1,0:T(8,128)S(1)}, u32[]{:S(2)}, u32[]{:S(2)}) collective-permute-start(f32[5,32,32]{2,1,0:T(8,128)S(1)} %fusion.24), channel_id=1, source_target_pairs={{0,32},{4,36},{8,40},{12,44},{16,48},{20,52},{24,56},{28,60},{32,0... | collective-permute-start | bytes 61448 | tf_op jit(solution)/shard_map/ppermute | solution.py:102
  80.4 0.3 collective-permute-done.11
  80.7 0.5 collective-permute-done.10
  81.2 3.9 %collective-permute-done.9 = f32[5,32,32]{2,1,0:T(8,128)S(1)} collective-permute-done((f32[5,32,32]{2,1,0:T(8,128)S(1)}, f32[5,32,32]{2,1,0:T(8,128)S(1)}, u32[]{:S(2)}, u32[]{:S(2)}) %collective-permute-start.9) | collective-permute-done | bytes 20512 | tf_op jit(solution)/shard_map/ppermute | solution.py:102
  85.2 0.7 collective-permute-start.13
  85.8 1.5 %collective-permute-start.12 = (f32[5,32,32]{2,1,0:T(8,128)S(1)}, f32[5,32,32]{2,1,0:T(8,128)S(1)}, u32[]{:S(2)}, u32[]{:S(2)}) collective-permute-start(f32[5,32,32]{2,1,0:T(8,128)S(1)} %add_add_fusion.1), channel_id=1, source_target_pairs={{0,8},{4,12},{8,0},{12,4},{16,24},{20,28},{24,16},{28,20},{32,40},... | collective-permute-start | bytes 61448 | tf_op jit(solution)/shard_map/ppermute | solution.py:102
  87.3 1.7 %collective-permute-done.14 = f32[5,32,32]{2,1,0:T(8,128)S(1)} collective-permute-done((f32[5,32,32]{2,1,0:T(8,128)S(1)}, f32[5,32,32]{2,1,0:T(8,128)S(1)}, u32[]{:S(2)}, u32[]{:S(2)}) %collective-permute-start.14) | collective-permute-done | bytes 20512 | tf_op jit(solution)/shard_map/ppermute | solution.py:102
  89.0 1.8 %collective-permute-done.12 = f32[5,32,32]{2,1,0:T(8,128)S(1)} collective-permute-done((f32[5,32,32]{2,1,0:T(8,128)S(1)}, f32[5,32,32]{2,1,0:T(8,128)S(1)}, u32[]{:S(2)}, u32[]{:S(2)}) %collective-permute-start.12) | collective-permute-done | bytes 20512 | tf_op jit(solution)/shard_map/ppermute | solution.py:102
  90.8 2.2 %collective-permute-start.17 = (f32[5,32,32]{2,1,0:T(8,128)S(1)}, f32[5,32,32]{2,1,0:T(8,128)S(1)}, u32[]{:S(2)}, u32[]{:S(2)}) collective-permute-start(f32[5,32,32]{2,1,0:T(8,128)S(1)} %add_add_fusion.own_ref), channel_id=1, source_target_pairs={{0,192},{4,196},{8,200},{12,204},{16,208},{20,212},{24,216},{28,22... | collective-permute-start | bytes 61448 | tf_op jit(solution)/shard_map/ppermute | solution.py:102
  93.1 2.5 %collective-permute-start.15 = (f32[5,32,32]{2,1,0:T(8,128)S(1)}, f32[5,32,32]{2,1,0:T(8,128)S(1)}, u32[]{:S(2)}, u32[]{:S(2)}) collective-permute-start(f32[5,32,32]{2,1,0:T(8,128)S(1)} %add_add_fusion.own_ref), channel_id=1, source_target_pairs={{0,128},{4,132},{8,136},{12,140},{16,144},{20,148},{24,152},{28,15... | collective-permute-start | bytes 61448 | tf_op jit(solution)/shard_map/ppermute | solution.py:102
  95.6 1.0 collective-permute-done.17.third_ref
  96.6 1.3 %collective-permute-done.16.second_ref = f32[5,32,32]{2,1,0:T(8,128)S(1)} collective-permute-done((f32[5,32,32]{2,1,0:T(8,128)S(1)}, f32[5,32,32]{2,1,0:T(8,128)S(1)}, u32[]{:S(2)}, u32[]{:S(2)}) %collective-permute-start.16) | collective-permute-done | bytes 20512 | tf_op jit(solution)/shard_map/ppermute | solution.py:102
  97.8 1.5 %collective-permute-done.15.first_ref = f32[5,32,32]{2,1,0:T(8,128)S(1)} collective-permute-done((f32[5,32,32]{2,1,0:T(8,128)S(1)}, f32[5,32,32]{2,1,0:T(8,128)S(1)}, u32[]{:S(2)}, u32[]{:S(2)}) %collective-permute-start.15) | collective-permute-done | bytes 20512 | tf_op jit(solution)/shard_map/ppermute | solution.py:102
  99.4 0.6 copy-done.7
  100.0 5.0 %shard_map.38 = f32[5,32,32]{2,1,0:T(8,128)} custom-call(f32[5,32,32]{2,1,0:T(8,128)} %copy-done.1, f32[5,32,32]{2,1,0:T(8,128)} %copy-done.7, f32[5,32,32]{2,1,0:T(8,128)} %copy-done.5, f32[5,32,32]{2,1,0:T(8,128)} %copy-done.3), custom_call_target="tpu_custom_call" | custom-call | tf_op jit(solution)/shard_map/pallas_call | solution.py:82
  104.9 2.1 %fusion.25 = f32[5,32,2048]{2,1,0:T(8,128)S(1)} fusion(f32[5,32,32]{2,1,0:T(8,128)} %shard_map.38, f32[5,32,2048]{2,1,0:T(8,128)S(1)} %fusion.23), kind=kOutput, calls=%fused_computation.49 | convolution fusion | flops 125829120 | bytes 2641920 | tf_op jit(solution)/shard_map/kij,kjp->kip/dot_general | solution.py:92
  107.1 2.2 %reshape.161 = f32[5,32,2,1024]{3,2,1,0:T(2,128)} reshape(f32[5,32,2048]{2,1,0:T(8,128)S(1)} %fusion.25) | data formatting | bytes 2621440 | tf_op jit(solution)/shard_map/reshape | solution.py:128
  (34 shorter events, 1.1 us)
Async XLA Ops:
  33.0 10.6 %collective-permute-start.2 = (f32[5,32,32]{2,1,0:T(8,128)S(1)}, f32[5,32,32]{2,1,0:T(8,128)S(1)}, u32[]{:S(2)}, u32[]{:S(2)}) collective-permute-start(f32[5,32,32]{2,1,0:T(8,128)S(1)} %fusion.22), channel_id=1, source_target_pairs={{0,48},{4,52},{8,56},{12,60},{16,32},{20,36},{24,40},{28,44},{32,1... | collective-permute-start | bytes 61448 | tf_op jit(solution)/shard_map/ppermute | solution.py:102
  39.4 8.4 %collective-permute-start.1 = (f32[5,32,32]{2,1,0:T(8,128)S(1)}, f32[5,32,32]{2,1,0:T(8,128)S(1)}, u32[]{:S(2)}, u32[]{:S(2)}) collective-permute-start(f32[5,32,32]{2,1,0:T(8,128)S(1)} %fusion.22), channel_id=1, source_target_pairs={{0,16},{4,20},{8,24},{12,28},{16,0},{20,4},{24,8},{28,12},{32,48},... | collective-permute-start | bytes 61448 | tf_op jit(solution)/shard_map/ppermute | solution.py:102
  40.8 9.4 %collective-permute-start = (f32[5,32,32]{2,1,0:T(8,128)S(1)}, f32[5,32,32]{2,1,0:T(8,128)S(1)}, u32[]{:S(2)}, u32[]{:S(2)}) collective-permute-start(f32[5,32,32]{2,1,0:T(8,128)S(1)} %fusion.22), channel_id=1, source_target_pairs={{0,32},{4,36},{8,40},{12,44},{16,48},{20,52},{24,56},{28,60},{32,0... | collective-permute-start | bytes 61448 | tf_op jit(solution)/shard_map/ppermute | solution.py:102
  50.2 4.1 %collective-permute-start.5 = (f32[5,32,32]{2,1,0:T(8,128)S(1)}, f32[5,32,32]{2,1,0:T(8,128)S(1)}, u32[]{:S(2)}, u32[]{:S(2)}) collective-permute-start(f32[5,32,32]{2,1,0:T(8,128)S(1)} %add_add_fusion.3), channel_id=1, source_target_pairs={{0,12},{4,8},{8,4},{12,0},{16,28},{20,24},{24,20},{28,16},{32,44},... | collective-permute-start | bytes 61448 | tf_op jit(solution)/shard_map/ppermute | solution.py:102
  50.3 4.0 %collective-permute-start.4 = (f32[5,32,32]{2,1,0:T(8,128)S(1)}, f32[5,32,32]{2,1,0:T(8,128)S(1)}, u32[]{:S(2)}, u32[]{:S(2)}) collective-permute-start(f32[5,32,32]{2,1,0:T(8,128)S(1)} %add_add_fusion.3), channel_id=1, source_target_pairs={{0,4},{4,0},{8,12},{12,8},{16,20},{20,16},{24,28},{28,24},{32,36},... | collective-permute-start | bytes 61448 | tf_op jit(solution)/shard_map/ppermute | solution.py:102
  50.4 5.4 %collective-permute-start.3 = (f32[5,32,32]{2,1,0:T(8,128)S(1)}, f32[5,32,32]{2,1,0:T(8,128)S(1)}, u32[]{:S(2)}, u32[]{:S(2)}) collective-permute-start(f32[5,32,32]{2,1,0:T(8,128)S(1)} %add_add_fusion.3), channel_id=1, source_target_pairs={{0,8},{4,12},{8,0},{12,4},{16,24},{20,28},{24,16},{28,20},{32,40},... | collective-permute-start | bytes 61448 | tf_op jit(solution)/shard_map/ppermute | solution.py:102
  55.8 9.0 %copy-start = (f32[5,32,32]{2,1,0:T(8,128)}, f32[5,32,32]{2,1,0:T(8,128)S(1)}, u32[]{:S(2)}) copy-start(f32[5,32,32]{2,1,0:T(8,128)S(1)} %add_add_fusion.2.own_ref) | copy-start | bytes 61444
  55.8 5.8 %collective-permute-start.8 = (f32[5,32,32]{2,1,0:T(8,128)S(1)}, f32[5,32,32]{2,1,0:T(8,128)S(1)}, u32[]{:S(2)}, u32[]{:S(2)}) collective-permute-start(f32[5,32,32]{2,1,0:T(8,128)S(1)} %add_add_fusion.2.own_ref), channel_id=1, source_target_pairs={{0,192},{4,196},{8,200},{12,204},{16,208},{20,212},{24,216},{28,22... | collective-permute-start | bytes 61448 | tf_op jit(solution)/shard_map/ppermute | solution.py:102
  58.7 5.1 %collective-permute-start.7 = (f32[5,32,32]{2,1,0:T(8,128)S(1)}, f32[5,32,32]{2,1,0:T(8,128)S(1)}, u32[]{:S(2)}, u32[]{:S(2)}) collective-permute-start(f32[5,32,32]{2,1,0:T(8,128)S(1)} %add_add_fusion.2.own_ref), channel_id=1, source_target_pairs={{0,64},{4,68},{8,72},{12,76},{16,80},{20,84},{24,88},{28,92},{32,9... | collective-permute-start | bytes 61448 | tf_op jit(solution)/shard_map/ppermute | solution.py:102
  58.9 5.9 %collective-permute-start.6 = (f32[5,32,32]{2,1,0:T(8,128)S(1)}, f32[5,32,32]{2,1,0:T(8,128)S(1)}, u32[]{:S(2)}, u32[]{:S(2)}) collective-permute-start(f32[5,32,32]{2,1,0:T(8,128)S(1)} %add_add_fusion.2.own_ref), channel_id=1, source_target_pairs={{0,128},{4,132},{8,136},{12,140},{16,144},{20,148},{24,152},{28,15... | collective-permute-start | bytes 61448 | tf_op jit(solution)/shard_map/ppermute | solution.py:102
  61.6 3.3 %copy-start.2 = (f32[5,32,32]{2,1,0:T(8,128)}, f32[5,32,32]{2,1,0:T(8,128)S(1)}, u32[]{:S(2)}) copy-start(f32[5,32,32]{2,1,0:T(8,128)S(1)} %collective-permute-done.8.third_ref) | copy-start | bytes 61444
  63.7 1.1 %copy-start.4 = (f32[5,32,32]{2,1,0:T(8,128)}, f32[5,32,32]{2,1,0:T(8,128)S(1)}, u32[]{:S(2)}) copy-start(f32[5,32,32]{2,1,0:T(8,128)S(1)} %collective-permute-done.7.second_ref) | copy-start | bytes 61444
  64.8 0.6 copy-start.6
  73.8 6.8 %collective-permute-start.11 = (f32[5,32,32]{2,1,0:T(8,128)S(1)}, f32[5,32,32]{2,1,0:T(8,128)S(1)}, u32[]{:S(2)}, u32[]{:S(2)}) collective-permute-start(f32[5,32,32]{2,1,0:T(8,128)S(1)} %fusion.24), channel_id=1, source_target_pairs={{0,48},{4,52},{8,56},{12,60},{16,32},{20,36},{24,40},{28,44},{32,1... | collective-permute-start | bytes 61448 | tf_op jit(solution)/shard_map/ppermute | solution.py:102
  74.9 6.2 %collective-permute-start.10 = (f32[5,32,32]{2,1,0:T(8,128)S(1)}, f32[5,32,32]{2,1,0:T(8,128)S(1)}, u32[]{:S(2)}, u32[]{:S(2)}) collective-permute-start(f32[5,32,32]{2,1,0:T(8,128)S(1)} %fusion.24), channel_id=1, source_target_pairs={{0,16},{4,20},{8,24},{12,28},{16,0},{20,4},{24,8},{28,12},{32,48},... | collective-permute-start | bytes 61448 | tf_op jit(solution)/shard_map/ppermute | solution.py:102
  76.3 8.7 %collective-permute-start.9 = (f32[5,32,32]{2,1,0:T(8,128)S(1)}, f32[5,32,32]{2,1,0:T(8,128)S(1)}, u32[]{:S(2)}, u32[]{:S(2)}) collective-permute-start(f32[5,32,32]{2,1,0:T(8,128)S(1)} %fusion.24), channel_id=1, source_target_pairs={{0,32},{4,36},{8,40},{12,44},{16,48},{20,52},{24,56},{28,60},{32,0... | collective-permute-start | bytes 61448 | tf_op jit(solution)/shard_map/ppermute | solution.py:102
  85.1 4.0 %collective-permute-start.14 = (f32[5,32,32]{2,1,0:T(8,128)S(1)}, f32[5,32,32]{2,1,0:T(8,128)S(1)}, u32[]{:S(2)}, u32[]{:S(2)}) collective-permute-start(f32[5,32,32]{2,1,0:T(8,128)S(1)} %add_add_fusion.1), channel_id=1, source_target_pairs={{0,12},{4,8},{8,4},{12,0},{16,28},{20,24},{24,20},{28,16},{32,44},... | collective-permute-start | bytes 61448 | tf_op jit(solution)/shard_map/ppermute | solution.py:102
  85.2 3.9 %collective-permute-start.13 = (f32[5,32,32]{2,1,0:T(8,128)S(1)}, f32[5,32,32]{2,1,0:T(8,128)S(1)}, u32[]{:S(2)}, u32[]{:S(2)}) collective-permute-start(f32[5,32,32]{2,1,0:T(8,128)S(1)} %add_add_fusion.1), channel_id=1, source_target_pairs={{0,4},{4,0},{8,12},{12,8},{16,20},{20,16},{24,28},{28,24},{32,36},... | collective-permute-start | bytes 61448 | tf_op jit(solution)/shard_map/ppermute | solution.py:102
  85.8 4.9 %collective-permute-start.12 = (f32[5,32,32]{2,1,0:T(8,128)S(1)}, f32[5,32,32]{2,1,0:T(8,128)S(1)}, u32[]{:S(2)}, u32[]{:S(2)}) collective-permute-start(f32[5,32,32]{2,1,0:T(8,128)S(1)} %add_add_fusion.1), channel_id=1, source_target_pairs={{0,8},{4,12},{8,0},{12,4},{16,24},{20,28},{24,16},{28,20},{32,40},... | collective-permute-start | bytes 61448 | tf_op jit(solution)/shard_map/ppermute | solution.py:102
  90.8 8.5 %copy-start.1 = (f32[5,32,32]{2,1,0:T(8,128)}, f32[5,32,32]{2,1,0:T(8,128)S(1)}, u32[]{:S(2)}) copy-start(f32[5,32,32]{2,1,0:T(8,128)S(1)} %add_add_fusion.own_ref) | copy-start | bytes 61444
  90.8 5.7 %collective-permute-start.17 = (f32[5,32,32]{2,1,0:T(8,128)S(1)}, f32[5,32,32]{2,1,0:T(8,128)S(1)}, u32[]{:S(2)}, u32[]{:S(2)}) collective-permute-start(f32[5,32,32]{2,1,0:T(8,128)S(1)} %add_add_fusion.own_ref), channel_id=1, source_target_pairs={{0,192},{4,196},{8,200},{12,204},{16,208},{20,212},{24,216},{28,22... | collective-permute-start | bytes 61448 | tf_op jit(solution)/shard_map/ppermute | solution.py:102
  93.0 4.8 %collective-permute-start.16 = (f32[5,32,32]{2,1,0:T(8,128)S(1)}, f32[5,32,32]{2,1,0:T(8,128)S(1)}, u32[]{:S(2)}, u32[]{:S(2)}) collective-permute-start(f32[5,32,32]{2,1,0:T(8,128)S(1)} %add_add_fusion.own_ref), channel_id=1, source_target_pairs={{0,64},{4,68},{8,72},{12,76},{16,80},{20,84},{24,88},{28,92},{32,9... | collective-permute-start | bytes 61448 | tf_op jit(solution)/shard_map/ppermute | solution.py:102
  93.1 6.3 %collective-permute-start.15 = (f32[5,32,32]{2,1,0:T(8,128)S(1)}, f32[5,32,32]{2,1,0:T(8,128)S(1)}, u32[]{:S(2)}, u32[]{:S(2)}) collective-permute-start(f32[5,32,32]{2,1,0:T(8,128)S(1)} %add_add_fusion.own_ref), channel_id=1, source_target_pairs={{0,128},{4,132},{8,136},{12,140},{16,144},{20,148},{24,152},{28,15... | collective-permute-start | bytes 61448 | tf_op jit(solution)/shard_map/ppermute | solution.py:102
  96.5 2.8 %copy-start.3 = (f32[5,32,32]{2,1,0:T(8,128)}, f32[5,32,32]{2,1,0:T(8,128)S(1)}, u32[]{:S(2)}) copy-start(f32[5,32,32]{2,1,0:T(8,128)S(1)} %collective-permute-done.17.third_ref) | copy-start | bytes 61444
  97.8 1.5 %copy-start.5 = (f32[5,32,32]{2,1,0:T(8,128)}, f32[5,32,32]{2,1,0:T(8,128)S(1)}, u32[]{:S(2)}) copy-start(f32[5,32,32]{2,1,0:T(8,128)S(1)} %collective-permute-done.16.second_ref) | copy-start | bytes 61444
  99.3 0.6 copy-start.7
